TPU v7x, 256 devices: a whole 4x4x8 slice. The times are simulated.
256 devices in a mesh: lag: 4 (over y_lo, core), recv: 8 (over z), src: 8 (over y_hi, x).
Axes of the slice: x: 4, y: 4 (y_hi: 2, y_lo: 2; y = y_hi * 2 + y_lo), z: 8, core: 2. Of those that a mesh axis runs over, the one named last changes fastest.
Arguments:
- kernel: bfloat16 [4096, 32, 4096], P('recv', 'lag', 'src'), may hold values from -0.0234375 to 0.0234375
- causal_mask: int32 [32, 32, 32], P('recv', 'lag', 'src'), may hold values from 0 to 1, as said below
- history: bfloat16 [32, 4096, 256], P('lag', 'src'), may hold values from -4 to 4
- background: float32 [4096, 256], P('recv'), may hold values from -6 to 6
- classes: int32 [4096], P('recv'), may hold values from 0 to 7
- rate_scale: float32 [8], replicated, may hold values from 0.5 to 2
- stress_scale: float32 [8], replicated, may hold values from 0.5 to 2
Outputs:
- rates: bfloat16 [3, 4096, 256], P(None, 'recv')
Inputs may be any that keep to these rules, and one draw needn't show every extreme that they name: causal_mask[p, l, q] is 1 exactly when |p - q| <= r_l for a whole number r_l that never falls as l grows.
All inputs are finite; a program needn't handle non-finite values.
Results may differ from a plain program's by a relative error of at most 0.0019.
Values may be sent and summed in bfloat16 or wider, within the bound.
No kernel may reach another device: no remote copies, remote signals or barrier semaphores. Data moves between devices by JAX's collectives and lax.ppermute only.
A program may use at most 64 MiB of HBM per device.

v0:
```python
import jax
import jax.numpy as jnp
from jax import lax
from jax.sharding import PartitionSpec as P

STEPS = 3


def passed_along(block, axis, distance):
    devices = range(lax.axis_size(axis))
    route = [(i - distance, i) for i in devices if i - distance in devices]
    return lax.ppermute(block, axis, route)


def friction(stress, offset, background, classes, rate_scale, stress_scale):
    row_total = stress.shape[0]
    element_class = lax.dynamic_slice_in_dim(classes, offset, row_total, 0)
    loaded = lax.dynamic_slice_in_dim(background, offset, row_total, 0)
    selector = (
        element_class[:, None] == jnp.arange(rate_scale.shape[0], dtype=jnp.int32)[None, :]
    ).astype(jnp.float32)
    limit = jnp.sum(selector * rate_scale[None, :], axis=1)[:, None]
    width_scale = jnp.sum(selector * stress_scale[None, :], axis=1)[:, None]
    return (limit * jnp.tanh((loaded + stress) / width_scale)).astype(jnp.bfloat16)


def local(kernel, causal_mask, history, background, classes, rate_scale, stress_scale):
    rows_here, lag_here, cols_here = kernel.shape
    block_size = rows_here // causal_mask.shape[0]
    allowed = jnp.repeat(jnp.repeat(causal_mask, block_size, 0), block_size, 2) > 0
    masked_rows = jnp.where(allowed, kernel, jnp.zeros_like(kernel)).reshape(
        rows_here, lag_here * cols_here
    )
    src_count = lax.axis_size("src")
    lag_pos = lax.axis_index("lag")
    src_pos = lax.axis_index("src")
    scenarios = history.shape[2]
    produced = []
    for step_index in range(STEPS):
        stacked = history.reshape(lag_here * cols_here, scenarios)
        share_rows = lax.psum_scatter(
            jnp.dot(masked_rows, stacked, preferred_element_type=jnp.float32),
            ("lag", "src"),
            scatter_dimension=0,
            tiled=True,
        )
        offset = (lag_pos * src_count + src_pos) * share_rows.shape[0]
        local_rates = friction(share_rows, offset, background, classes, rate_scale, stress_scale)
        new_rates = lax.all_gather(local_rates, ("lag", "src"), axis=0, tiled=True)
        produced.append(new_rates)
        if step_index + 1 < STEPS:
            gathered = lax.all_gather(new_rates, "recv", axis=0, tiled=True)
            newest = lax.dynamic_slice_in_dim(gathered, src_pos * cols_here, cols_here, 0)
            aged_block = passed_along(history[-1], "lag", 1)
            incoming = jnp.where(lag_pos == 0, newest, aged_block)
            history = jnp.concatenate([incoming[None], history[:-1]], axis=0)
    return jnp.stack(produced)


def solution(mesh):
    in_specs = (
        P("recv", "lag", "src"),
        P("recv", "lag", "src"),
        P("lag", "src", None),
        P("recv", None),
        P("recv"),
        P(),
        P(),
    )
    out_specs = P(None, "recv", None)
    return jax.shard_map(local, mesh=mesh, in_specs=in_specs, out_specs=out_specs, check_vma=False)
```

profile of v0, /device:TPU:225, one launch (start us, length us, event | category | flops | bytes accessed | tf_op | source)
XLA Modules:
  0.0 809.9 jit_solution(2592756840679076065)
XLA Ops:
  7.4 8.7 %bitcast_select_fusion = bf16[512,8,512]{2,1,0:T(8,128)(2,1)S(1)} fusion(bf16[512,8,512]{2,1,0:T(8,128)(2,1)} %param.7, pred[512,8,4]{1,2,0:T(4,128)(4,1)S(1)} %bitcast.23), kind=kLoop, calls=%fused_computation | loop fusion | flops 2097152 | bytes 8404992 | tf_op jit(solution)/shard_map/jit(_where)/select_n | solution.py:31
  16.1 1.9 copy-done
  18.1 3.2 fusion.13
  22.2 147.5 %reduce-scatter.4.cloned.1.call-done = f32[16,256]{1,0:T(8,128)} async-done(((f32[512,256]{1,0:T(8,128)}), f32[16,256]{1,0:T(8,128)}) %reduce-scatter.4.cloned.1.call-update) | async-done | bytes 16400 | tf_op jit(solution)/shard_map/reduce_scatter | solution.py:41
  169.7 0.8 multiply_convert_fusion.2
  170.5 80.0 %all_gather.15 = bf16[512,256]{1,0:T(8,128)(2,1)} all-gather(bf16[16,256]{1,0:T(8,128)(2,1)S(1)} %multiply_convert_fusion.2), channel_id=1, replica_groups=mesh['lag'=4,'recv'=8,'src'=8] {'lag','src'}, dimensions={0}, use_global_device_ids=true | all-gather | bytes 270336 | tf_op jit(solution)/shard_map/all_gather | solution.py:49
  250.6 1.9 collective-permute-start
  252.5 1.4 slice.14
  253.9 2.0 collective-permute-done
  255.9 33.0 %all-gather.3.cloned.1.call-done = bf16[4096,256]{1,0:T(8,128)(2,1)} async-done(((bf16[512,256]{1,0:T(8,128)(2,1)}), bf16[4096,256]{1,0:T(8,128)(2,1)}) %all-gather.3.cloned.1.call-update) | async-done | bytes 2097168 | tf_op jit(solution)/shard_map/all_gather | solution.py:52
  288.9 1.0 select_bitcast_fusion.1
  289.9 6.2 fusion.16
  296.2 152.5 %reduce-scatter.6.cloned.1.call-done = f32[16,256]{1,0:T(8,128)} async-done(((f32[512,256]{1,0:T(8,128)}), f32[16,256]{1,0:T(8,128)}) %reduce-scatter.6.cloned.1.call-update) | async-done | bytes 16400 | tf_op jit(solution)/shard_map/reduce_scatter | solution.py:41
  448.7 0.8 multiply_convert_fusion.1
  449.5 79.7 %all_gather.17 = bf16[512,256]{1,0:T(8,128)(2,1)} all-gather(bf16[16,256]{1,0:T(8,128)(2,1)S(1)} %multiply_convert_fusion.1), channel_id=1, replica_groups=mesh['lag'=4,'recv'=8,'src'=8] {'lag','src'}, dimensions={0}, use_global_device_ids=true | all-gather | bytes 270336 | tf_op jit(solution)/shard_map/all_gather | solution.py:49
  529.3 1.9 collective-permute-start.1
  531.3 3.4 collective-permute-done.1
  534.7 32.9 %all-gather.5.cloned.1.call-done = bf16[4096,256]{1,0:T(8,128)(2,1)} async-done(((bf16[512,256]{1,0:T(8,128)(2,1)}), bf16[4096,256]{1,0:T(8,128)(2,1)}) %all-gather.5.cloned.1.call-update) | async-done | bytes 2097168 | tf_op jit(solution)/shard_map/all_gather | solution.py:52
  567.5 1.0 select_bitcast_fusion
  568.6 5.7 fusion.21
  574.3 152.6 %reduce-scatter.8.cloned.1.call-done = f32[16,256]{1,0:T(8,128)} async-done(((f32[512,256]{1,0:T(8,128)}), f32[16,256]{1,0:T(8,128)}) %reduce-scatter.8.cloned.1.call-update) | async-done | bytes 16400 | tf_op jit(solution)/shard_map/reduce_scatter | solution.py:41
  726.8 0.8 multiply_convert_fusion
  727.7 74.8 %all_gather.19 = bf16[512,256]{1,0:T(8,128)(2,1)S(1)} all-gather(bf16[16,256]{1,0:T(8,128)(2,1)S(1)} %multiply_convert_fusion), channel_id=1, replica_groups=mesh['lag'=4,'recv'=8,'src'=8] {'lag','src'}, dimensions={0}, use_global_device_ids=true | all-gather | bytes 270336 | tf_op jit(solution)/shard_map/all_gather | solution.py:49
  802.4 1.0 pad_maximum_fusion.1
  (28 shorter events, 2.0 us)
Async XLA Ops:
  6.5 163.2 %reduce-scatter.4.cloned.1.call-start = ((), (), s32[]{:S(2)}) async-start(), calls=%async_computation.3 | async-start | bytes 540672 | tf_op jit(solution)/shard_map/reduce_scatter | solution.py:41
  7.4 10.7 %copy-start.1 = (bf16[8,512,256]{2,1,0:T(8,128)(2,1)S(1)}, bf16[8,512,256]{2,1,0:T(8,128)(2,1)}, u32[]{:S(2)}) copy-start(bf16[8,512,256]{2,1,0:T(8,128)(2,1)} %param.9) | copy-start | bytes 6291460
  16.1 2.0 copy-start
  18.1 4.1 copy-start.5
  18.1 4.1 copy-start.6
  21.3 267.6 %all-gather.3.cloned.1.call-start = ((), (), s32[]{:S(2)}) async-start(), calls=%async_computation.4 | async-start | bytes 2359296 | tf_op jit(solution)/shard_map/all_gather | solution.py:52
  250.5 198.2 %reduce-scatter.6.cloned.1.call-start = ((), (), s32[]{:S(2)}) async-start(), calls=%async_computation.5 | async-start | bytes 540672 | tf_op jit(solution)/shard_map/reduce_scatter | solution.py:41
  250.6 5.3 collective-permute-start
  289.9 278.7 %copy-start.4 = (bf16[7,512,256]{2,1,0:T(8,128)(2,1)S(1)}, bf16[7,512,256]{2,1,0:T(8,128)(2,1)}, u32[]{:S(2)}) copy-start(bf16[7,512,256]{2,1,0:T(8,128)(2,1)} %slice.14) | copy-start | bytes 5505028
  296.1 271.4 %all-gather.5.cloned.1.call-start = ((), (), s32[]{:S(2)}) async-start(), calls=%async_computation.6 | async-start | bytes 2359296 | tf_op jit(solution)/shard_map/all_gather | solution.py:52
  529.3 197.5 %reduce-scatter.8.cloned.1.call-start = ((), (), s32[]{:S(2)}) async-start(), calls=%async_computation.7 | async-start | bytes 540672 | tf_op jit(solution)/shard_map/reduce_scatter | solution.py:41
  529.3 5.3 collective-permute-start.1
  568.6 233.9 %copy-start.2 = (bf16[512,256]{1,0:T(8,128)(2,1)S(1)}, bf16[512,256]{1,0:T(8,128)(2,1)}, u32[]{:S(2)}) copy-start(bf16[512,256]{1,0:T(8,128)(2,1)} %all_gather.15) | copy-start | bytes 786436
  568.6 233.9 %copy-start.3 = (bf16[512,256]{1,0:T(8,128)(2,1)S(1)}, bf16[512,256]{1,0:T(8,128)(2,1)}, u32[]{:S(2)}) copy-start(bf16[512,256]{1,0:T(8,128)(2,1)} %all_gather.17) | copy-start | bytes 786436
Sparse Core Ops, SparseCore 0:
  21.4 148.2 reduce-scatter.3
  250.6 38.2 all-gather.2
  296.3 152.4 reduce-scatter.5
  529.4 38.0 all-gather.4
  574.4 152.3 reduce-scatter.7
where the time goes:
time: 817 us; the launch traced here: 810 us
  waiting for transfers between devices  524 us (64%)
  blocking collectives  234 us (29%)
  matrix products  15.1 us (2%)
  other arithmetic  14.9 us (2%)
  between operations  13.3 us (2%)
    reduce_scatter x3, waiting for transfers between devices, local(): lax.psum_scatter(jnp.dot(masked_rows, stacked, preferred_element_type=jnp...  453 us
    all_gather x3, blocking collectives, local(): new_rates = lax.all_gather(local_rates, ('lag', 'src'), axis=0, tiled=True)  234 us
    all_gather x2, waiting for transfers between devices, local(): gathered = lax.all_gather(new_rates, 'recv', axis=0, tiled=True)  65.9 us
  transfers between devices with their start and end apart: 7, of which 7 were waited for; matrix products, arithmetic and copies ran while one was open for 0% of the time, Pallas kernels for 0%

commit v1 on v0

v1 whole, which is shorter than its diff:
```python
import jax
import jax.numpy as jnp
from jax import lax
from jax.sharding import PartitionSpec as P

STEPS = 3


def swap(block, axis, mask):
    size = lax.axis_size(axis)
    return lax.ppermute(block, axis, [(i, i ^ mask) for i in range(size)])


def tree_stages():
    stages = []
    for axis in ("lag", "src"):
        mask = 1
        while mask < lax.axis_size(axis):
            stages.append((axis, mask))
            mask *= 2
    return stages


def reduce_scatter(x, stages):
    offset = 0
    for axis, mask in stages:
        half = x.shape[0] // 2
        bit = (lax.axis_index(axis) // mask) % 2
        keep = lax.dynamic_slice_in_dim(x, bit * half, half, 0)
        send = lax.dynamic_slice_in_dim(x, (1 - bit) * half, half, 0)
        x = keep + swap(send, axis, mask)
        offset = offset + bit * half
    return x, offset


def all_gather(y, stages):
    for axis, mask in reversed(stages):
        bit = (lax.axis_index(axis) // mask) % 2
        other = swap(y, axis, mask)
        first = jnp.where(bit == 0, y, other)
        second = jnp.where(bit == 0, other, y)
        y = jnp.concatenate([first, second], axis=0)
    return y


def friction(stress, offset, background, classes, rate_scale, stress_scale):
    row_total = stress.shape[0]
    element_class = lax.dynamic_slice_in_dim(classes, offset, row_total, 0)
    loaded = lax.dynamic_slice_in_dim(background, offset, row_total, 0)
    selector = (
        element_class[:, None] == jnp.arange(rate_scale.shape[0], dtype=jnp.int32)[None, :]
    ).astype(jnp.float32)
    limit = jnp.sum(selector * rate_scale[None, :], axis=1)[:, None]
    width_scale = jnp.sum(selector * stress_scale[None, :], axis=1)[:, None]
    return (limit * jnp.tanh((loaded + stress) / width_scale)).astype(jnp.bfloat16)


def newest_to_sources(new_rates):
    recv_n = lax.axis_size("recv")
    src_n = lax.axis_size("src")
    route = [(s * src_n + r, r * src_n + s) for r in range(recv_n) for s in range(src_n)]
    return lax.ppermute(new_rates, ("lag", "recv", "src"), route)


def aged_from_previous(oldest):
    n = lax.axis_size("lag")
    return lax.ppermute(oldest, "lag", [(i, i + 1) for i in range(n - 1)])


def local(kernel, causal_mask, history, background, classes, rate_scale, stress_scale):
    rows_here, lag_here, cols_here = kernel.shape
    block_size = rows_here // causal_mask.shape[0]
    allowed = jnp.repeat(jnp.repeat(causal_mask, block_size, 0), block_size, 2) > 0
    masked_rows = jnp.where(allowed, kernel, jnp.zeros_like(kernel)).reshape(
        rows_here, lag_here * cols_here
    )
    lag_pos = lax.axis_index("lag")
    scenarios = history.shape[2]
    stages = tree_stages()
    produced = []
    for step_index in range(STEPS):
        stacked = history.reshape(lag_here * cols_here, scenarios)
        partial = jnp.dot(masked_rows, stacked, preferred_element_type=jnp.float32)
        share_rows, offset = reduce_scatter(partial, stages)
        local_rates = friction(share_rows, offset, background, classes, rate_scale, stress_scale)
        new_rates = all_gather(local_rates, stages)
        produced.append(new_rates)
        if step_index + 1 < STEPS:
            newest = newest_to_sources(new_rates)
            aged_block = aged_from_previous(history[-1])
            incoming = jnp.where(lag_pos == 0, newest, aged_block)
            history = jnp.concatenate([incoming[None], history[:-1]], axis=0)
    return jnp.stack(produced)


def solution(mesh):
    in_specs = (
        P("recv", "lag", "src"),
        P("recv", "lag", "src"),
        P("lag", "src", None),
        P("recv", None),
        P("recv"),
        P(),
        P(),
    )
    out_specs = P(None, "recv", None)
    return jax.shard_map(local, mesh=mesh, in_specs=in_specs, out_specs=out_specs, check_vma=False)
```

time: 817 us -> 200 us (0.24)
  waiting for transfers between devices: 524 us -> 79 us
  blocking collectives: 234 us -> 0 us
  starting transfers between devices: 4.01 us -> 96.9 us
  between operations: 13.3 us -> 0.54 us
    reduce_scatter x3 -> x0, waiting for transfers between devices: 453 us -> none  [local(): lax.psum_scatter(jnp.dot(masked_rows, stacked, preferred_element_type=jnp...]
    all_gather x3 -> x0, blocking collectives: 234 us -> none  [local(): new_rates = lax.all_gather(local_rates, ('lag', 'src'), axis=0, tiled=True)]
    ppermute x2 -> x34, starting transfers between devices: 3.84 us -> 96.9 us  [the longest x30 89.8 us: swap(): return lax.ppermute(block, axis, [(i, i ^ mask) for i in range(size)])]
    ppermute x2 -> x34, waiting for transfers between devices: 5.36 us -> 79 us  [the longest x30 74.9 us: swap(): return lax.ppermute(block, axis, [(i, i ^ mask) for i in range(size)])]
    all_gather x2 -> x0, waiting for transfers between devices: 65.9 us -> none  [local(): gathered = lax.all_gather(new_rates, 'recv', axis=0, tiled=True)]
  transfers between devices with their start and end apart: 7 -> 34, of which waited for: 7 -> 30; matrix products, arithmetic and copies ran while one was open for 0% -> 1% of each run, Pallas kernels for 0% -> 0%
where the time goes in v1:
time: 200 us; the launch traced here: 199 us
  starting transfers between devices  96.9 us (48%)
  waiting for transfers between devices  79 us (40%)
  other arithmetic  13.6 us (7%)
  matrix products  7.59 us (4%)
    ppermute x30, starting transfers between devices, swap(): return lax.ppermute(block, axis, [(i, i ^ mask) for i in range(size)])  89.8 us
    ppermute x30, waiting for transfers between devices, swap(): return lax.ppermute(block, axis, [(i, i ^ mask) for i in range(size)])  74.9 us
    select_n x1, other arithmetic, local(): jnp.where(allowed, kernel, jnp.zeros_like(kernel))  8.71 us
    dot_general x3, matrix products, local(): partial = jnp.dot(masked_rows, stacked, preferred_element_type=jnp.float32)  7.59 us
    ppermute x2, starting transfers between devices, aged_from_previous(): return lax.ppermute(oldest, 'lag', [(i, i + 1) for i in range(n - 1)])  5.02 us
    ppermute x2, waiting for transfers between devices, aged_from_previous(): return lax.ppermute(oldest, 'lag', [(i, i + 1) for i in range(n - 1)])  4.16 us
  transfers between devices with their start and end apart: 34, of which 30 were waited for; matrix products, arithmetic and copies ran while one was open for 1% of the time, Pallas kernels for 0%

profile of v1, /device:TPU:225, one launch (start us, length us, event | category | flops | bytes accessed | tf_op | source)
XLA Modules:
  0.0 199.3 jit_solution(13298118873395940439)
XLA Ops:
  0.9 8.7 %bitcast_select_fusion = bf16[512,8,512]{2,1,0:T(8,128)(2,1)S(1)} fusion(bf16[512,8,512]{2,1,0:T(8,128)(2,1)} %param.7, pred[512,8,4]{1,2,0:T(4,128)(4,1)S(1)} %bitcast.24), kind=kLoop, calls=%fused_computation | loop fusion | flops 2097152 | bytes 8404992 | tf_op jit(solution)/shard_map/jit(_where)/select_n | solution.py:74
  15.5 3.4 %collective-permute-done.1 = f32[128,256]{1,0:T(8,128)S(1)} collective-permute-done((f32[128,256]{1,0:T(8,128)S(1)}, f32[128,256]{1,0:T(8,128)S(1)}, u32[]{:S(2)}, u32[]{:S(2)}) %collective-permute-start.1) | collective-permute-done | bytes 131104 | tf_op jit(solution)/shard_map/ppermute | solution.py:11
  26.5 3.0 %collective-permute-start.4 = (f32[16,256]{1,0:T(8,128)S(1)}, f32[16,256]{1,0:T(8,128)S(1)}, u32[]{:S(2)}, u32[]{:S(2)}) collective-permute-start(f32[16,256]{1,0:T(8,128)S(1)} %constant_dynamic-slice_fusion.9), channel_id=1, source_target_pairs={{0,4},{1,5},{2,6},{3,7},{4,0},{5,1},{6,2},{7,3},{8,12},{9,13},{10,... | collective-permute-start | bytes 49160 | tf_op jit(solution)/shard_map/ppermute | solution.py:11
  31.5 3.0 %collective-permute-start.5 = (bf16[16,256]{1,0:T(8,128)(2,1)S(1)}, bf16[16,256]{1,0:T(8,128)(2,1)S(1)}, u32[]{:S(2)}, u32[]{:S(2)}) collective-permute-start(bf16[16,256]{1,0:T(8,128)(2,1)S(1)} %multiply_convert_fusion.2), channel_id=1, source_target_pairs={{0,4},{1,5},{2,6},{3,7},{4,0},{5,1},{6,2},{7,3},{8,12},{9,13},{10,... | collective-permute-start | bytes 24584 | tf_op jit(solution)/shard_map/ppermute | solution.py:11
  46.2 9.1 %collective-permute-start.9 = (bf16[256,256]{1,0:T(8,128)(2,1)S(1)}, bf16[256,256]{1,0:T(8,128)(2,1)S(1)}, u32[]{:S(2)}, u32[]{:S(2)}) collective-permute-start(bf16[256,256]{1,0:T(8,128)(2,1)S(1)} %pad_maximum_fusion.4), channel_id=1, source_target_pairs={{0,64},{64,0},{128,192},{192,128},{1,65},{65,1},{129,193},{193,129... | collective-permute-start | bytes 393224 | tf_op jit(solution)/shard_map/ppermute | solution.py:11
  55.3 3.1 %collective-permute-start.11 = (bf16[512,256]{1,0:T(8,128)(2,1)S(1)}, bf16[512,256]{1,0:T(8,128)(2,1)S(1)}, u32[]{:S(2)}, u32[]{:S(2)}) collective-permute-start(bf16[512,256]{1,0:T(8,128)(2,1)S(1)} %get-tuple-element.8), channel_id=1, source_target_pairs={{0,64},{64,128},{128,192},{1,65},{65,129},{129,193},{2,66},{66,130... | collective-permute-start | bytes 786440 | tf_op jit(solution)/shard_map/ppermute | solution.py:67
  64.7 18.0 %collective-permute-start.12 = (f32[256,256]{1,0:T(8,128)S(1)}, f32[256,256]{1,0:T(8,128)S(1)}, u32[]{:S(2)}, u32[]{:S(2)}) collective-permute-start(f32[256,256]{1,0:T(8,128)S(1)} %constant_dynamic-slice_fusion.8), channel_id=1, source_target_pairs={{0,64},{64,0},{128,192},{192,128},{1,65},{65,1},{129,193},{193,129... | collective-permute-start | bytes 786440 | tf_op jit(solution)/shard_map/ppermute | solution.py:11
  84.0 4.7 %collective-permute-done.13 = f32[128,256]{1,0:T(8,128)S(1)} collective-permute-done((f32[128,256]{1,0:T(8,128)S(1)}, f32[128,256]{1,0:T(8,128)S(1)}, u32[]{:S(2)}, u32[]{:S(2)}) %collective-permute-start.13) | collective-permute-done | bytes 131104 | tf_op jit(solution)/shard_map/ppermute | solution.py:11
  88.8 3.0 %collective-permute-start.14 = (f32[64,256]{1,0:T(8,128)S(1)}, f32[64,256]{1,0:T(8,128)S(1)}, u32[]{:S(2)}, u32[]{:S(2)}) collective-permute-start(f32[64,256]{1,0:T(8,128)S(1)} %constant_dynamic-slice_fusion.6), channel_id=1, source_target_pairs={{0,1},{1,0},{2,3},{3,2},{4,5},{5,4},{6,7},{7,6},{8,9},{9,8},{10,11... | collective-permute-start | bytes 196616 | tf_op jit(solution)/shard_map/ppermute | solution.py:11
  93.6 4.3 %collective-permute-done.15 = f32[32,256]{1,0:T(8,128)S(1)} collective-permute-done((f32[32,256]{1,0:T(8,128)S(1)}, f32[32,256]{1,0:T(8,128)S(1)}, u32[]{:S(2)}, u32[]{:S(2)}) %collective-permute-start.15) | collective-permute-done | bytes 32800 | tf_op jit(solution)/shard_map/ppermute | solution.py:11
  97.9 4.1 %collective-permute-done.16 = f32[16,256]{1,0:T(8,128)S(1)} collective-permute-done((f32[16,256]{1,0:T(8,128)S(1)}, f32[16,256]{1,0:T(8,128)S(1)}, u32[]{:S(2)}, u32[]{:S(2)}) %collective-permute-start.16) | collective-permute-done | bytes 16416 | tf_op jit(solution)/shard_map/ppermute | solution.py:11
  102.9 4.0 %collective-permute-done.17 = bf16[16,256]{1,0:T(8,128)(2,1)S(1)} collective-permute-done((bf16[16,256]{1,0:T(8,128)(2,1)S(1)}, bf16[16,256]{1,0:T(8,128)(2,1)S(1)}, u32[]{:S(2)}, u32[]{:S(2)}) %collective-permute-start.17) | collective-permute-done | bytes 8224 | tf_op jit(solution)/shard_map/ppermute | solution.py:11
  107.4 3.7 %collective-permute-done.18 = bf16[32,256]{1,0:T(8,128)(2,1)S(1)} collective-permute-done((bf16[32,256]{1,0:T(8,128)(2,1)S(1)}, bf16[32,256]{1,0:T(8,128)(2,1)S(1)}, u32[]{:S(2)}, u32[]{:S(2)}) %collective-permute-start.18) | collective-permute-done | bytes 16416 | tf_op jit(solution)/shard_map/ppermute | solution.py:11
  114.4 3.0 %collective-permute-done.20 = bf16[128,256]{1,0:T(8,128)(2,1)S(1)} collective-permute-done((bf16[128,256]{1,0:T(8,128)(2,1)S(1)}, bf16[128,256]{1,0:T(8,128)(2,1)S(1)}, u32[]{:S(2)}, u32[]{:S(2)}) %collective-permute-start.20) | collective-permute-done | bytes 65568 | tf_op jit(solution)/shard_map/ppermute | solution.py:11
  117.4 9.2 %collective-permute-start.21 = (bf16[256,256]{1,0:T(8,128)(2,1)S(1)}, bf16[256,256]{1,0:T(8,128)(2,1)S(1)}, u32[]{:S(2)}, u32[]{:S(2)}) collective-permute-start(bf16[256,256]{1,0:T(8,128)(2,1)S(1)} %pad_maximum_fusion.5), channel_id=1, source_target_pairs={{0,64},{64,0},{128,192},{192,128},{1,65},{65,1},{129,193},{193,129... | collective-permute-start | bytes 393224 | tf_op jit(solution)/shard_map/ppermute | solution.py:11
  134.6 19.9 %collective-permute-start.24 = (f32[256,256]{1,0:T(8,128)S(1)}, f32[256,256]{1,0:T(8,128)S(1)}, u32[]{:S(2)}, u32[]{:S(2)}) collective-permute-start(f32[256,256]{1,0:T(8,128)S(1)} %constant_dynamic-slice_fusion.3), channel_id=1, source_target_pairs={{0,64},{64,0},{128,192},{192,128},{1,65},{65,1},{129,193},{193,129... | collective-permute-start | bytes 786440 | tf_op jit(solution)/shard_map/ppermute | solution.py:11
  155.8 4.7 %collective-permute-done.25 = f32[128,256]{1,0:T(8,128)S(1)} collective-permute-done((f32[128,256]{1,0:T(8,128)S(1)}, f32[128,256]{1,0:T(8,128)S(1)}, u32[]{:S(2)}, u32[]{:S(2)}) %collective-permute-start.25) | collective-permute-done | bytes 131104 | tf_op jit(solution)/shard_map/ppermute | solution.py:11
  160.6 3.1 %collective-permute-done.26 = f32[64,256]{1,0:T(8,128)S(1)} collective-permute-done((f32[64,256]{1,0:T(8,128)S(1)}, f32[64,256]{1,0:T(8,128)S(1)}, u32[]{:S(2)}, u32[]{:S(2)}) %collective-permute-start.26) | collective-permute-done | bytes 65568 | tf_op jit(solution)/shard_map/ppermute | solution.py:11
  163.9 4.3 %collective-permute-done.27 = f32[32,256]{1,0:T(8,128)S(1)} collective-permute-done((f32[32,256]{1,0:T(8,128)S(1)}, f32[32,256]{1,0:T(8,128)S(1)}, u32[]{:S(2)}, u32[]{:S(2)}) %collective-permute-start.27) | collective-permute-done | bytes 32800 | tf_op jit(solution)/shard_map/ppermute | solution.py:11
  168.2 4.1 %collective-permute-done.28 = f32[16,256]{1,0:T(8,128)S(1)} collective-permute-done((f32[16,256]{1,0:T(8,128)S(1)}, f32[16,256]{1,0:T(8,128)S(1)}, u32[]{:S(2)}, u32[]{:S(2)}) %collective-permute-start.28) | collective-permute-done | bytes 16416 | tf_op jit(solution)/shard_map/ppermute | solution.py:11
  173.2 4.0 %collective-permute-done.29 = bf16[16,256]{1,0:T(8,128)(2,1)S(1)} collective-permute-done((bf16[16,256]{1,0:T(8,128)(2,1)S(1)}, bf16[16,256]{1,0:T(8,128)(2,1)S(1)}, u32[]{:S(2)}, u32[]{:S(2)}) %collective-permute-start.29) | collective-permute-done | bytes 8224 | tf_op jit(solution)/shard_map/ppermute | solution.py:11
  177.3 4.1 %collective-permute-done.30 = bf16[32,256]{1,0:T(8,128)(2,1)S(1)} collective-permute-done((bf16[32,256]{1,0:T(8,128)(2,1)S(1)}, bf16[32,256]{1,0:T(8,128)(2,1)S(1)}, u32[]{:S(2)}, u32[]{:S(2)}) %collective-permute-start.30) | collective-permute-done | bytes 16416 | tf_op jit(solution)/shard_map/ppermute | solution.py:11
  184.7 3.3 %collective-permute-done.32 = bf16[128,256]{1,0:T(8,128)(2,1)S(1)} collective-permute-done((bf16[128,256]{1,0:T(8,128)(2,1)S(1)}, bf16[128,256]{1,0:T(8,128)(2,1)S(1)}, u32[]{:S(2)}, u32[]{:S(2)}) %collective-permute-start.32) | collective-permute-done | bytes 65568 | tf_op jit(solution)/shard_map/ppermute | solution.py:11
  188.0 9.2 %collective-permute-start.33 = (bf16[256,256]{1,0:T(8,128)(2,1)S(1)}, bf16[256,256]{1,0:T(8,128)(2,1)S(1)}, u32[]{:S(2)}, u32[]{:S(2)}) collective-permute-start(bf16[256,256]{1,0:T(8,128)(2,1)S(1)} %pad_maximum_fusion.6), channel_id=1, source_target_pairs={{0,64},{64,0},{128,192},{192,128},{1,65},{65,1},{129,193},{193,129... | collective-permute-start | bytes 393224 | tf_op jit(solution)/shard_map/ppermute | solution.py:11
  (127 shorter events, 57.9 us)
Async XLA Ops:
  14.1 4.8 %collective-permute-start.1 = (f32[128,256]{1,0:T(8,128)S(1)}, f32[128,256]{1,0:T(8,128)S(1)}, u32[]{:S(2)}, u32[]{:S(2)}) collective-permute-start(f32[128,256]{1,0:T(8,128)S(1)} %constant_dynamic-slice_fusion.12), channel_id=1, source_target_pairs={{0,128},{64,192},{128,0},{192,64},{1,129},{65,193},{129,1},{193,65... | collective-permute-start | bytes 393224 | tf_op jit(solution)/shard_map/ppermute | solution.py:11
  22.1 4.4 %collective-permute-start.3 = (f32[32,256]{1,0:T(8,128)S(1)}, f32[32,256]{1,0:T(8,128)S(1)}, u32[]{:S(2)}, u32[]{:S(2)}) collective-permute-start(f32[32,256]{1,0:T(8,128)S(1)} %constant_dynamic-slice_fusion.10), channel_id=1, source_target_pairs={{0,2},{1,3},{2,0},{3,1},{4,6},{5,7},{6,4},{7,5},{8,10},{9,11},{10,... | collective-permute-start | bytes 98312 | tf_op jit(solution)/shard_map/ppermute | solution.py:11
  26.5 4.2 %collective-permute-start.4 = (f32[16,256]{1,0:T(8,128)S(1)}, f32[16,256]{1,0:T(8,128)S(1)}, u32[]{:S(2)}, u32[]{:S(2)}) collective-permute-start(f32[16,256]{1,0:T(8,128)S(1)} %constant_dynamic-slice_fusion.9), channel_id=1, source_target_pairs={{0,4},{1,5},{2,6},{3,7},{4,0},{5,1},{6,2},{7,3},{8,12},{9,13},{10,... | collective-permute-start | bytes 49160 | tf_op jit(solution)/shard_map/ppermute | solution.py:11
  31.5 4.1 %collective-permute-start.5 = (bf16[16,256]{1,0:T(8,128)(2,1)S(1)}, bf16[16,256]{1,0:T(8,128)(2,1)S(1)}, u32[]{:S(2)}, u32[]{:S(2)}) collective-permute-start(bf16[16,256]{1,0:T(8,128)(2,1)S(1)} %multiply_convert_fusion.2), channel_id=1, source_target_pairs={{0,4},{1,5},{2,6},{3,7},{4,0},{5,1},{6,2},{7,3},{8,12},{9,13},{10,... | collective-permute-start | bytes 24584 | tf_op jit(solution)/shard_map/ppermute | solution.py:11
  35.6 4.2 %collective-permute-start.6 = (bf16[32,256]{1,0:T(8,128)(2,1)S(1)}, bf16[32,256]{1,0:T(8,128)(2,1)S(1)}, u32[]{:S(2)}, u32[]{:S(2)}) collective-permute-start(bf16[32,256]{1,0:T(8,128)(2,1)S(1)} %pad_maximum_fusion.13), channel_id=1, source_target_pairs={{0,2},{1,3},{2,0},{3,1},{4,6},{5,7},{6,4},{7,5},{8,10},{9,11},{10,... | collective-permute-start | bytes 49160 | tf_op jit(solution)/shard_map/ppermute | solution.py:11
  46.2 12.2 %collective-permute-start.9 = (bf16[256,256]{1,0:T(8,128)(2,1)S(1)}, bf16[256,256]{1,0:T(8,128)(2,1)S(1)}, u32[]{:S(2)}, u32[]{:S(2)}) collective-permute-start(bf16[256,256]{1,0:T(8,128)(2,1)S(1)} %pad_maximum_fusion.4), channel_id=1, source_target_pairs={{0,64},{64,0},{128,192},{192,128},{1,65},{65,1},{129,193},{193,129... | collective-permute-start | bytes 393224 | tf_op jit(solution)/shard_map/ppermute | solution.py:11
  55.3 6.4 %collective-permute-start.11 = (bf16[512,256]{1,0:T(8,128)(2,1)S(1)}, bf16[512,256]{1,0:T(8,128)(2,1)S(1)}, u32[]{:S(2)}, u32[]{:S(2)}) collective-permute-start(bf16[512,256]{1,0:T(8,128)(2,1)S(1)} %get-tuple-element.8), channel_id=1, source_target_pairs={{0,64},{64,128},{128,192},{1,65},{65,129},{129,193},{2,66},{66,130... | collective-permute-start | bytes 786440 | tf_op jit(solution)/shard_map/ppermute | solution.py:67
  64.7 19.2 %collective-permute-start.12 = (f32[256,256]{1,0:T(8,128)S(1)}, f32[256,256]{1,0:T(8,128)S(1)}, u32[]{:S(2)}, u32[]{:S(2)}) collective-permute-start(f32[256,256]{1,0:T(8,128)S(1)} %constant_dynamic-slice_fusion.8), channel_id=1, source_target_pairs={{0,64},{64,0},{128,192},{192,128},{1,65},{65,1},{129,193},{193,129... | collective-permute-start | bytes 786440 | tf_op jit(solution)/shard_map/ppermute | solution.py:11
  83.9 4.8 %collective-permute-start.13 = (f32[128,256]{1,0:T(8,128)S(1)}, f32[128,256]{1,0:T(8,128)S(1)}, u32[]{:S(2)}, u32[]{:S(2)}) collective-permute-start(f32[128,256]{1,0:T(8,128)S(1)} %constant_dynamic-slice_fusion.7), channel_id=1, source_target_pairs={{0,128},{64,192},{128,0},{192,64},{1,129},{65,193},{129,1},{193,65... | collective-permute-start | bytes 393224 | tf_op jit(solution)/shard_map/ppermute | solution.py:11
  88.8 4.7 %collective-permute-start.14 = (f32[64,256]{1,0:T(8,128)S(1)}, f32[64,256]{1,0:T(8,128)S(1)}, u32[]{:S(2)}, u32[]{:S(2)}) collective-permute-start(f32[64,256]{1,0:T(8,128)S(1)} %constant_dynamic-slice_fusion.6), channel_id=1, source_target_pairs={{0,1},{1,0},{2,3},{3,2},{4,5},{5,4},{6,7},{7,6},{8,9},{9,8},{10,11... | collective-permute-start | bytes 196616 | tf_op jit(solution)/shard_map/ppermute | solution.py:11
  93.5 4.4 %collective-permute-start.15 = (f32[32,256]{1,0:T(8,128)S(1)}, f32[32,256]{1,0:T(8,128)S(1)}, u32[]{:S(2)}, u32[]{:S(2)}) collective-permute-start(f32[32,256]{1,0:T(8,128)S(1)} %constant_dynamic-slice_fusion.5), channel_id=1, source_target_pairs={{0,2},{1,3},{2,0},{3,1},{4,6},{5,7},{6,4},{7,5},{8,10},{9,11},{10,... | collective-permute-start | bytes 98312 | tf_op jit(solution)/shard_map/ppermute | solution.py:11
  97.8 4.2 %collective-permute-start.16 = (f32[16,256]{1,0:T(8,128)S(1)}, f32[16,256]{1,0:T(8,128)S(1)}, u32[]{:S(2)}, u32[]{:S(2)}) collective-permute-start(f32[16,256]{1,0:T(8,128)S(1)} %constant_dynamic-slice_fusion.4), channel_id=1, source_target_pairs={{0,4},{1,5},{2,6},{3,7},{4,0},{5,1},{6,2},{7,3},{8,12},{9,13},{10,... | collective-permute-start | bytes 49160 | tf_op jit(solution)/shard_map/ppermute | solution.py:11
  102.8 4.1 %collective-permute-start.17 = (bf16[16,256]{1,0:T(8,128)(2,1)S(1)}, bf16[16,256]{1,0:T(8,128)(2,1)S(1)}, u32[]{:S(2)}, u32[]{:S(2)}) collective-permute-start(bf16[16,256]{1,0:T(8,128)(2,1)S(1)} %multiply_convert_fusion.1), channel_id=1, source_target_pairs={{0,4},{1,5},{2,6},{3,7},{4,0},{5,1},{6,2},{7,3},{8,12},{9,13},{10,... | collective-permute-start | bytes 24584 | tf_op jit(solution)/shard_map/ppermute | solution.py:11
  106.9 4.2 %collective-permute-start.18 = (bf16[32,256]{1,0:T(8,128)(2,1)S(1)}, bf16[32,256]{1,0:T(8,128)(2,1)S(1)}, u32[]{:S(2)}, u32[]{:S(2)}) collective-permute-start(bf16[32,256]{1,0:T(8,128)(2,1)S(1)} %pad_maximum_fusion.14), channel_id=1, source_target_pairs={{0,2},{1,3},{2,0},{3,1},{4,6},{5,7},{6,4},{7,5},{8,10},{9,11},{10,... | collective-permute-start | bytes 49160 | tf_op jit(solution)/shard_map/ppermute | solution.py:11
  117.4 11.2 %collective-permute-start.21 = (bf16[256,256]{1,0:T(8,128)(2,1)S(1)}, bf16[256,256]{1,0:T(8,128)(2,1)S(1)}, u32[]{:S(2)}, u32[]{:S(2)}) collective-permute-start(bf16[256,256]{1,0:T(8,128)(2,1)S(1)} %pad_maximum_fusion.5), channel_id=1, source_target_pairs={{0,64},{64,0},{128,192},{192,128},{1,65},{65,1},{129,193},{193,129... | collective-permute-start | bytes 393224 | tf_op jit(solution)/shard_map/ppermute | solution.py:11
  126.7 5.2 %collective-permute-start.23 = (bf16[512,256]{1,0:T(8,128)(2,1)S(1)}, bf16[512,256]{1,0:T(8,128)(2,1)S(1)}, u32[]{:S(2)}, u32[]{:S(2)}) collective-permute-start(bf16[512,256]{1,0:T(8,128)(2,1)S(1)} %get-tuple-element.7), channel_id=1, source_target_pairs={{0,64},{64,128},{128,192},{1,65},{65,129},{129,193},{2,66},{66,130... | collective-permute-start | bytes 786440 | tf_op jit(solution)/shard_map/ppermute | solution.py:67
  134.6 21.0 %collective-permute-start.24 = (f32[256,256]{1,0:T(8,128)S(1)}, f32[256,256]{1,0:T(8,128)S(1)}, u32[]{:S(2)}, u32[]{:S(2)}) collective-permute-start(f32[256,256]{1,0:T(8,128)S(1)} %constant_dynamic-slice_fusion.3), channel_id=1, source_target_pairs={{0,64},{64,0},{128,192},{192,128},{1,65},{65,1},{129,193},{193,129... | collective-permute-start | bytes 786440 | tf_op jit(solution)/shard_map/ppermute | solution.py:11
  155.7 4.8 %collective-permute-start.25 = (f32[128,256]{1,0:T(8,128)S(1)}, f32[128,256]{1,0:T(8,128)S(1)}, u32[]{:S(2)}, u32[]{:S(2)}) collective-permute-start(f32[128,256]{1,0:T(8,128)S(1)} %constant_dynamic-slice_fusion.2), channel_id=1, source_target_pairs={{0,128},{64,192},{128,0},{192,64},{1,129},{65,193},{129,1},{193,65... | collective-permute-start | bytes 393224 | tf_op jit(solution)/shard_map/ppermute | solution.py:11
  163.8 4.4 %collective-permute-start.27 = (f32[32,256]{1,0:T(8,128)S(1)}, f32[32,256]{1,0:T(8,128)S(1)}, u32[]{:S(2)}, u32[]{:S(2)}) collective-permute-start(f32[32,256]{1,0:T(8,128)S(1)} %constant_dynamic-slice_fusion), channel_id=1, source_target_pairs={{0,2},{1,3},{2,0},{3,1},{4,6},{5,7},{6,4},{7,5},{8,10},{9,11},{10,... | collective-permute-start | bytes 98312 | tf_op jit(solution)/shard_map/ppermute | solution.py:11
  168.1 4.2 %collective-permute-start.28 = (f32[16,256]{1,0:T(8,128)S(1)}, f32[16,256]{1,0:T(8,128)S(1)}, u32[]{:S(2)}, u32[]{:S(2)}) collective-permute-start(f32[16,256]{1,0:T(8,128)S(1)} %constant_dynamic-slice_fusion.14), channel_id=1, source_target_pairs={{0,4},{1,5},{2,6},{3,7},{4,0},{5,1},{6,2},{7,3},{8,12},{9,13},{10,... | collective-permute-start | bytes 49160 | tf_op jit(solution)/shard_map/ppermute | solution.py:11
  173.1 4.1 %collective-permute-start.29 = (bf16[16,256]{1,0:T(8,128)(2,1)S(1)}, bf16[16,256]{1,0:T(8,128)(2,1)S(1)}, u32[]{:S(2)}, u32[]{:S(2)}) collective-permute-start(bf16[16,256]{1,0:T(8,128)(2,1)S(1)} %multiply_convert_fusion), channel_id=1, source_target_pairs={{0,4},{1,5},{2,6},{3,7},{4,0},{5,1},{6,2},{7,3},{8,12},{9,13},{10,... | collective-permute-start | bytes 24584 | tf_op jit(solution)/shard_map/ppermute | solution.py:11
  177.2 4.2 %collective-permute-start.30 = (bf16[32,256]{1,0:T(8,128)(2,1)S(1)}, bf16[32,256]{1,0:T(8,128)(2,1)S(1)}, u32[]{:S(2)}, u32[]{:S(2)}) collective-permute-start(bf16[32,256]{1,0:T(8,128)(2,1)S(1)} %pad_maximum_fusion.15), channel_id=1, source_target_pairs={{0,2},{1,3},{2,0},{3,1},{4,6},{5,7},{6,4},{7,5},{8,10},{9,11},{10,... | collective-permute-start | bytes 49160 | tf_op jit(solution)/shard_map/ppermute | solution.py:11
  184.5 3.5 %collective-permute-start.32 = (bf16[128,256]{1,0:T(8,128)(2,1)S(1)}, bf16[128,256]{1,0:T(8,128)(2,1)S(1)}, u32[]{:S(2)}, u32[]{:S(2)}) collective-permute-start(bf16[128,256]{1,0:T(8,128)(2,1)S(1)} %pad_maximum_fusion.9), channel_id=1, source_target_pairs={{0,128},{64,192},{128,0},{192,64},{1,129},{65,193},{129,1},{193,65... | collective-permute-start | bytes 196616 | tf_op jit(solution)/shard_map/ppermute | solution.py:11
  188.0 10.2 %collective-permute-start.33 = (bf16[256,256]{1,0:T(8,128)(2,1)S(1)}, bf16[256,256]{1,0:T(8,128)(2,1)S(1)}, u32[]{:S(2)}, u32[]{:S(2)}) collective-permute-start(bf16[256,256]{1,0:T(8,128)(2,1)S(1)} %pad_maximum_fusion.6), channel_id=1, source_target_pairs={{0,64},{64,0},{128,192},{192,128},{1,65},{65,1},{129,193},{193,129... | collective-permute-start | bytes 393224 | tf_op jit(solution)/shard_map/ppermute | solution.py:11
  (15 other events, 78.6 us)

commit v2 on v0

v2 whole, which is shorter than its diff:
```python
import jax
import jax.numpy as jnp
from jax import lax
from jax.sharding import PartitionSpec as P

STEPS = 3


def swap_src(block, mask):
    size = lax.axis_size("src")
    route = [(i, i ^ mask) for i in range(size)]
    return lax.ppermute(block, ("lag", "src"), route)


def bit_masks(axis):
    masks = []
    mask = 1
    while mask < lax.axis_size(axis):
        masks.append(mask)
        mask *= 2
    return masks


def reduce_scatter_src(x):
    offset = 0
    for mask in bit_masks("src"):
        half = x.shape[0] // 2
        bit = (lax.axis_index("src") // mask) % 2
        keep = lax.dynamic_slice_in_dim(x, bit * half, half, 0)
        send = lax.dynamic_slice_in_dim(x, (1 - bit) * half, half, 0)
        x = keep + swap_src(send, mask)
        offset = offset + bit * half
    return x, offset


def all_gather_src(y):
    for mask in reversed(bit_masks("src")):
        bit = (lax.axis_index("src") // mask) % 2
        other = swap_src(y, mask)
        first = jnp.where(bit == 0, y, other)
        second = jnp.where(bit == 0, other, y)
        y = jnp.concatenate([first, second], axis=0)
    return y


def reduce_to_lag0(x):
    n = lax.axis_size("lag")
    for mask in bit_masks("lag"):
        route = [(i, i - mask) for i in range(n) if i % (2 * mask) == mask]
        x = x + lax.ppermute(x, "lag", route)
    return x


def broadcast_from_lag0(x):
    n = lax.axis_size("lag")
    pos = lax.axis_index("lag")
    for mask in reversed(bit_masks("lag")):
        route = [(i, i + mask) for i in range(n) if i % (2 * mask) == 0]
        arrived = lax.ppermute(x, "lag", route)
        x = jnp.where(pos % (2 * mask) == mask, arrived, x)
    return x


def to_sources(rates_block):
    recv_n = lax.axis_size("recv")
    src_n = lax.axis_size("src")
    route = [(s * src_n + r, r * src_n + s) for r in range(recv_n) for s in range(src_n)]
    return lax.ppermute(rates_block, ("lag", "recv", "src"), route)


def friction(stress, offset, background, classes, rate_scale, stress_scale):
    row_total = stress.shape[0]
    element_class = lax.dynamic_slice_in_dim(classes, offset, row_total, 0)
    loaded = lax.dynamic_slice_in_dim(background, offset, row_total, 0)
    selector = (
        element_class[:, None] == jnp.arange(rate_scale.shape[0], dtype=jnp.int32)[None, :]
    ).astype(jnp.float32)
    limit = jnp.sum(selector * rate_scale[None, :], axis=1)[:, None]
    width_scale = jnp.sum(selector * stress_scale[None, :], axis=1)[:, None]
    return (limit * jnp.tanh((loaded + stress) / width_scale)).astype(jnp.bfloat16)


def local(kernel, causal_mask, history, background, classes, rate_scale, stress_scale):
    rows_here, lag_here, cols_here = kernel.shape
    block_size = rows_here // causal_mask.shape[0]
    allowed = jnp.repeat(jnp.repeat(causal_mask, block_size, 0), block_size, 2) > 0
    masked = jnp.where(allowed, kernel, jnp.zeros_like(kernel))
    masked_rows = masked.reshape(rows_here, lag_here * cols_here)
    scenarios = history.shape[2]
    lag_n = lax.axis_size("lag")

    def rates_of(partial):
        share, offset = reduce_scatter_src(partial)
        return all_gather_src(friction(share, offset, background, classes, rate_scale, stress_scale))

    ahead = STEPS - 1
    earlier = lax.ppermute(history[lag_here - ahead:], "lag", [(i, i + 1) for i in range(lag_n - 1)])
    extended = jnp.concatenate([earlier, history], axis=0)
    first = jnp.dot(masked_rows, history.reshape(lag_here * cols_here, scenarios),
                    preferred_element_type=jnp.float32)
    later = []
    for step_index in range(1, STEPS):
        shifted = extended[ahead - step_index: ahead - step_index + lag_here]
        later.append(jnp.dot(masked_rows, shifted.reshape(lag_here * cols_here, scenarios),
                             preferred_element_type=jnp.float32))
    later = reduce_to_lag0(jnp.concatenate(later, axis=1))

    produced = [rates_of(reduce_to_lag0(first))]
    sources = []
    for step_index in range(1, STEPS):
        sources.append(to_sources(produced[-1]))
        partial = later[:, (step_index - 1) * scenarios: step_index * scenarios]
        for lag_pos in range(step_index):
            partial = partial + jnp.dot(masked[:, lag_pos, :], sources[step_index - 1 - lag_pos],
                                        preferred_element_type=jnp.float32)
        produced.append(rates_of(partial))
    return jnp.stack([broadcast_from_lag0(r) for r in produced])


def solution(mesh):
    in_specs = (
        P("recv", "lag", "src"),
        P("recv", "lag", "src"),
        P("lag", "src", None),
        P("recv", None),
        P("recv"),
        P(),
        P(),
    )
    out_specs = P(None, "recv", None)
    return jax.shard_map(local, mesh=mesh, in_specs=in_specs, out_specs=out_specs, check_vma=False)
```

time: 817 us -> 255 us (0.31)
  waiting for transfers between devices: 524 us -> 159 us
  blocking collectives: 234 us -> 0 us
  starting transfers between devices: 4.01 us -> 41.9 us
  local copies, waits for them, and re-layouts: 4.31 us -> 25.4 us
  between operations: 13.3 us -> 0.94 us
    reduce_scatter x3 -> x0, waiting for transfers between devices: 453 us -> none  [local(): lax.psum_scatter(jnp.dot(masked_rows, stacked, preferred_element_type=jnp...]
    all_gather x3 -> x0, blocking collectives: 234 us -> none  [local(): new_rates = lax.all_gather(local_rates, ('lag', 'src'), axis=0, tiled=True)]
    ppermute x2 -> x31, waiting for transfers between devices: 5.36 us -> 159 us  [the longest x6 156 us: broadcast_from_lag0(): arrived = lax.ppermute(x, 'lag', route)]
    all_gather x2 -> x0, waiting for transfers between devices: 65.9 us -> none  [local(): gathered = lax.all_gather(new_rates, 'recv', axis=0, tiled=True)]
    ppermute x2 -> x31, starting transfers between devices: 3.84 us -> 41.9 us  [the longest x4 20.7 us: reduce_to_lag0(): x = x + lax.ppermute(x, 'lag', route)]
    broadcast_in_dim x0 -> x1, local copies, waits for them, and re-layouts: none -> 14.7 us  [local(): jnp.repeat(jnp.repeat(causal_mask, block_size, 0), block_size, 2) > 0]
  transfers between devices with their start and end apart: 7 -> 31, of which waited for: 7 -> 4; matrix products, arithmetic and copies ran while one was open for 0% -> 5% of each run, Pallas kernels for 0% -> 0%
where the time goes in v2:
time: 255 us; the launch traced here: 251 us
  waiting for transfers between devices  159 us (62%)
  starting transfers between devices  41.9 us (16%)
  local copies, waits for them, and re-layouts  25.4 us (10%)
  other arithmetic  13.2 us (5%)
  matrix products  11.1 us (4%)
    ppermute x6, waiting for transfers between devices, broadcast_from_lag0(): arrived = lax.ppermute(x, 'lag', route)  156 us
    ppermute x4, starting transfers between devices, reduce_to_lag0(): x = x + lax.ppermute(x, 'lag', route)  20.7 us
    broadcast_in_dim x1, local copies, waits for them, and re-layouts, local(): jnp.repeat(jnp.repeat(causal_mask, block_size, 0), block_size, 2) > 0  14.7 us
    ppermute x18, starting transfers between devices, swap_src(): return lax.ppermute(block, ('lag', 'src'), route)  12 us
    ppermute x6, starting transfers between devices, broadcast_from_lag0(): arrived = lax.ppermute(x, 'lag', route)  5.91 us
    dot_general x2, matrix products, local(): jnp.dot(masked_rows, shifted.reshape(lag_here * cols_here, scenarios), pr...  5.82 us
    gt x2, local copies, waits for them, and re-layouts, local(): jnp.repeat(jnp.repeat(causal_mask, block_size, 0), block_size, 2) > 0  5.13 us
  transfers between devices with their start and end apart: 31, of which 4 were waited for; matrix products, arithmetic and copies ran while one was open for 5% of the time, Pallas kernels for 0%

profile of v2, /device:TPU:225, one launch (start us, length us, event | category | flops | bytes accessed | tf_op | source)
XLA Modules:
  0.0 251.2 jit_solution(6550606728832303186)
XLA Ops:
  1.0 14.7 %broadcast_in_dim.7 = pred[512,8,4,128]{3,2,0,1:T(4,128)(4,1)} broadcast(pred[512,8,4]{2,0,1:T(8,128)(4,1)S(1)} %bitcast.33), dimensions={0,1,2} | broadcast | bytes 2113536 | tf_op jit(solution)/shard_map/broadcast_in_dim | solution.py:86
  15.7 5.0 %gt.17 = pred[512,8,512]{2,0,1:T(8,128)(4,1)S(1)} reshape(pred[512,8,4,128]{3,2,0,1:T(4,128)(4,1)} %broadcast_in_dim.7) | data formatting | bytes 4194304 | tf_op jit(solution)/shard_map/gt | solution.py:86
  20.7 5.0 %copy_select_fusion = bf16[512,8,512]{2,0,1:T(8,128)(2,1)S(1)} fusion(pred[512,8,512]{2,0,1:T(8,128)(4,1)S(1)} %gt.17, bf16[512,8,512]{2,1,0:T(8,128)(2,1)} %param.7), kind=kLoop, calls=%fused_computation | loop fusion | flops 2097152 | bytes 10485760 | tf_op jit(solution)/shard_map/jit(_where)/select_n | solution.py:87
  25.8 1.2 convolution_bitcast_fusion
  27.8 3.4 %collective-permute-start = (f32[512,256]{1,0:T(8,128)S(1)}, f32[512,256]{1,0:T(8,128)}, u32[]{:S(2)}, u32[]{:S(2)}) collective-permute-start(f32[512,256]{1,0:T(8,128)S(1)} %convolution_bitcast_fusion), channel_id=1, source_target_pairs={{64,0},{192,128},{65,1},{193,129},{66,2},{194,130},{67,3},{195,131... | collective-permute-start | bytes 1572872 | tf_op jit(solution)/shard_map/ppermute | solution.py:50
  31.2 2.9 %copy.23 = bf16[8,512,256]{1,2,0:T(8,128)(2,1)S(1)} copy(bf16[8,512,256]{2,1,0:T(8,128)(2,1)} %param.9) | data formatting | bytes 4194304 | tf_op args[2]
  34.9 1.9 collective-permute-start.10
  36.8 1.1 add.151
  37.9 1.5 collective-permute-start.1
  40.2 3.0 %collective-permute-done.10 = bf16[2,512,256]{1,2,0:T(8,128)(2,1)} collective-permute-done((bf16[2,512,256]{1,2,0:T(8,128)(2,1)}, bf16[2,512,256]{1,2,0:T(8,128)(2,1)}, u32[]{:S(2)}, u32[]{:S(2)}) %collective-permute-start.10) | collective-permute-done | bytes 524320 | tf_op jit(solution)/shard_map/ppermute | solution.py:97
  43.2 3.5 %fusion.6 = f32[512,256]{1,0:T(8,128)S(1)} fusion(bf16[512,8,512]{2,0,1:T(8,128)(2,1)} %copy-done, bf16[2,512,256]{1,2,0:T(8,128)(2,1)} %collective-permute-done.10, bf16[8,512,256]{1,2,0:T(8,128)(2,1)S(1)} %copy.23), kind=kOutput, calls=%fused_computation.9 | convolution fusion | flops 1074790400 | bytes 7340032 | tf_op jit(solution)/shard_map/dot_general | solution.py:104
  46.7 1.1 add.152
  48.6 2.3 fusion.5
  51.8 15.1 %collective-permute-start.11 = (f32[512,512]{1,0:T(8,128)S(1)}, f32[512,512]{1,0:T(8,128)S(1)}, u32[]{:S(2)}, u32[]{:S(2)}) collective-permute-start(f32[512,512]{1,0:T(8,128)S(1)} %pad_maximum_fusion.4), channel_id=1, source_target_pairs={{64,0},{192,128},{65,1},{193,129},{66,2},{194,130},{67,3},{195,131... | collective-permute-start | bytes 3145736 | tf_op jit(solution)/shard_map/ppermute | solution.py:50
  72.8 1.3 slice_add_fusion.1
  80.2 1.3 fusion.11
  81.6 1.4 fusion.10
  90.5 1.3 collective-permute-start.9
  91.8 1.3 collective-permute-start.21
  93.2 1.3 collective-permute-start.30
  94.5 151.2 %collective-permute-done.9 = bf16[512,256]{1,0:T(8,128)(2,1)S(1)} collective-permute-done((bf16[512,256]{1,0:T(8,128)(2,1)S(1)}, bf16[512,256]{1,0:T(8,128)(2,1)S(1)}, u32[]{:S(2)}, u32[]{:S(2)}) %collective-permute-start.9) | collective-permute-done | bytes 262176 | tf_op jit(solution)/shard_map/ppermute | solution.py:59
  245.8 1.6 collective-permute-done.21
  247.5 2.8 %collective-permute-done.30 = bf16[512,256]{1,0:T(8,128)(2,1)S(1)} collective-permute-done((bf16[512,256]{1,0:T(8,128)(2,1)S(1)}, bf16[512,256]{1,0:T(8,128)(2,1)S(1)}, u32[]{:S(2)}, u32[]{:S(2)}) %collective-permute-start.30) | collective-permute-done | bytes 262176 | tf_op jit(solution)/shard_map/ppermute | solution.py:59
  250.3 1.0 pad_maximum_fusion.5
  (112 shorter events, 23.9 us)
Async XLA Ops:
  27.8 9.0 %collective-permute-start = (f32[512,256]{1,0:T(8,128)S(1)}, f32[512,256]{1,0:T(8,128)}, u32[]{:S(2)}, u32[]{:S(2)}) collective-permute-start(f32[512,256]{1,0:T(8,128)S(1)} %convolution_bitcast_fusion), channel_id=1, source_target_pairs={{64,0},{192,128},{65,1},{193,129},{66,2},{194,130},{67,3},{195,131... | collective-permute-start | bytes 1572872 | tf_op jit(solution)/shard_map/ppermute | solution.py:50
  34.9 8.3 %collective-permute-start.10 = (bf16[2,512,256]{1,2,0:T(8,128)(2,1)}, bf16[2,512,256]{1,2,0:T(8,128)(2,1)}, u32[]{:S(2)}, u32[]{:S(2)}) collective-permute-start(bf16[2,512,256]{1,2,0:T(8,128)(2,1)} %slice.29), channel_id=1, source_target_pairs={{0,64},{64,128},{128,192},{1,65},{65,129},{129,193},{2,66},{66,130... | collective-permute-start | bytes 1572872 | tf_op jit(solution)/shard_map/ppermute | solution.py:97
  37.9 8.8 %collective-permute-start.1 = (f32[512,256]{1,0:T(8,128)S(1)}, f32[512,256]{1,0:T(8,128)}, u32[]{:S(2)}, u32[]{:S(2)}) collective-permute-start(f32[512,256]{1,0:T(8,128)S(1)} %add.151), channel_id=1, source_target_pairs={{128,0},{129,1},{130,2},{131,3},{132,4},{133,5},{134,6},{135,7},{1... | collective-permute-start | bytes 1572872 | tf_op jit(solution)/shard_map/ppermute | solution.py:50
  47.9 3.1 %collective-permute-start.2 = (f32[256,256]{1,0:T(8,128)S(1)}, f32[256,256]{1,0:T(8,128)S(1)}, u32[]{:S(2)}, u32[]{:S(2)}) collective-permute-start(f32[256,256]{1,0:T(8,128)S(1)} %constant_dynamic-slice_fusion.7), channel_id=1, source_target_pairs={{0,1},{1,0},{2,3},{3,2},{4,5},{5,4},{6,7},{7,6},{8,9},{9,8},{10,11... | collective-permute-start | bytes 786440 | tf_op jit(solution)/shard_map/ppermute | solution.py:12
  51.0 15.9 %collective-permute-start.3 = (f32[128,256]{1,0:T(8,128)S(1)}, f32[128,256]{1,0:T(8,128)S(1)}, u32[]{:S(2)}, u32[]{:S(2)}) collective-permute-start(f32[128,256]{1,0:T(8,128)S(1)} %constant_dynamic-slice_fusion.6), channel_id=1, source_target_pairs={{0,2},{1,3},{2,0},{3,1},{4,6},{5,7},{6,4},{7,5},{8,10},{9,11},{10,... | collective-permute-start | bytes 393224 | tf_op jit(solution)/shard_map/ppermute | solution.py:12
  51.8 18.3 %collective-permute-start.11 = (f32[512,512]{1,0:T(8,128)S(1)}, f32[512,512]{1,0:T(8,128)S(1)}, u32[]{:S(2)}, u32[]{:S(2)}) collective-permute-start(f32[512,512]{1,0:T(8,128)S(1)} %pad_maximum_fusion.4), channel_id=1, source_target_pairs={{64,0},{192,128},{65,1},{193,129},{66,2},{194,130},{67,3},{195,131... | collective-permute-start | bytes 3145736 | tf_op jit(solution)/shard_map/ppermute | solution.py:50
  67.0 0.8 collective-permute-start.4
  68.7 0.7 collective-permute-start.5
  69.4 1.6 collective-permute-start.6
  70.3 2.3 collective-permute-start.12
  71.1 0.7 collective-permute-start.7
  71.9 0.9 collective-permute-start.13
  74.2 0.7 collective-permute-start.14
  74.9 0.7 collective-permute-start.15
  79.5 0.7 collective-permute-start.22
  82.9 0.7 collective-permute-start.23
  83.7 0.7 collective-permute-start.24
  87.5 2.1 collective-permute-start.28
  88.2 2.2 collective-permute-start.8
  88.9 2.8 %collective-permute-start.20 = (bf16[512,256]{1,0:T(8,128)(2,1)S(1)}, bf16[512,256]{1,0:T(8,128)(2,1)S(1)}, u32[]{:S(2)}, u32[]{:S(2)}) collective-permute-start(bf16[512,256]{1,0:T(8,128)(2,1)S(1)} %pad_maximum_fusion.7), channel_id=1, source_target_pairs={{0,128},{1,129},{2,130},{3,131},{4,132},{5,133},{6,134},{7,135},{8... | collective-permute-start | bytes 786440 | tf_op jit(solution)/shard_map/ppermute | solution.py:59
  89.7 3.5 %collective-permute-start.29 = (bf16[512,256]{1,0:T(8,128)(2,1)S(1)}, bf16[512,256]{1,0:T(8,128)(2,1)S(1)}, u32[]{:S(2)}, u32[]{:S(2)}) collective-permute-start(bf16[512,256]{1,0:T(8,128)(2,1)S(1)} %pad_maximum_fusion.8), channel_id=1, source_target_pairs={{0,128},{1,129},{2,130},{3,131},{4,132},{5,133},{6,134},{7,135},{8... | collective-permute-start | bytes 786440 | tf_op jit(solution)/shard_map/ppermute | solution.py:59
  90.5 155.3 %collective-permute-start.9 = (bf16[512,256]{1,0:T(8,128)(2,1)S(1)}, bf16[512,256]{1,0:T(8,128)(2,1)S(1)}, u32[]{:S(2)}, u32[]{:S(2)}) collective-permute-start(bf16[512,256]{1,0:T(8,128)(2,1)S(1)} %broadcast_select_fusion.2), channel_id=1, source_target_pairs={{0,64},{128,192},{1,65},{129,193},{2,66},{130,194},{3,67},{131,195... | collective-permute-start | bytes 786440 | tf_op jit(solution)/shard_map/ppermute | solution.py:59
  91.8 155.6 %collective-permute-start.21 = (bf16[512,256]{1,0:T(8,128)(2,1)S(1)}, bf16[512,256]{1,0:T(8,128)(2,1)S(1)}, u32[]{:S(2)}, u32[]{:S(2)}) collective-permute-start(bf16[512,256]{1,0:T(8,128)(2,1)S(1)} %broadcast_select_fusion.1), channel_id=1, source_target_pairs={{0,64},{128,192},{1,65},{129,193},{2,66},{130,194},{3,67},{131,195... | collective-permute-start | bytes 786440 | tf_op jit(solution)/shard_map/ppermute | solution.py:59
  93.2 157.0 %collective-permute-start.30 = (bf16[512,256]{1,0:T(8,128)(2,1)S(1)}, bf16[512,256]{1,0:T(8,128)(2,1)S(1)}, u32[]{:S(2)}, u32[]{:S(2)}) collective-permute-start(bf16[512,256]{1,0:T(8,128)(2,1)S(1)} %broadcast_select_fusion), channel_id=1, source_target_pairs={{0,64},{128,192},{1,65},{129,193},{2,66},{130,194},{3,67},{131,195... | collective-permute-start | bytes 786440 | tf_op jit(solution)/shard_map/ppermute | solution.py:59
  (12 other events, 53.7 us)

commit v3 on v2

v3 whole, which is shorter than its diff:
```python
import jax
import jax.numpy as jnp
from jax import lax
from jax.sharding import PartitionSpec as P

STEPS = 3


def bit_masks(axis):
    masks = []
    mask = 1
    while mask < lax.axis_size(axis):
        masks.append(mask)
        mask *= 2
    return masks


def swap(block, axis, mask):
    size = lax.axis_size(axis)
    return lax.ppermute(block, axis, [(i, i ^ mask) for i in range(size)])


def reduce_scatter_lag(x):
    offset = 0
    for mask in bit_masks("lag"):
        half = x.shape[0] // 2
        bit = (lax.axis_index("lag") // mask) % 2
        keep = lax.dynamic_slice_in_dim(x, bit * half, half, 0)
        send = lax.dynamic_slice_in_dim(x, (1 - bit) * half, half, 0)
        x = keep + swap(send, "lag", mask)
        offset = offset + bit * half
    return x, offset


def all_reduce_src(x):
    for mask in bit_masks("src"):
        x = x + swap(x, "src", mask)
    return x


def all_gather_lag(y):
    for mask in reversed(bit_masks("lag")):
        bit = (lax.axis_index("lag") // mask) % 2
        other = swap(y, "lag", mask)
        first = jnp.where(bit == 0, y, other)
        second = jnp.where(bit == 0, other, y)
        y = jnp.concatenate([first, second], axis=0)
    return y


def to_sources(rates_block):
    recv_n = lax.axis_size("recv")
    src_n = lax.axis_size("src")
    route = [(s * src_n + r, r * src_n + s) for r in range(recv_n) for s in range(src_n)]
    return lax.ppermute(rates_block, ("lag", "recv", "src"), route)


def friction(stress, offset, background, classes, rate_scale, stress_scale):
    row_total = stress.shape[0]
    element_class = lax.dynamic_slice_in_dim(classes, offset, row_total, 0)
    loaded = lax.dynamic_slice_in_dim(background, offset, row_total, 0)
    selector = (
        element_class[:, None] == jnp.arange(rate_scale.shape[0], dtype=jnp.int32)[None, :]
    ).astype(jnp.float32)
    limit = jnp.sum(selector * rate_scale[None, :], axis=1)[:, None]
    width_scale = jnp.sum(selector * stress_scale[None, :], axis=1)[:, None]
    return (limit * jnp.tanh((loaded + stress) / width_scale)).astype(jnp.bfloat16)


def local(kernel, causal_mask, history, background, classes, rate_scale, stress_scale):
    rows_here, lag_here, cols_here = kernel.shape
    block_size = rows_here // causal_mask.shape[0]
    allowed = jnp.repeat(jnp.repeat(causal_mask, block_size, 0), block_size, 2) > 0
    masked_rows = jnp.where(allowed, kernel, jnp.zeros_like(kernel)).reshape(
        rows_here, lag_here * cols_here
    )
    scenarios = history.shape[2]
    lag_n = lax.axis_size("lag")

    def rates_of(partial):
        share, offset = reduce_scatter_lag(partial)
        total = all_reduce_src(share)
        return all_gather_lag(friction(total, offset, background, classes, rate_scale, stress_scale))

    ahead = STEPS - 1
    earlier = lax.ppermute(history[lag_here - ahead:], "lag", [(i, i + 1) for i in range(lag_n - 1)])
    extended = jnp.concatenate([earlier, history], axis=0)
    known = [jnp.dot(masked_rows, history.reshape(lag_here * cols_here, scenarios),
                     preferred_element_type=jnp.float32)]
    for step_index in range(1, STEPS):
        shifted = extended[ahead - step_index: ahead - step_index + lag_here]
        known.append(jnp.dot(masked_rows, shifted.reshape(lag_here * cols_here, scenarios),
                             preferred_element_type=jnp.float32))

    produced = [rates_of(known[0])]
    sources = []
    for step_index in range(1, STEPS):
        sources.append(to_sources(produced[-1]))
        partial = known[step_index]
        for lag_pos in range(step_index):
            partial = partial + jnp.dot(
                masked_rows[:, lag_pos * cols_here: (lag_pos + 1) * cols_here],
                sources[step_index - 1 - lag_pos],
                preferred_element_type=jnp.float32,
            )
        produced.append(rates_of(partial))
    return jnp.stack(produced)


def solution(mesh):
    in_specs = (
        P("recv", "lag", "src"),
        P("recv", "lag", "src"),
        P("lag", "src", None),
        P("recv", None),
        P("recv"),
        P(),
        P(),
    )
    out_specs = P(None, "recv", None)
    return jax.shard_map(local, mesh=mesh, in_specs=in_specs, out_specs=out_specs, check_vma=False)
```

time: 255 us -> 164 us (0.64); the launches traced: 251 us -> 164 us
  waiting for transfers between devices: 159 us -> 58 us
  starting transfers between devices: 41.9 us -> 78.5 us
  local copies, waits for them, and re-layouts: 25.4 us -> 6.27 us
  matrix products: 11.1 us -> 8.16 us
    ppermute x28 -> x21, waiting for transfers between devices: 156 us -> 58 us  [swap(): return lax.ppermute(block, axis, [(i, i ^ mask) for i in range(size)])]
    ppermute x28 -> x21, starting transfers between devices: 38.6 us -> 69.9 us  [swap(): return lax.ppermute(block, axis, [(i, i ^ mask) for i in range(size)])]
    broadcast_in_dim x1 -> x0, local copies, waits for them, and re-layouts: 14.7 us -> none  [local(): jnp.repeat(jnp.repeat(causal_mask, block_size, 0), block_size, 2) > 0]
    gt x2 -> x0, local copies, waits for them, and re-layouts: 5.13 us -> none  [local(): jnp.repeat(jnp.repeat(causal_mask, block_size, 0), block_size, 2) > 0]
    ppermute x1, starting transfers between devices: 1.91 us -> 6.92 us  [local(): lax.ppermute(history[lag_here - ahead:], 'lag', [(i, i + 1) for i in rang...]
    select_n x13 -> x7, other arithmetic: 5.49 us -> 8.89 us  [the longest x1 8.71 us: local(): jnp.where(allowed, kernel, jnp.zeros_like(kernel))]
    dot_general x3, matrix products: 4.03 us -> 0.89 us  [local(): jnp.dot(masked_rows[:, lag_pos * cols_here:(lag_pos + 1) * cols_here], so...]
    ppermute x1, waiting for transfers between devices: 3.04 us -> 0.01 us  [local(): lax.ppermute(history[lag_here - ahead:], 'lag', [(i, i + 1) for i in rang...]
  transfers between devices with their start and end apart: 31 -> 24, of which waited for: 4 -> 19; matrix products, arithmetic and copies ran while one was open for 5% -> 4% of each run, Pallas kernels for 0% -> 0%
where the time goes in v3:
time: 164 us
  starting transfers between devices  78.5 us (48%)
  waiting for transfers between devices  58 us (35%)
  other arithmetic  12.2 us (7%)
  matrix products  8.16 us (5%)
  local copies, waits for them, and re-layouts  6.27 us (4%)
    ppermute x21, starting transfers between devices, swap(): return lax.ppermute(block, axis, [(i, i ^ mask) for i in range(size)])  69.9 us
    ppermute x21, waiting for transfers between devices, swap(): return lax.ppermute(block, axis, [(i, i ^ mask) for i in range(size)])  58 us
    select_n x1, other arithmetic, local(): jnp.where(allowed, kernel, jnp.zeros_like(kernel))  8.71 us
    ppermute x1, starting transfers between devices, local(): lax.ppermute(history[lag_here - ahead:], 'lag', [(i, i + 1) for i in rang...  6.92 us
    unnamed x14, local copies, waits for them, and re-layouts  5.07 us
    dot_general x2, matrix products, local(): jnp.dot(masked_rows, shifted.reshape(lag_here * cols_here, scenarios), pr...  4.85 us
  transfers between devices with their start and end apart: 24, of which 19 were waited for; matrix products, arithmetic and copies ran while one was open for 4% of the time, Pallas kernels for 0%

profile of v3, /device:TPU:225, one launch (start us, length us, event | category | flops | bytes accessed | tf_op | source)
XLA Modules:
  0.0 163.7 jit_solution(17433000767198784402)
XLA Ops:
  0.9 8.7 %bitcast_select_fusion = bf16[512,8,512]{2,1,0:T(8,128)(2,1)S(1)} fusion(bf16[512,8,512]{2,1,0:T(8,128)(2,1)} %param.7, pred[512,8,4]{1,2,0:T(4,128)(4,1)S(1)} %bitcast.31), kind=kLoop, calls=%fused_computation | loop fusion | flops 2097152 | bytes 8404992 | tf_op jit(solution)/shard_map/jit(_where)/select_n | solution.py:74
  15.5 3.4 %collective-permute-done.1 = f32[128,256]{1,0:T(8,128)S(1)} collective-permute-done((f32[128,256]{1,0:T(8,128)S(1)}, f32[128,256]{1,0:T(8,128)S(1)}, u32[]{:S(2)}, u32[]{:S(2)}) %collective-permute-start.1) | collective-permute-done | bytes 131104 | tf_op jit(solution)/shard_map/ppermute | solution.py:20
  20.2 2.6 %collective-permute-done.2 = f32[128,256]{1,0:T(8,128)S(1)} collective-permute-done((f32[128,256]{1,0:T(8,128)S(1)}, f32[128,256]{1,0:T(8,128)S(1)}, u32[]{:S(2)}, u32[]{:S(2)}) %collective-permute-start.2) | collective-permute-done | bytes 131104 | tf_op jit(solution)/shard_map/ppermute | solution.py:20
  22.8 2.8 %collective-permute-start.3 = (f32[128,256]{1,0:T(8,128)S(1)}, f32[128,256]{1,0:T(8,128)S(1)}, u32[]{:S(2)}, u32[]{:S(2)}) collective-permute-start(f32[128,256]{1,0:T(8,128)S(1)} %add.125), channel_id=1, source_target_pairs={{0,2},{1,3},{2,0},{3,1},{4,6},{5,7},{6,4},{7,5},{8,10},{9,11},{10,... | collective-permute-start | bytes 393224 | tf_op jit(solution)/shard_map/ppermute | solution.py:20
  25.6 2.6 %collective-permute-done.3 = f32[128,256]{1,0:T(8,128)S(1)} collective-permute-done((f32[128,256]{1,0:T(8,128)S(1)}, f32[128,256]{1,0:T(8,128)S(1)}, u32[]{:S(2)}, u32[]{:S(2)}) %collective-permute-start.3) | collective-permute-done | bytes 131104 | tf_op jit(solution)/shard_map/ppermute | solution.py:20
  28.2 3.0 %collective-permute-start.4 = (f32[128,256]{1,0:T(8,128)S(1)}, f32[128,256]{1,0:T(8,128)S(1)}, u32[]{:S(2)}, u32[]{:S(2)}) collective-permute-start(f32[128,256]{1,0:T(8,128)S(1)} %add.126), channel_id=1, source_target_pairs={{0,4},{1,5},{2,6},{3,7},{4,0},{5,1},{6,2},{7,3},{8,12},{9,13},{10,... | collective-permute-start | bytes 393224 | tf_op jit(solution)/shard_map/ppermute | solution.py:20
  36.1 6.9 %collective-permute-start.7 = (bf16[2,512,256]{2,1,0:T(8,128)(2,1)S(1)}, bf16[2,512,256]{2,1,0:T(8,128)(2,1)S(1)}, u32[]{:S(2)}, u32[]{:S(2)}) collective-permute-start(bf16[2,512,256]{2,1,0:T(8,128)(2,1)S(1)} %slice.16), channel_id=1, source_target_pairs={{0,64},{64,128},{128,192},{1,65},{65,129},{129,193},{2,66},{66,130... | collective-permute-start | bytes 1572872 | tf_op jit(solution)/shard_map/ppermute | solution.py:86
  43.8 4.5 %copy.14 = bf16[64,8,8,512]{3,1,2,0:T(8,128)(2,1)S(1)} copy(bf16[64,8,8,512]{3,2,1,0:T(8,128)(2,1)} %bitcast.27) | data formatting | bytes 8388608
  50.4 2.4 %fusion.26 = f32[512,256]{1,0:T(8,128)S(1)} fusion(f32[512,256]{1,0:T(8,128)S(1)} %fusion.40, bf16[10,512,256]{2,1,0:T(8,128)(2,1)S(1)} %constant_dynamic-update-slice_fusion, bf16[512,8,512]{2,1,0:T(8,128)(2,1)S(1)} %copy-done.1), kind=kOutput, calls=%fused_computation.13 | convolution fusion | flops 1073872896 | bytes 7340032 | tf_op jit(solution)/shard_map/dot_general | solution.py:92
  52.9 19.7 %collective-permute-start.9 = (f32[256,256]{1,0:T(8,128)S(1)}, f32[256,256]{1,0:T(8,128)S(1)}, u32[]{:S(2)}, u32[]{:S(2)}) collective-permute-start(f32[256,256]{1,0:T(8,128)S(1)} %constant_dynamic-slice_fusion.3), channel_id=1, source_target_pairs={{0,64},{64,0},{128,192},{192,128},{1,65},{65,1},{129,193},{193,129... | collective-permute-start | bytes 786440 | tf_op jit(solution)/shard_map/ppermute | solution.py:20
  73.9 4.7 %collective-permute-done.10 = f32[128,256]{1,0:T(8,128)S(1)} collective-permute-done((f32[128,256]{1,0:T(8,128)S(1)}, f32[128,256]{1,0:T(8,128)S(1)}, u32[]{:S(2)}, u32[]{:S(2)}) %collective-permute-start.10) | collective-permute-done | bytes 131104 | tf_op jit(solution)/shard_map/ppermute | solution.py:20
  78.6 3.6 %collective-permute-start.11 = (f32[128,256]{1,0:T(8,128)S(1)}, f32[128,256]{1,0:T(8,128)S(1)}, u32[]{:S(2)}, u32[]{:S(2)}) collective-permute-start(f32[128,256]{1,0:T(8,128)S(1)} %dynamic-slice_add_fusion.4), channel_id=1, source_target_pairs={{0,1},{1,0},{2,3},{3,2},{4,5},{5,4},{6,7},{7,6},{8,9},{9,8},{10,11... | collective-permute-start | bytes 393224 | tf_op jit(solution)/shard_map/ppermute | solution.py:20
  84.7 5.3 %collective-permute-done.12 = f32[128,256]{1,0:T(8,128)S(1)} collective-permute-done((f32[128,256]{1,0:T(8,128)S(1)}, f32[128,256]{1,0:T(8,128)S(1)}, u32[]{:S(2)}, u32[]{:S(2)}) %collective-permute-start.12) | collective-permute-done | bytes 131104 | tf_op jit(solution)/shard_map/ppermute | solution.py:20
  90.1 5.3 %collective-permute-done.13 = f32[128,256]{1,0:T(8,128)S(1)} collective-permute-done((f32[128,256]{1,0:T(8,128)S(1)}, f32[128,256]{1,0:T(8,128)S(1)}, u32[]{:S(2)}, u32[]{:S(2)}) %collective-permute-start.13) | collective-permute-done | bytes 131104 | tf_op jit(solution)/shard_map/ppermute | solution.py:20
  96.5 2.6 %collective-permute-done.14 = bf16[128,256]{1,0:T(8,128)(2,1)S(1)} collective-permute-done((bf16[128,256]{1,0:T(8,128)(2,1)S(1)}, bf16[128,256]{1,0:T(8,128)(2,1)S(1)}, u32[]{:S(2)}, u32[]{:S(2)}) %collective-permute-start.14) | collective-permute-done | bytes 65568 | tf_op jit(solution)/shard_map/ppermute | solution.py:20
  99.1 6.2 %collective-permute-start.15 = (bf16[256,256]{1,0:T(8,128)(2,1)S(1)}, bf16[256,256]{1,0:T(8,128)(2,1)S(1)}, u32[]{:S(2)}, u32[]{:S(2)}) collective-permute-start(bf16[256,256]{1,0:T(8,128)(2,1)S(1)} %pad_maximum_fusion.4), channel_id=1, source_target_pairs={{0,64},{64,0},{128,192},{192,128},{1,65},{65,1},{129,193},{193,129... | collective-permute-start | bytes 393224 | tf_op jit(solution)/shard_map/ppermute | solution.py:20
  107.6 2.4 %fusion.31 = f32[512,256]{1,0:T(8,128)S(1)} fusion(f32[512,256]{1,0:T(8,128)S(1)} %fusion.36, f32[512,256]{1,0:T(8,128)S(1)} %fusion.38, bf16[10,512,256]{2,1,0:T(8,128)(2,1)S(1)} %constant_dynamic-update-slice_fusion, bf16[512,8,512]{2,1,0:T(8,128)(2,1)S(1)} %copy-done.1), kind=kOutput, calls=%fused_computation.14 | convolution fusion | flops 1074003968 | bytes 7864320 | tf_op jit(solution)/shard_map/dot_general | solution.py:92
  110.1 20.9 %collective-permute-start.17 = (f32[256,256]{1,0:T(8,128)S(1)}, f32[256,256]{1,0:T(8,128)S(1)}, u32[]{:S(2)}, u32[]{:S(2)}) collective-permute-start(f32[256,256]{1,0:T(8,128)S(1)} %constant_dynamic-slice_fusion.1), channel_id=1, source_target_pairs={{0,64},{64,0},{128,192},{192,128},{1,65},{65,1},{129,193},{193,129... | collective-permute-start | bytes 786440 | tf_op jit(solution)/shard_map/ppermute | solution.py:20
  132.3 4.7 %collective-permute-done.18 = f32[128,256]{1,0:T(8,128)S(1)} collective-permute-done((f32[128,256]{1,0:T(8,128)S(1)}, f32[128,256]{1,0:T(8,128)S(1)}, u32[]{:S(2)}, u32[]{:S(2)}) %collective-permute-start.18) | collective-permute-done | bytes 131104 | tf_op jit(solution)/shard_map/ppermute | solution.py:20
  137.1 3.8 %collective-permute-done.19 = f32[128,256]{1,0:T(8,128)S(1)} collective-permute-done((f32[128,256]{1,0:T(8,128)S(1)}, f32[128,256]{1,0:T(8,128)S(1)}, u32[]{:S(2)}, u32[]{:S(2)}) %collective-permute-start.19) | collective-permute-done | bytes 131104 | tf_op jit(solution)/shard_map/ppermute | solution.py:20
  141.0 5.3 %collective-permute-done.20 = f32[128,256]{1,0:T(8,128)S(1)} collective-permute-done((f32[128,256]{1,0:T(8,128)S(1)}, f32[128,256]{1,0:T(8,128)S(1)}, u32[]{:S(2)}, u32[]{:S(2)}) %collective-permute-start.20) | collective-permute-done | bytes 131104 | tf_op jit(solution)/shard_map/ppermute | solution.py:20
  146.5 5.3 %collective-permute-done.21 = f32[128,256]{1,0:T(8,128)S(1)} collective-permute-done((f32[128,256]{1,0:T(8,128)S(1)}, f32[128,256]{1,0:T(8,128)S(1)}, u32[]{:S(2)}, u32[]{:S(2)}) %collective-permute-start.21) | collective-permute-done | bytes 131104 | tf_op jit(solution)/shard_map/ppermute | solution.py:20
  152.2 3.1 %collective-permute-done.22 = bf16[128,256]{1,0:T(8,128)(2,1)S(1)} collective-permute-done((bf16[128,256]{1,0:T(8,128)(2,1)S(1)}, bf16[128,256]{1,0:T(8,128)(2,1)S(1)}, u32[]{:S(2)}, u32[]{:S(2)}) %collective-permute-start.22) | collective-permute-done | bytes 65568 | tf_op jit(solution)/shard_map/ppermute | solution.py:20
  155.4 6.2 %collective-permute-start.23 = (bf16[256,256]{1,0:T(8,128)(2,1)S(1)}, bf16[256,256]{1,0:T(8,128)(2,1)S(1)}, u32[]{:S(2)}, u32[]{:S(2)}) collective-permute-start(bf16[256,256]{1,0:T(8,128)(2,1)S(1)} %pad_maximum_fusion.5), channel_id=1, source_target_pairs={{0,64},{64,0},{128,192},{192,128},{1,65},{65,1},{129,193},{193,129... | collective-permute-start | bytes 393224 | tf_op jit(solution)/shard_map/ppermute | solution.py:20
  (85 shorter events, 27.2 us)
Async XLA Ops:
  12.1 1.9 %collective-permute-start = (f32[256,256]{1,0:T(8,128)S(1)}, f32[256,256]{1,0:T(8,128)S(1)}, u32[]{:S(2)}, u32[]{:S(2)}) collective-permute-start(f32[256,256]{1,0:T(8,128)S(1)} %constant_dynamic-slice_fusion.5), channel_id=1, source_target_pairs={{0,64},{64,0},{128,192},{192,128},{1,65},{65,1},{129,193},{193,129... | collective-permute-start | bytes 786440 | tf_op jit(solution)/shard_map/ppermute | solution.py:20
  14.1 4.8 %collective-permute-start.1 = (f32[128,256]{1,0:T(8,128)S(1)}, f32[128,256]{1,0:T(8,128)S(1)}, u32[]{:S(2)}, u32[]{:S(2)}) collective-permute-start(f32[128,256]{1,0:T(8,128)S(1)} %constant_dynamic-slice_fusion.4), channel_id=1, source_target_pairs={{0,128},{64,192},{128,0},{192,64},{1,129},{65,193},{129,1},{193,65... | collective-permute-start | bytes 393224 | tf_op jit(solution)/shard_map/ppermute | solution.py:20
  18.9 3.9 %collective-permute-start.2 = (f32[128,256]{1,0:T(8,128)S(1)}, f32[128,256]{1,0:T(8,128)S(1)}, u32[]{:S(2)}, u32[]{:S(2)}) collective-permute-start(f32[128,256]{1,0:T(8,128)S(1)} %dynamic-slice_add_fusion.5), channel_id=1, source_target_pairs={{0,1},{1,0},{2,3},{3,2},{4,5},{5,4},{6,7},{7,6},{8,9},{9,8},{10,11... | collective-permute-start | bytes 393224 | tf_op jit(solution)/shard_map/ppermute | solution.py:20
  22.8 5.4 %collective-permute-start.3 = (f32[128,256]{1,0:T(8,128)S(1)}, f32[128,256]{1,0:T(8,128)S(1)}, u32[]{:S(2)}, u32[]{:S(2)}) collective-permute-start(f32[128,256]{1,0:T(8,128)S(1)} %add.125), channel_id=1, source_target_pairs={{0,2},{1,3},{2,0},{3,1},{4,6},{5,7},{6,4},{7,5},{8,10},{9,11},{10,... | collective-permute-start | bytes 393224 | tf_op jit(solution)/shard_map/ppermute | solution.py:20
  28.2 5.4 %collective-permute-start.4 = (f32[128,256]{1,0:T(8,128)S(1)}, f32[128,256]{1,0:T(8,128)S(1)}, u32[]{:S(2)}, u32[]{:S(2)}) collective-permute-start(f32[128,256]{1,0:T(8,128)S(1)} %add.126), channel_id=1, source_target_pairs={{0,4},{1,5},{2,6},{3,7},{4,0},{5,1},{6,2},{7,3},{8,12},{9,13},{10,... | collective-permute-start | bytes 393224 | tf_op jit(solution)/shard_map/ppermute | solution.py:20
  34.6 8.4 %collective-permute-start.5 = (bf16[128,256]{1,0:T(8,128)(2,1)S(1)}, bf16[128,256]{1,0:T(8,128)(2,1)S(1)}, u32[]{:S(2)}, u32[]{:S(2)}) collective-permute-start(bf16[128,256]{1,0:T(8,128)(2,1)S(1)} %multiply_convert_fusion.2), channel_id=1, source_target_pairs={{0,128},{64,192},{128,0},{192,64},{1,129},{65,193},{129,1},{193,65... | collective-permute-start | bytes 196616 | tf_op jit(solution)/shard_map/ppermute | solution.py:20
  36.1 13.3 %collective-permute-start.7 = (bf16[2,512,256]{2,1,0:T(8,128)(2,1)S(1)}, bf16[2,512,256]{2,1,0:T(8,128)(2,1)S(1)}, u32[]{:S(2)}, u32[]{:S(2)}) collective-permute-start(bf16[2,512,256]{2,1,0:T(8,128)(2,1)S(1)} %slice.16), channel_id=1, source_target_pairs={{0,64},{64,128},{128,192},{1,65},{65,129},{129,193},{2,66},{66,130... | collective-permute-start | bytes 1572872 | tf_op jit(solution)/shard_map/ppermute | solution.py:86
  43.0 5.2 %collective-permute-start.6 = (bf16[256,256]{1,0:T(8,128)(2,1)S(1)}, bf16[256,256]{1,0:T(8,128)(2,1)S(1)}, u32[]{:S(2)}, u32[]{:S(2)}) collective-permute-start(bf16[256,256]{1,0:T(8,128)(2,1)S(1)} %pad_maximum_fusion.3), channel_id=1, source_target_pairs={{0,64},{64,0},{128,192},{192,128},{1,65},{65,1},{129,193},{193,129... | collective-permute-start | bytes 393224 | tf_op jit(solution)/shard_map/ppermute | solution.py:20
  48.4 1.2 collective-permute-start.8
  52.9 20.8 %collective-permute-start.9 = (f32[256,256]{1,0:T(8,128)S(1)}, f32[256,256]{1,0:T(8,128)S(1)}, u32[]{:S(2)}, u32[]{:S(2)}) collective-permute-start(f32[256,256]{1,0:T(8,128)S(1)} %constant_dynamic-slice_fusion.3), channel_id=1, source_target_pairs={{0,64},{64,0},{128,192},{192,128},{1,65},{65,1},{129,193},{193,129... | collective-permute-start | bytes 786440 | tf_op jit(solution)/shard_map/ppermute | solution.py:20
  73.8 4.8 %collective-permute-start.10 = (f32[128,256]{1,0:T(8,128)S(1)}, f32[128,256]{1,0:T(8,128)S(1)}, u32[]{:S(2)}, u32[]{:S(2)}) collective-permute-start(f32[128,256]{1,0:T(8,128)S(1)} %constant_dynamic-slice_fusion.2), channel_id=1, source_target_pairs={{0,128},{64,192},{128,0},{192,64},{1,129},{65,193},{129,1},{193,65... | collective-permute-start | bytes 393224 | tf_op jit(solution)/shard_map/ppermute | solution.py:20
  78.6 6.0 %collective-permute-start.11 = (f32[128,256]{1,0:T(8,128)S(1)}, f32[128,256]{1,0:T(8,128)S(1)}, u32[]{:S(2)}, u32[]{:S(2)}) collective-permute-start(f32[128,256]{1,0:T(8,128)S(1)} %dynamic-slice_add_fusion.4), channel_id=1, source_target_pairs={{0,1},{1,0},{2,3},{3,2},{4,5},{5,4},{6,7},{7,6},{8,9},{9,8},{10,11... | collective-permute-start | bytes 393224 | tf_op jit(solution)/shard_map/ppermute | solution.py:20
  84.6 5.4 %collective-permute-start.12 = (f32[128,256]{1,0:T(8,128)S(1)}, f32[128,256]{1,0:T(8,128)S(1)}, u32[]{:S(2)}, u32[]{:S(2)}) collective-permute-start(f32[128,256]{1,0:T(8,128)S(1)} %add.132), channel_id=1, source_target_pairs={{0,2},{1,3},{2,0},{3,1},{4,6},{5,7},{6,4},{7,5},{8,10},{9,11},{10,... | collective-permute-start | bytes 393224 | tf_op jit(solution)/shard_map/ppermute | solution.py:20
  90.0 5.4 %collective-permute-start.13 = (f32[128,256]{1,0:T(8,128)S(1)}, f32[128,256]{1,0:T(8,128)S(1)}, u32[]{:S(2)}, u32[]{:S(2)}) collective-permute-start(f32[128,256]{1,0:T(8,128)S(1)} %add.133), channel_id=1, source_target_pairs={{0,4},{1,5},{2,6},{3,7},{4,0},{5,1},{6,2},{7,3},{8,12},{9,13},{10,... | collective-permute-start | bytes 393224 | tf_op jit(solution)/shard_map/ppermute | solution.py:20
  95.5 3.5 %collective-permute-start.14 = (bf16[128,256]{1,0:T(8,128)(2,1)S(1)}, bf16[128,256]{1,0:T(8,128)(2,1)S(1)}, u32[]{:S(2)}, u32[]{:S(2)}) collective-permute-start(bf16[128,256]{1,0:T(8,128)(2,1)S(1)} %multiply_convert_fusion.1), channel_id=1, source_target_pairs={{0,128},{64,192},{128,0},{192,64},{1,129},{65,193},{129,1},{193,65... | collective-permute-start | bytes 196616 | tf_op jit(solution)/shard_map/ppermute | solution.py:20
  99.1 7.2 %collective-permute-start.15 = (bf16[256,256]{1,0:T(8,128)(2,1)S(1)}, bf16[256,256]{1,0:T(8,128)(2,1)S(1)}, u32[]{:S(2)}, u32[]{:S(2)}) collective-permute-start(bf16[256,256]{1,0:T(8,128)(2,1)S(1)} %pad_maximum_fusion.4), channel_id=1, source_target_pairs={{0,64},{64,0},{128,192},{192,128},{1,65},{65,1},{129,193},{193,129... | collective-permute-start | bytes 393224 | tf_op jit(solution)/shard_map/ppermute | solution.py:20
  106.3 1.0 collective-permute-start.16
  110.1 22.0 %collective-permute-start.17 = (f32[256,256]{1,0:T(8,128)S(1)}, f32[256,256]{1,0:T(8,128)S(1)}, u32[]{:S(2)}, u32[]{:S(2)}) collective-permute-start(f32[256,256]{1,0:T(8,128)S(1)} %constant_dynamic-slice_fusion.1), channel_id=1, source_target_pairs={{0,64},{64,0},{128,192},{192,128},{1,65},{65,1},{129,193},{193,129... | collective-permute-start | bytes 786440 | tf_op jit(solution)/shard_map/ppermute | solution.py:20
  132.2 4.8 %collective-permute-start.18 = (f32[128,256]{1,0:T(8,128)S(1)}, f32[128,256]{1,0:T(8,128)S(1)}, u32[]{:S(2)}, u32[]{:S(2)}) collective-permute-start(f32[128,256]{1,0:T(8,128)S(1)} %constant_dynamic-slice_fusion), channel_id=1, source_target_pairs={{0,128},{64,192},{128,0},{192,64},{1,129},{65,193},{129,1},{193,65... | collective-permute-start | bytes 393224 | tf_op jit(solution)/shard_map/ppermute | solution.py:20
  137.0 3.9 %collective-permute-start.19 = (f32[128,256]{1,0:T(8,128)S(1)}, f32[128,256]{1,0:T(8,128)S(1)}, u32[]{:S(2)}, u32[]{:S(2)}) collective-permute-start(f32[128,256]{1,0:T(8,128)S(1)} %dynamic-slice_add_fusion.3), channel_id=1, source_target_pairs={{0,1},{1,0},{2,3},{3,2},{4,5},{5,4},{6,7},{7,6},{8,9},{9,8},{10,11... | collective-permute-start | bytes 393224 | tf_op jit(solution)/shard_map/ppermute | solution.py:20
  140.9 5.4 %collective-permute-start.20 = (f32[128,256]{1,0:T(8,128)S(1)}, f32[128,256]{1,0:T(8,128)S(1)}, u32[]{:S(2)}, u32[]{:S(2)}) collective-permute-start(f32[128,256]{1,0:T(8,128)S(1)} %add.140), channel_id=1, source_target_pairs={{0,2},{1,3},{2,0},{3,1},{4,6},{5,7},{6,4},{7,5},{8,10},{9,11},{10,... | collective-permute-start | bytes 393224 | tf_op jit(solution)/shard_map/ppermute | solution.py:20
  146.4 5.4 %collective-permute-start.21 = (f32[128,256]{1,0:T(8,128)S(1)}, f32[128,256]{1,0:T(8,128)S(1)}, u32[]{:S(2)}, u32[]{:S(2)}) collective-permute-start(f32[128,256]{1,0:T(8,128)S(1)} %add.141), channel_id=1, source_target_pairs={{0,4},{1,5},{2,6},{3,7},{4,0},{5,1},{6,2},{7,3},{8,12},{9,13},{10,... | collective-permute-start | bytes 393224 | tf_op jit(solution)/shard_map/ppermute | solution.py:20
  151.9 3.5 %collective-permute-start.22 = (bf16[128,256]{1,0:T(8,128)(2,1)S(1)}, bf16[128,256]{1,0:T(8,128)(2,1)S(1)}, u32[]{:S(2)}, u32[]{:S(2)}) collective-permute-start(bf16[128,256]{1,0:T(8,128)(2,1)S(1)} %multiply_convert_fusion), channel_id=1, source_target_pairs={{0,128},{64,192},{128,0},{192,64},{1,129},{65,193},{129,1},{193,65... | collective-permute-start | bytes 196616 | tf_op jit(solution)/shard_map/ppermute | solution.py:20
  155.4 7.2 %collective-permute-start.23 = (bf16[256,256]{1,0:T(8,128)(2,1)S(1)}, bf16[256,256]{1,0:T(8,128)(2,1)S(1)}, u32[]{:S(2)}, u32[]{:S(2)}) collective-permute-start(bf16[256,256]{1,0:T(8,128)(2,1)S(1)} %pad_maximum_fusion.5), channel_id=1, source_target_pairs={{0,64},{64,0},{128,192},{192,128},{1,65},{65,1},{129,193},{193,129... | collective-permute-start | bytes 393224 | tf_op jit(solution)/shard_map/ppermute | solution.py:20
  (6 other events, 103.1 us)

commit v4 on v3

--- a/solution.py
+++ b/solution.py
@@ -4,6 +4,7 @@
 from jax.sharding import PartitionSpec as P
 
 STEPS = 3
+SERIAL = 2
 
 
 def bit_masks(axis):
@@ -20,16 +21,22 @@
     return lax.ppermute(block, axis, [(i, i ^ mask) for i in range(size)])
 
 
+def chunk_offset(lag_pos, rows):
+    offset = 0
+    for mask in bit_masks("lag"):
+        rows = rows // 2
+        offset = offset + ((lag_pos // mask) % 2) * rows
+    return offset
+
+
 def reduce_scatter_lag(x):
-    offset = 0
     for mask in bit_masks("lag"):
         half = x.shape[0] // 2
         bit = (lax.axis_index("lag") // mask) % 2
         keep = lax.dynamic_slice_in_dim(x, bit * half, half, 0)
         send = lax.dynamic_slice_in_dim(x, (1 - bit) * half, half, 0)
         x = keep + swap(send, "lag", mask)
-        offset = offset + bit * half
-    return x, offset
+    return x
 
 
 def all_reduce_src(x):
@@ -48,11 +55,11 @@
     return y
 
 
-def to_sources(rates_block):
+def transposed(chunk):
     recv_n = lax.axis_size("recv")
     src_n = lax.axis_size("src")
     route = [(s * src_n + r, r * src_n + s) for r in range(recv_n) for s in range(src_n)]
-    return lax.ppermute(rates_block, ("lag", "recv", "src"), route)
+    return lax.ppermute(chunk, ("recv", "src"), route)
 
 
 def friction(stress, offset, background, classes, rate_scale, stress_scale):
@@ -76,35 +83,50 @@
     )
     scenarios = history.shape[2]
     lag_n = lax.axis_size("lag")
+    lag_pos = lax.axis_index("lag")
+    chunk_rows = rows_here // lag_n
+    offset = chunk_offset(lag_pos, rows_here)
 
-    def rates_of(partial):
-        share, offset = reduce_scatter_lag(partial)
-        total = all_reduce_src(share)
-        return all_gather_lag(friction(total, offset, background, classes, rate_scale, stress_scale))
+    serial = []
+    for lag_index in range(SERIAL):
+        allowed_here = jnp.repeat(jnp.repeat(causal_mask[:, lag_index, :], block_size, 0), block_size, 1) > 0
+        serial.append(jnp.where(allowed_here, kernel[:, lag_index, :], jnp.zeros_like(kernel[:, lag_index, :])))
+    serial = jnp.stack(serial)
+    own = lax.dynamic_slice_in_dim(serial, offset, chunk_rows, 1)
+    for target in range(1, lag_n):
+        start = chunk_offset(target, rows_here)
+        arrived = lax.ppermute(serial[:, start:start + chunk_rows], "lag", [(0, target)])
+        own = jnp.where(lag_pos == target, arrived, own)
 
     ahead = STEPS - 1
     earlier = lax.ppermute(history[lag_here - ahead:], "lag", [(i, i + 1) for i in range(lag_n - 1)])
     extended = jnp.concatenate([earlier, history], axis=0)
-    known = [jnp.dot(masked_rows, history.reshape(lag_here * cols_here, scenarios),
-                     preferred_element_type=jnp.float32)]
+    first = jnp.dot(masked_rows, history.reshape(lag_here * cols_here, scenarios),
+                    preferred_element_type=jnp.float32)
+    later = []
     for step_index in range(1, STEPS):
         shifted = extended[ahead - step_index: ahead - step_index + lag_here]
-        known.append(jnp.dot(masked_rows, shifted.reshape(lag_here * cols_here, scenarios),
+        later.append(jnp.dot(masked_rows, shifted.reshape(lag_here * cols_here, scenarios),
                              preferred_element_type=jnp.float32))
+    later = reduce_scatter_lag(jnp.concatenate(later, axis=1))
+    known = [reduce_scatter_lag(first)] + [
+        later[:, (t - 1) * scenarios: t * scenarios] for t in range(1, STEPS)
+    ]
 
-    produced = [rates_of(known[0])]
+    outputs = []
     sources = []
-    for step_index in range(1, STEPS):
-        sources.append(to_sources(produced[-1]))
+    for step_index in range(STEPS):
         partial = known[step_index]
-        for lag_pos in range(step_index):
-            partial = partial + jnp.dot(
-                masked_rows[:, lag_pos * cols_here: (lag_pos + 1) * cols_here],
-                sources[step_index - 1 - lag_pos],
-                preferred_element_type=jnp.float32,
-            )
-        produced.append(rates_of(partial))
-    return jnp.stack(produced)
+        for lag_index in range(min(step_index, SERIAL)):
+            partial = partial + jnp.dot(own[lag_index], sources[step_index - 1 - lag_index],
+                                        preferred_element_type=jnp.float32)
+        total = all_reduce_src(partial)
+        rates_chunk = friction(total, offset, background, classes, rate_scale, stress_scale)
+        if step_index + 1 < STEPS:
+            block = all_gather_lag(transposed(rates_chunk))
+            sources.append(block)
+        outputs.append(all_gather_lag(rates_chunk))
+    return jnp.stack(outputs)
 
 
 def solution(mesh):

time: 164 us -> 151 us (0.921)
  starting transfers between devices: 78.5 us -> 47 us
  local copies, waits for them, and re-layouts: 6.27 us -> 13.4 us
  other arithmetic: 12.2 us -> 16.8 us
  matrix products: 8.16 us -> 11.9 us
  waiting for transfers between devices: 58 us -> 60.4 us
    ppermute x21 -> x23, starting transfers between devices: 69.9 us -> 36.7 us  [swap(): return lax.ppermute(block, axis, [(i, i ^ mask) for i in range(size)])]
    ppermute x2 -> x5, waiting for transfers between devices: 0.01 us -> 19.8 us  [the longest x2 19.8 us: transposed(): return lax.ppermute(chunk, ('recv', 'src'), route)]
    ppermute x21 -> x23, waiting for transfers between devices: 58 us -> 40.6 us  [swap(): return lax.ppermute(block, axis, [(i, i ^ mask) for i in range(size)])]
    ppermute x2 -> x5, starting transfers between devices: 1.67 us -> 7.14 us  [the longest x2 3.84 us: transposed(): return lax.ppermute(chunk, ('recv', 'src'), route)]
    slice x0 -> x1, local copies, waits for them, and re-layouts: none -> 4.91 us  [local(): kernel[:, lag_index, :]]
    dot_general x2, matrix products: 4.85 us -> 8.9 us  [local(): jnp.dot(masked_rows, shifted.reshape(lag_here * cols_here, scenarios), pr...]
    ppermute x1, starting transfers between devices: 6.92 us -> 3.1 us  [local(): lax.ppermute(history[lag_here - ahead:], 'lag', [(i, i + 1) for i in rang...]
    broadcast_in_dim x0 -> x4, local copies, waits for them, and re-layouts: none -> 3.25 us  [the longest x2 3.2 us: local(): jnp.repeat(jnp.repeat(causal_mask[:, lag_index, :], block_size, 0), block...]
  transfers between devices with their start and end apart: 24 -> 29, of which waited for: 19 -> 14; matrix products, arithmetic and copies ran while one was open for 4% -> 19% of each run, Pallas kernels for 0% -> 0%
where the time goes in v4:
time: 151 us; the launch traced here: 150 us
  waiting for transfers between devices  60.4 us (40%)
  starting transfers between devices  47 us (31%)
  other arithmetic  16.8 us (11%)
  local copies, waits for them, and re-layouts  13.4 us (9%)
  matrix products  11.9 us (8%)
    ppermute x23, waiting for transfers between devices, swap(): return lax.ppermute(block, axis, [(i, i ^ mask) for i in range(size)])  40.6 us
    ppermute x23, starting transfers between devices, swap(): return lax.ppermute(block, axis, [(i, i ^ mask) for i in range(size)])  36.7 us
    ppermute x2, waiting for transfers between devices, transposed(): return lax.ppermute(chunk, ('recv', 'src'), route)  19.8 us
    dot_general x2, matrix products, local(): jnp.dot(masked_rows, shifted.reshape(lag_here * cols_here, scenarios), pr...  8.9 us
    select_n x1, other arithmetic, local(): jnp.where(allowed, kernel, jnp.zeros_like(kernel))  8.71 us
    slice x1, local copies, waits for them, and re-layouts, local(): kernel[:, lag_index, :]  4.91 us
    ppermute x2, starting transfers between devices, transposed(): return lax.ppermute(chunk, ('recv', 'src'), route)  3.84 us
    ppermute x3, starting transfers between devices, local(): lax.ppermute(serial[:, start:start + chunk_rows], 'lag', [(0, target)])  3.3 us
  transfers between devices with their start and end apart: 29, of which 14 were waited for; matrix products, arithmetic and copies ran while one was open for 19% of the time, Pallas kernels for 0%

profile of v4, /device:TPU:225, one launch (start us, length us, event | category | flops | bytes accessed | tf_op | source)
XLA Modules:
  0.0 150.1 jit_solution(18326373838952067920)
XLA Ops:
  0.9 8.7 %bitcast_select_fusion = bf16[512,8,512]{2,1,0:T(8,128)(2,1)S(1)} fusion(bf16[512,8,512]{2,1,0:T(8,128)(2,1)} %param.7, pred[512,8,4]{1,2,0:T(4,128)(4,1)S(1)} %bitcast.37), kind=kLoop, calls=%fused_computation | loop fusion | flops 2097152 | bytes 8404992 | tf_op jit(solution)/shard_map/jit(_where)/select_n | solution.py:81
  9.6 2.4 %fusion.9 = f32[512,256]{1,0:T(8,128)S(1)} fusion(bf16[8,512,256]{2,1,0:T(8,128)(2,1)S(1)} %copy-done.4, bf16[512,8,512]{2,1,0:T(8,128)(2,1)S(1)} %bitcast_select_fusion), kind=kOutput, calls=%fused_computation.24 | convolution fusion | flops 1073741824 | bytes 6815744 | tf_op jit(solution)/shard_map/dot_general | solution.py:104
  12.8 2.9 %copy.26 = bf16[8,512,256]{1,2,0:T(8,128)(2,1)S(1)} copy(bf16[8,512,256]{2,1,0:T(8,128)(2,1)} %param.9) | data formatting | bytes 4194304 | tf_op args[2]
  16.6 3.1 %collective-permute-start.7 = (bf16[2,512,256]{1,2,0:T(8,128)(2,1)}, bf16[2,512,256]{1,2,0:T(8,128)(2,1)}, u32[]{:S(2)}, u32[]{:S(2)}) collective-permute-start(bf16[2,512,256]{1,2,0:T(8,128)(2,1)} %slice.57), channel_id=1, source_target_pairs={{0,64},{64,128},{128,192},{1,65},{65,129},{129,193},{2,66},{66,130... | collective-permute-start | bytes 1572872 | tf_op jit(solution)/shard_map/ppermute | solution.py:102
  19.9 4.9 %fusion.46 = (bf16[512,1,512]{2,1,0:T(2,128)(2,1)S(1)}, bf16[512,1,512]{2,1,0:T(2,128)(2,1)S(1)}) fusion(bf16[512,8,512]{2,1,0:T(8,128)(2,1)} %param.7), kind=kLoop, calls=%fused_computation.104 | loop fusion | bytes 2097152 | tf_op jit(solution)/shard_map/slice | solution.py:93
  33.8 2.8 %collective-permute-start.3 = (f32[128,256]{1,0:T(8,128)S(1)}, f32[128,256]{1,0:T(8,128)S(1)}, u32[]{:S(2)}, u32[]{:S(2)}) collective-permute-start(f32[128,256]{1,0:T(8,128)S(1)} %add.118), channel_id=1, source_target_pairs={{0,2},{1,3},{2,0},{3,1},{4,6},{5,7},{6,4},{7,5},{8,10},{9,11},{10,... | collective-permute-start | bytes 393224 | tf_op jit(solution)/shard_map/ppermute | solution.py:21
  36.6 5.3 %fusion.15 = f32[512,256]{1,0:T(8,128)S(1)} fusion(bf16[2,512,256]{1,2,0:T(8,128)(2,1)} %collective-permute-done.7, bf16[8,512,256]{1,2,0:T(8,128)(2,1)} %copy-done.2, bf16[512,8,512]{2,1,0:T(8,128)(2,1)} %copy-done), kind=kOutput, calls=%fused_computation.26 | convolution fusion | flops 1074790400 | bytes 7340032 | tf_op jit(solution)/shard_map/dot_general | solution.py:109
  42.0 2.9 %collective-permute-start.4 = (f32[128,256]{1,0:T(8,128)S(1)}, f32[128,256]{1,0:T(8,128)S(1)}, u32[]{:S(2)}, u32[]{:S(2)}) collective-permute-start(f32[128,256]{1,0:T(8,128)S(1)} %add.119), channel_id=1, source_target_pairs={{0,4},{1,5},{2,6},{3,7},{4,0},{5,1},{6,2},{7,3},{8,12},{9,13},{10,... | collective-permute-start | bytes 393224 | tf_op jit(solution)/shard_map/ppermute | solution.py:21
  44.9 3.6 %fusion.12 = f32[512,256]{1,0:T(8,128)S(1)} fusion(bf16[8,512,256]{1,2,0:T(8,128)(2,1)S(1)} %copy-done.3, bf16[2,512,256]{1,2,0:T(8,128)(2,1)} %collective-permute-done.7, bf16[512,8,512]{2,1,0:T(8,128)(2,1)S(1)} %copy-done.1), kind=kOutput, calls=%fused_computation.25 | convolution fusion | flops 1074790400 | bytes 7340032 | tf_op jit(solution)/shard_map/dot_general | solution.py:109
  51.2 1.9 %collective-permute-start.13 = (bf16[128,256]{1,0:T(8,128)(2,1)S(1)}, bf16[128,256]{1,0:T(8,128)(2,1)S(1)}, u32[]{:S(2)}, u32[]{:S(2)}) collective-permute-start(bf16[128,256]{1,0:T(8,128)(2,1)S(1)} %multiply_convert_fusion.2), channel_id=1, source_target_pairs={{0,0},{8,1},{16,2},{24,3},{32,4},{40,5},{48,6},{56,7},{1,8},{9,9},... | collective-permute-start | bytes 196616 | tf_op jit(solution)/shard_map/ppermute | solution.py:62
  53.2 9.4 %collective-permute-done.13 = bf16[128,256]{1,0:T(8,128)(2,1)S(1)} collective-permute-done((bf16[128,256]{1,0:T(8,128)(2,1)S(1)}, bf16[128,256]{1,0:T(8,128)(2,1)S(1)}, u32[]{:S(2)}, u32[]{:S(2)}) %collective-permute-start.13) | collective-permute-done | bytes 65568 | tf_op jit(solution)/shard_map/ppermute | solution.py:62
  66.9 8.9 %collective-permute-start.15 = (bf16[256,256]{1,0:T(8,128)(2,1)S(1)}, bf16[256,256]{1,0:T(8,128)(2,1)S(1)}, u32[]{:S(2)}, u32[]{:S(2)}) collective-permute-start(bf16[256,256]{1,0:T(8,128)(2,1)S(1)} %pad_maximum_fusion.9), channel_id=1, source_target_pairs={{0,64},{64,0},{128,192},{192,128},{1,65},{65,1},{129,193},{193,129... | collective-permute-start | bytes 393224 | tf_op jit(solution)/shard_map/ppermute | solution.py:21
  78.3 6.6 %collective-permute-done.9 = f32[128,512]{1,0:T(8,128)S(1)} collective-permute-done((f32[128,512]{1,0:T(8,128)S(1)}, f32[128,512]{1,0:T(8,128)S(1)}, u32[]{:S(2)}, u32[]{:S(2)}) %collective-permute-start.9) | collective-permute-done | bytes 262176 | tf_op jit(solution)/shard_map/ppermute | solution.py:21
  85.4 4.0 %collective-permute-done.16 = f32[128,256]{1,0:T(8,128)S(1)} collective-permute-done((f32[128,256]{1,0:T(8,128)S(1)}, f32[128,256]{1,0:T(8,128)S(1)}, u32[]{:S(2)}, u32[]{:S(2)}) %collective-permute-start.16) | collective-permute-done | bytes 131104 | tf_op jit(solution)/shard_map/ppermute | solution.py:21
  89.5 5.3 %collective-permute-done.17 = f32[128,256]{1,0:T(8,128)S(1)} collective-permute-done((f32[128,256]{1,0:T(8,128)S(1)}, f32[128,256]{1,0:T(8,128)S(1)}, u32[]{:S(2)}, u32[]{:S(2)}) %collective-permute-start.17) | collective-permute-done | bytes 131104 | tf_op jit(solution)/shard_map/ppermute | solution.py:21
  95.0 5.3 %collective-permute-done.18 = f32[128,256]{1,0:T(8,128)S(1)} collective-permute-done((f32[128,256]{1,0:T(8,128)S(1)}, f32[128,256]{1,0:T(8,128)S(1)}, u32[]{:S(2)}, u32[]{:S(2)}) %collective-permute-start.18) | collective-permute-done | bytes 131104 | tf_op jit(solution)/shard_map/ppermute | solution.py:21
  102.3 10.4 %collective-permute-done.21 = bf16[128,256]{1,0:T(8,128)(2,1)S(1)} collective-permute-done((bf16[128,256]{1,0:T(8,128)(2,1)S(1)}, bf16[128,256]{1,0:T(8,128)(2,1)S(1)}, u32[]{:S(2)}, u32[]{:S(2)}) %collective-permute-start.21) | collective-permute-done | bytes 65568 | tf_op jit(solution)/shard_map/ppermute | solution.py:62
  113.6 2.6 %collective-permute-done.22 = bf16[128,256]{1,0:T(8,128)(2,1)S(1)} collective-permute-done((bf16[128,256]{1,0:T(8,128)(2,1)S(1)}, bf16[128,256]{1,0:T(8,128)(2,1)S(1)}, u32[]{:S(2)}, u32[]{:S(2)}) %collective-permute-start.22) | collective-permute-done | bytes 65568 | tf_op jit(solution)/shard_map/ppermute | solution.py:21
  116.2 5.9 %collective-permute-start.23 = (bf16[256,256]{1,0:T(8,128)(2,1)S(1)}, bf16[256,256]{1,0:T(8,128)(2,1)S(1)}, u32[]{:S(2)}, u32[]{:S(2)}) collective-permute-start(bf16[256,256]{1,0:T(8,128)(2,1)S(1)} %pad_maximum_fusion.11), channel_id=1, source_target_pairs={{0,64},{64,0},{128,192},{192,128},{1,65},{65,1},{129,193},{193,129... | collective-permute-start | bytes 393224 | tf_op jit(solution)/shard_map/ppermute | solution.py:21
  124.6 3.8 %collective-permute-done.24 = f32[128,256]{1,0:T(8,128)S(1)} collective-permute-done((f32[128,256]{1,0:T(8,128)S(1)}, f32[128,256]{1,0:T(8,128)S(1)}, u32[]{:S(2)}, u32[]{:S(2)}) %collective-permute-start.24) | collective-permute-done | bytes 131104 | tf_op jit(solution)/shard_map/ppermute | solution.py:21
  130.5 3.3 %collective-permute-done.25 = f32[128,256]{1,0:T(8,128)S(1)} collective-permute-done((f32[128,256]{1,0:T(8,128)S(1)}, f32[128,256]{1,0:T(8,128)S(1)}, u32[]{:S(2)}, u32[]{:S(2)}) %collective-permute-start.25) | collective-permute-done | bytes 131104 | tf_op jit(solution)/shard_map/ppermute | solution.py:21
  133.9 5.3 %collective-permute-done.26 = f32[128,256]{1,0:T(8,128)S(1)} collective-permute-done((f32[128,256]{1,0:T(8,128)S(1)}, f32[128,256]{1,0:T(8,128)S(1)}, u32[]{:S(2)}, u32[]{:S(2)}) %collective-permute-start.26) | collective-permute-done | bytes 131104 | tf_op jit(solution)/shard_map/ppermute | solution.py:21
  139.7 4.6 %collective-permute-start.20 = (bf16[256,256]{1,0:T(8,128)(2,1)S(1)}, bf16[256,256]{1,0:T(8,128)(2,1)S(1)}, u32[]{:S(2)}, u32[]{:S(2)}) collective-permute-start(bf16[256,256]{1,0:T(8,128)(2,1)S(1)} %pad_maximum_fusion.10), channel_id=1, source_target_pairs={{0,64},{64,0},{128,192},{192,128},{1,65},{65,1},{129,193},{193,129... | collective-permute-start | bytes 393224 | tf_op jit(solution)/shard_map/ppermute | solution.py:21
  144.3 3.7 %collective-permute-start.28 = (bf16[256,256]{1,0:T(8,128)(2,1)S(1)}, bf16[256,256]{1,0:T(8,128)(2,1)S(1)}, u32[]{:S(2)}, u32[]{:S(2)}) collective-permute-start(bf16[256,256]{1,0:T(8,128)(2,1)S(1)} %pad_maximum_fusion.12), channel_id=1, source_target_pairs={{0,64},{64,0},{128,192},{192,128},{1,65},{65,1},{129,193},{193,129... | collective-permute-start | bytes 393224 | tf_op jit(solution)/shard_map/ppermute | solution.py:21
  (112 shorter events, 31.7 us)
Async XLA Ops:
  12.1 7.7 %collective-permute-start = (f32[256,256]{1,0:T(8,128)S(1)}, f32[256,256]{1,0:T(8,128)S(1)}, u32[]{:S(2)}, u32[]{:S(2)}) collective-permute-start(f32[256,256]{1,0:T(8,128)S(1)} %constant_dynamic-slice_fusion.2), channel_id=1, source_target_pairs={{0,64},{64,0},{128,192},{192,128},{1,65},{65,1},{129,193},{193,129... | collective-permute-start | bytes 786440 | tf_op jit(solution)/shard_map/ppermute | solution.py:21
  16.6 20.0 %collective-permute-start.7 = (bf16[2,512,256]{1,2,0:T(8,128)(2,1)}, bf16[2,512,256]{1,2,0:T(8,128)(2,1)}, u32[]{:S(2)}, u32[]{:S(2)}) collective-permute-start(bf16[2,512,256]{1,2,0:T(8,128)(2,1)} %slice.57), channel_id=1, source_target_pairs={{0,64},{64,128},{128,192},{1,65},{65,129},{129,193},{2,66},{66,130... | collective-permute-start | bytes 1572872 | tf_op jit(solution)/shard_map/ppermute | solution.py:102
  19.8 9.0 %collective-permute-start.1 = (f32[128,256]{1,0:T(8,128)S(1)}, f32[128,256]{1,0:T(8,128)S(1)}, u32[]{:S(2)}, u32[]{:S(2)}) collective-permute-start(f32[128,256]{1,0:T(8,128)S(1)} %constant_dynamic-slice_fusion.1), channel_id=1, source_target_pairs={{0,128},{64,192},{128,0},{192,64},{1,129},{65,193},{129,1},{193,65... | collective-permute-start | bytes 393224 | tf_op jit(solution)/shard_map/ppermute | solution.py:21
  28.8 4.9 %collective-permute-start.2 = (f32[128,256]{1,0:T(8,128)S(1)}, f32[128,256]{1,0:T(8,128)S(1)}, u32[]{:S(2)}, u32[]{:S(2)}) collective-permute-start(f32[128,256]{1,0:T(8,128)S(1)} %dynamic-slice_add_fusion.2), channel_id=1, source_target_pairs={{0,1},{1,0},{2,3},{3,2},{4,5},{5,4},{6,7},{7,6},{8,9},{9,8},{10,11... | collective-permute-start | bytes 393224 | tf_op jit(solution)/shard_map/ppermute | solution.py:21
  33.8 8.2 %collective-permute-start.3 = (f32[128,256]{1,0:T(8,128)S(1)}, f32[128,256]{1,0:T(8,128)S(1)}, u32[]{:S(2)}, u32[]{:S(2)}) collective-permute-start(f32[128,256]{1,0:T(8,128)S(1)} %add.118), channel_id=1, source_target_pairs={{0,2},{1,3},{2,0},{3,1},{4,6},{5,7},{6,4},{7,5},{8,10},{9,11},{10,... | collective-permute-start | bytes 393224 | tf_op jit(solution)/shard_map/ppermute | solution.py:21
  42.0 8.2 %collective-permute-start.4 = (f32[128,256]{1,0:T(8,128)S(1)}, f32[128,256]{1,0:T(8,128)S(1)}, u32[]{:S(2)}, u32[]{:S(2)}) collective-permute-start(f32[128,256]{1,0:T(8,128)S(1)} %add.119), channel_id=1, source_target_pairs={{0,4},{1,5},{2,6},{3,7},{4,0},{5,1},{6,2},{7,3},{8,12},{9,13},{10,... | collective-permute-start | bytes 393224 | tf_op jit(solution)/shard_map/ppermute | solution.py:21
  49.3 26.5 %collective-permute-start.8 = (f32[256,512]{1,0:T(8,128)}, f32[256,512]{1,0:T(8,128)}, u32[]{:S(2)}, u32[]{:S(2)}) collective-permute-start(f32[256,512]{1,0:T(8,128)} %fusion.20), channel_id=1, source_target_pairs={{0,64},{64,0},{128,192},{192,128},{1,65},{65,1},{129,193},{193,129... | collective-permute-start | bytes 1572872 | tf_op jit(solution)/shard_map/ppermute | solution.py:21
  51.2 11.4 %collective-permute-start.13 = (bf16[128,256]{1,0:T(8,128)(2,1)S(1)}, bf16[128,256]{1,0:T(8,128)(2,1)S(1)}, u32[]{:S(2)}, u32[]{:S(2)}) collective-permute-start(bf16[128,256]{1,0:T(8,128)(2,1)S(1)} %multiply_convert_fusion.2), channel_id=1, source_target_pairs={{0,0},{8,1},{16,2},{24,3},{32,4},{40,5},{48,6},{56,7},{1,8},{9,9},... | collective-permute-start | bytes 196616 | tf_op jit(solution)/shard_map/ppermute | solution.py:62
  63.5 13.6 %collective-permute-start.10 = (bf16[2,128,512]{2,1,0:T(8,128)(2,1)}, bf16[2,128,512]{2,1,0:T(8,128)(2,1)S(1)}, u32[]{:S(2)}, u32[]{:S(2)}) collective-permute-start(bf16[2,128,512]{2,1,0:T(8,128)(2,1)} %get-tuple-element.12), channel_id=1, source_target_pairs={{0,192},{1,193},{2,194},{3,195},{4,196},{5,197},{6,198},{7,199},{8... | collective-permute-start | bytes 786440 | tf_op jit(solution)/shard_map/ppermute | solution.py:98
  64.2 12.9 %collective-permute-start.11 = (bf16[2,128,512]{2,1,0:T(8,128)(2,1)}, bf16[2,128,512]{2,1,0:T(8,128)(2,1)}, u32[]{:S(2)}, u32[]{:S(2)}) collective-permute-start(bf16[2,128,512]{2,1,0:T(8,128)(2,1)} %get-tuple-element.13), channel_id=1, source_target_pairs={{0,128},{1,129},{2,130},{3,131},{4,132},{5,133},{6,134},{7,135},{8... | collective-permute-start | bytes 786440 | tf_op jit(solution)/shard_map/ppermute | solution.py:98
  65.5 11.6 %collective-permute-start.12 = (bf16[2,128,512]{2,1,0:T(8,128)(2,1)S(1)}, bf16[2,128,512]{2,1,0:T(8,128)(2,1)}, u32[]{:S(2)}, u32[]{:S(2)}) collective-permute-start(bf16[2,128,512]{2,1,0:T(8,128)(2,1)S(1)} %get-tuple-element.11), channel_id=1, source_target_pairs={{0,64},{1,65},{2,66},{3,67},{4,68},{5,69},{6,70},{7,71},{8,72},{9,... | collective-permute-start | bytes 786440 | tf_op jit(solution)/shard_map/ppermute | solution.py:98
  66.9 11.3 %collective-permute-start.15 = (bf16[256,256]{1,0:T(8,128)(2,1)S(1)}, bf16[256,256]{1,0:T(8,128)(2,1)S(1)}, u32[]{:S(2)}, u32[]{:S(2)}) collective-permute-start(bf16[256,256]{1,0:T(8,128)(2,1)S(1)} %pad_maximum_fusion.9), channel_id=1, source_target_pairs={{0,64},{64,0},{128,192},{192,128},{1,65},{65,1},{129,193},{193,129... | collective-permute-start | bytes 393224 | tf_op jit(solution)/shard_map/ppermute | solution.py:21
  77.0 7.9 %collective-permute-start.9 = (f32[128,512]{1,0:T(8,128)S(1)}, f32[128,512]{1,0:T(8,128)S(1)}, u32[]{:S(2)}, u32[]{:S(2)}) collective-permute-start(f32[128,512]{1,0:T(8,128)S(1)} %constant_dynamic-slice_fusion), channel_id=1, source_target_pairs={{0,128},{64,192},{128,0},{192,64},{1,129},{65,193},{129,1},{193,65... | collective-permute-start | bytes 786440 | tf_op jit(solution)/shard_map/ppermute | solution.py:21
  89.4 5.4 %collective-permute-start.17 = (f32[128,256]{1,0:T(8,128)S(1)}, f32[128,256]{1,0:T(8,128)S(1)}, u32[]{:S(2)}, u32[]{:S(2)}) collective-permute-start(f32[128,256]{1,0:T(8,128)S(1)} %add.125), channel_id=1, source_target_pairs={{0,2},{1,3},{2,0},{3,1},{4,6},{5,7},{6,4},{7,5},{8,10},{9,11},{10,... | collective-permute-start | bytes 393224 | tf_op jit(solution)/shard_map/ppermute | solution.py:21
  94.9 5.4 %collective-permute-start.18 = (f32[128,256]{1,0:T(8,128)S(1)}, f32[128,256]{1,0:T(8,128)S(1)}, u32[]{:S(2)}, u32[]{:S(2)}) collective-permute-start(f32[128,256]{1,0:T(8,128)S(1)} %add.126), channel_id=1, source_target_pairs={{0,4},{1,5},{2,6},{3,7},{4,0},{5,1},{6,2},{7,3},{8,12},{9,13},{10,... | collective-permute-start | bytes 393224 | tf_op jit(solution)/shard_map/ppermute | solution.py:21
  100.4 12.4 %collective-permute-start.21 = (bf16[128,256]{1,0:T(8,128)(2,1)S(1)}, bf16[128,256]{1,0:T(8,128)(2,1)S(1)}, u32[]{:S(2)}, u32[]{:S(2)}) collective-permute-start(bf16[128,256]{1,0:T(8,128)(2,1)S(1)} %multiply_convert_fusion.1), channel_id=1, source_target_pairs={{0,0},{8,1},{16,2},{24,3},{32,4},{40,5},{48,6},{56,7},{1,8},{9,9},... | collective-permute-start | bytes 196616 | tf_op jit(solution)/shard_map/ppermute | solution.py:62
  116.2 6.9 %collective-permute-start.23 = (bf16[256,256]{1,0:T(8,128)(2,1)S(1)}, bf16[256,256]{1,0:T(8,128)(2,1)S(1)}, u32[]{:S(2)}, u32[]{:S(2)}) collective-permute-start(bf16[256,256]{1,0:T(8,128)(2,1)S(1)} %pad_maximum_fusion.11), channel_id=1, source_target_pairs={{0,64},{64,0},{128,192},{192,128},{1,65},{65,1},{129,193},{193,129... | collective-permute-start | bytes 393224 | tf_op jit(solution)/shard_map/ppermute | solution.py:21
  123.6 4.8 %collective-permute-start.24 = (f32[128,256]{1,0:T(8,128)S(1)}, f32[128,256]{1,0:T(8,128)S(1)}, u32[]{:S(2)}, u32[]{:S(2)}) collective-permute-start(f32[128,256]{1,0:T(8,128)S(1)} %fusion.38), channel_id=1, source_target_pairs={{0,1},{1,0},{2,3},{3,2},{4,5},{5,4},{6,7},{7,6},{8,9},{9,8},{10,11... | collective-permute-start | bytes 393224 | tf_op jit(solution)/shard_map/ppermute | solution.py:21
  128.4 5.4 %collective-permute-start.25 = (f32[128,256]{1,0:T(8,128)S(1)}, f32[128,256]{1,0:T(8,128)S(1)}, u32[]{:S(2)}, u32[]{:S(2)}) collective-permute-start(f32[128,256]{1,0:T(8,128)S(1)} %add.131), channel_id=1, source_target_pairs={{0,2},{1,3},{2,0},{3,1},{4,6},{5,7},{6,4},{7,5},{8,10},{9,11},{10,... | collective-permute-start | bytes 393224 | tf_op jit(solution)/shard_map/ppermute | solution.py:21
  128.5 5.4 %collective-permute-start.19 = (bf16[128,256]{1,0:T(8,128)(2,1)S(1)}, bf16[128,256]{1,0:T(8,128)(2,1)S(1)}, u32[]{:S(2)}, u32[]{:S(2)}) collective-permute-start(bf16[128,256]{1,0:T(8,128)(2,1)S(1)} %multiply_convert_fusion.1), channel_id=1, source_target_pairs={{0,128},{64,192},{128,0},{192,64},{1,129},{65,193},{129,1},{193,65... | collective-permute-start | bytes 196616 | tf_op jit(solution)/shard_map/ppermute | solution.py:21
  128.9 19.1 %collective-permute-start.6 = (bf16[256,256]{1,0:T(8,128)(2,1)S(1)}, bf16[256,256]{1,0:T(8,128)(2,1)S(1)}, u32[]{:S(2)}, u32[]{:S(2)}) collective-permute-start(bf16[256,256]{1,0:T(8,128)(2,1)S(1)} %pad_maximum_fusion.8), channel_id=1, source_target_pairs={{0,64},{64,0},{128,192},{192,128},{1,65},{65,1},{129,193},{193,129... | collective-permute-start | bytes 393224 | tf_op jit(solution)/shard_map/ppermute | solution.py:21
  133.8 5.4 %collective-permute-start.26 = (f32[128,256]{1,0:T(8,128)S(1)}, f32[128,256]{1,0:T(8,128)S(1)}, u32[]{:S(2)}, u32[]{:S(2)}) collective-permute-start(f32[128,256]{1,0:T(8,128)S(1)} %add.132), channel_id=1, source_target_pairs={{0,4},{1,5},{2,6},{3,7},{4,0},{5,1},{6,2},{7,3},{8,12},{9,13},{10,... | collective-permute-start | bytes 393224 | tf_op jit(solution)/shard_map/ppermute | solution.py:21
  139.3 5.0 %collective-permute-start.27 = (bf16[128,256]{1,0:T(8,128)(2,1)S(1)}, bf16[128,256]{1,0:T(8,128)(2,1)S(1)}, u32[]{:S(2)}, u32[]{:S(2)}) collective-permute-start(bf16[128,256]{1,0:T(8,128)(2,1)S(1)} %multiply_convert_fusion), channel_id=1, source_target_pairs={{0,128},{64,192},{128,0},{192,64},{1,129},{65,193},{129,1},{193,65... | collective-permute-start | bytes 196616 | tf_op jit(solution)/shard_map/ppermute | solution.py:21
  139.7 8.4 %collective-permute-start.20 = (bf16[256,256]{1,0:T(8,128)(2,1)S(1)}, bf16[256,256]{1,0:T(8,128)(2,1)S(1)}, u32[]{:S(2)}, u32[]{:S(2)}) collective-permute-start(bf16[256,256]{1,0:T(8,128)(2,1)S(1)} %pad_maximum_fusion.10), channel_id=1, source_target_pairs={{0,64},{64,0},{128,192},{192,128},{1,65},{65,1},{129,193},{193,129... | collective-permute-start | bytes 393224 | tf_op jit(solution)/shard_map/ppermute | solution.py:21
  (14 other events, 103.4 us)

commit v5 on v4

--- a/solution.py
+++ b/solution.py
@@ -55,10 +55,27 @@
     return y
 
 
+def ring_distance(a, b, size):
+    d = abs(a - b) % size
+    return min(d, size - d)
+
+
+def src_distance(a, b):
+    x_size = 4
+    hops_x = ring_distance(a % x_size, b % x_size, x_size)
+    hops_y = 2 * ring_distance(a // x_size, b // x_size, 2)
+    return hops_x + hops_y
+
+
 def transposed(chunk):
     recv_n = lax.axis_size("recv")
     src_n = lax.axis_size("src")
-    route = [(s * src_n + r, r * src_n + s) for r in range(recv_n) for s in range(src_n)]
+    route = []
+    for s in range(src_n):
+        far_first = sorted(range(recv_n), key=lambda r: (-ring_distance(r, s, recv_n), r))
+        near_first = sorted(range(src_n), key=lambda q: (src_distance(q, s), q))
+        for r, sender in zip(far_first, near_first):
+            route.append((s * src_n + sender, r * src_n + s))
     return lax.ppermute(chunk, ("recv", "src"), route)
 
 

time: 151 us -> 143 us (0.947)
  starting transfers between devices: 47 us -> 41.1 us
  waiting for transfers between devices: 60.4 us -> 57.3 us
    ppermute x2, starting transfers between devices: 3.84 us -> 0.2 us  [transposed(): return lax.ppermute(chunk, ('recv', 'src'), route)]
    ppermute x23, starting transfers between devices: 36.7 us -> 34.5 us  [swap(): return lax.ppermute(block, axis, [(i, i ^ mask) for i in range(size)])]
    ppermute x2, waiting for transfers between devices: 19.8 us -> 18 us  [transposed(): return lax.ppermute(chunk, ('recv', 'src'), route)]
  transfers between devices with their start and end apart: 29 -> 29, of which waited for: 14 -> 14; matrix products, arithmetic and copies ran while one was open for 19% -> 20% of each run, Pallas kernels for 0% -> 0%
where the time goes in v5:
time: 143 us; the launch traced here: 141 us
  waiting for transfers between devices  57.3 us (40%)
  starting transfers between devices  41.1 us (29%)
  other arithmetic  16.8 us (12%)
  local copies, waits for them, and re-layouts  13.4 us (9%)
  matrix products  11.9 us (8%)
    ppermute x23, waiting for transfers between devices, swap(): return lax.ppermute(block, axis, [(i, i ^ mask) for i in range(size)])  39.2 us
    ppermute x23, starting transfers between devices, swap(): return lax.ppermute(block, axis, [(i, i ^ mask) for i in range(size)])  34.5 us
    ppermute x2, waiting for transfers between devices, transposed(): return lax.ppermute(chunk, ('recv', 'src'), route)  18 us
    dot_general x2, matrix products, local(): jnp.dot(masked_rows, shifted.reshape(lag_here * cols_here, scenarios), pr...  8.9 us
    select_n x1, other arithmetic, local(): jnp.where(allowed, kernel, jnp.zeros_like(kernel))  8.71 us
    slice x1, local copies, waits for them, and re-layouts, local(): kernel[:, lag_index, :]  4.91 us
    ppermute x3, starting transfers between devices, local(): lax.ppermute(serial[:, start:start + chunk_rows], 'lag', [(0, target)])  3.3 us
    broadcast_in_dim x2, local copies, waits for them, and re-layouts, local(): jnp.repeat(jnp.repeat(causal_mask[:, lag_index, :], block_size, 0), block...  3.2 us
  transfers between devices with their start and end apart: 29, of which 14 were waited for; matrix products, arithmetic and copies ran while one was open for 20% of the time, Pallas kernels for 0%

profile of v5, /device:TPU:225, one launch (start us, length us, event | category | flops | bytes accessed | tf_op | source)
XLA Modules:
  0.0 141.1 jit_solution(8351719670061146403)
XLA Ops:
  0.9 8.7 %bitcast_select_fusion = bf16[512,8,512]{2,1,0:T(8,128)(2,1)S(1)} fusion(bf16[512,8,512]{2,1,0:T(8,128)(2,1)} %param.7, pred[512,8,4]{1,2,0:T(4,128)(4,1)S(1)} %bitcast.37), kind=kLoop, calls=%fused_computation | loop fusion | flops 2097152 | bytes 8404992 | tf_op jit(solution)/shard_map/jit(_where)/select_n | solution.py:98
  9.6 2.4 %fusion.9 = f32[512,256]{1,0:T(8,128)S(1)} fusion(bf16[8,512,256]{2,1,0:T(8,128)(2,1)S(1)} %copy-done.4, bf16[512,8,512]{2,1,0:T(8,128)(2,1)S(1)} %bitcast_select_fusion), kind=kOutput, calls=%fused_computation.24 | convolution fusion | flops 1073741824 | bytes 6815744 | tf_op jit(solution)/shard_map/dot_general | solution.py:121
  12.8 2.9 %copy.26 = bf16[8,512,256]{1,2,0:T(8,128)(2,1)S(1)} copy(bf16[8,512,256]{2,1,0:T(8,128)(2,1)} %param.9) | data formatting | bytes 4194304 | tf_op args[2]
  16.6 3.1 %collective-permute-start.7 = (bf16[2,512,256]{1,2,0:T(8,128)(2,1)}, bf16[2,512,256]{1,2,0:T(8,128)(2,1)}, u32[]{:S(2)}, u32[]{:S(2)}) collective-permute-start(bf16[2,512,256]{1,2,0:T(8,128)(2,1)} %slice.57), channel_id=1, source_target_pairs={{0,64},{64,128},{128,192},{1,65},{65,129},{129,193},{2,66},{66,130... | collective-permute-start | bytes 1572872 | tf_op jit(solution)/shard_map/ppermute | solution.py:119
  19.9 4.9 %fusion.46 = (bf16[512,1,512]{2,1,0:T(2,128)(2,1)S(1)}, bf16[512,1,512]{2,1,0:T(2,128)(2,1)S(1)}) fusion(bf16[512,8,512]{2,1,0:T(8,128)(2,1)} %param.7), kind=kLoop, calls=%fused_computation.104 | loop fusion | bytes 2097152 | tf_op jit(solution)/shard_map/slice | solution.py:110
  27.1 1.7 %collective-permute-done.1 = f32[128,256]{1,0:T(8,128)S(1)} collective-permute-done((f32[128,256]{1,0:T(8,128)S(1)}, f32[128,256]{1,0:T(8,128)S(1)}, u32[]{:S(2)}, u32[]{:S(2)}) %collective-permute-start.1) | collective-permute-done | bytes 131104 | tf_op jit(solution)/shard_map/ppermute | solution.py:21
  33.8 2.8 %collective-permute-start.3 = (f32[128,256]{1,0:T(8,128)S(1)}, f32[128,256]{1,0:T(8,128)S(1)}, u32[]{:S(2)}, u32[]{:S(2)}) collective-permute-start(f32[128,256]{1,0:T(8,128)S(1)} %add.118), channel_id=1, source_target_pairs={{0,2},{1,3},{2,0},{3,1},{4,6},{5,7},{6,4},{7,5},{8,10},{9,11},{10,... | collective-permute-start | bytes 393224 | tf_op jit(solution)/shard_map/ppermute | solution.py:21
  36.6 5.3 %fusion.15 = f32[512,256]{1,0:T(8,128)S(1)} fusion(bf16[2,512,256]{1,2,0:T(8,128)(2,1)} %collective-permute-done.7, bf16[8,512,256]{1,2,0:T(8,128)(2,1)} %copy-done.2, bf16[512,8,512]{2,1,0:T(8,128)(2,1)} %copy-done), kind=kOutput, calls=%fused_computation.26 | convolution fusion | flops 1074790400 | bytes 7340032 | tf_op jit(solution)/shard_map/dot_general | solution.py:126
  42.0 2.9 %collective-permute-start.4 = (f32[128,256]{1,0:T(8,128)S(1)}, f32[128,256]{1,0:T(8,128)S(1)}, u32[]{:S(2)}, u32[]{:S(2)}) collective-permute-start(f32[128,256]{1,0:T(8,128)S(1)} %add.119), channel_id=1, source_target_pairs={{0,4},{1,5},{2,6},{3,7},{4,0},{5,1},{6,2},{7,3},{8,12},{9,13},{10,... | collective-permute-start | bytes 393224 | tf_op jit(solution)/shard_map/ppermute | solution.py:21
  44.9 3.6 %fusion.12 = f32[512,256]{1,0:T(8,128)S(1)} fusion(bf16[8,512,256]{1,2,0:T(8,128)(2,1)S(1)} %copy-done.3, bf16[2,512,256]{1,2,0:T(8,128)(2,1)} %collective-permute-done.7, bf16[512,8,512]{2,1,0:T(8,128)(2,1)S(1)} %copy-done.1), kind=kOutput, calls=%fused_computation.25 | convolution fusion | flops 1074790400 | bytes 7340032 | tf_op jit(solution)/shard_map/dot_general | solution.py:126
  51.4 9.2 %collective-permute-done.13 = bf16[128,256]{1,0:T(8,128)(2,1)S(1)} collective-permute-done((bf16[128,256]{1,0:T(8,128)(2,1)S(1)}, bf16[128,256]{1,0:T(8,128)(2,1)S(1)}, u32[]{:S(2)}, u32[]{:S(2)}) %collective-permute-start.13) | collective-permute-done | bytes 65568 | tf_op jit(solution)/shard_map/ppermute | solution.py:79
  65.0 5.1 %collective-permute-start.15 = (bf16[256,256]{1,0:T(8,128)(2,1)S(1)}, bf16[256,256]{1,0:T(8,128)(2,1)S(1)}, u32[]{:S(2)}, u32[]{:S(2)}) collective-permute-start(bf16[256,256]{1,0:T(8,128)(2,1)S(1)} %pad_maximum_fusion.9), channel_id=1, source_target_pairs={{0,64},{64,0},{128,192},{192,128},{1,65},{65,1},{129,193},{193,129... | collective-permute-start | bytes 393224 | tf_op jit(solution)/shard_map/ppermute | solution.py:21
  72.5 6.6 %collective-permute-done.9 = f32[128,512]{1,0:T(8,128)S(1)} collective-permute-done((f32[128,512]{1,0:T(8,128)S(1)}, f32[128,512]{1,0:T(8,128)S(1)}, u32[]{:S(2)}, u32[]{:S(2)}) %collective-permute-start.9) | collective-permute-done | bytes 262176 | tf_op jit(solution)/shard_map/ppermute | solution.py:21
  79.5 4.2 %collective-permute-done.16 = f32[128,256]{1,0:T(8,128)S(1)} collective-permute-done((f32[128,256]{1,0:T(8,128)S(1)}, f32[128,256]{1,0:T(8,128)S(1)}, u32[]{:S(2)}, u32[]{:S(2)}) %collective-permute-start.16) | collective-permute-done | bytes 131104 | tf_op jit(solution)/shard_map/ppermute | solution.py:21
  84.7 4.4 %collective-permute-done.17 = f32[128,256]{1,0:T(8,128)S(1)} collective-permute-done((f32[128,256]{1,0:T(8,128)S(1)}, f32[128,256]{1,0:T(8,128)S(1)}, u32[]{:S(2)}, u32[]{:S(2)}) %collective-permute-start.17) | collective-permute-done | bytes 131104 | tf_op jit(solution)/shard_map/ppermute | solution.py:21
  90.4 4.1 %collective-permute-done.18 = f32[128,256]{1,0:T(8,128)S(1)} collective-permute-done((f32[128,256]{1,0:T(8,128)S(1)}, f32[128,256]{1,0:T(8,128)S(1)}, u32[]{:S(2)}, u32[]{:S(2)}) %collective-permute-start.18) | collective-permute-done | bytes 131104 | tf_op jit(solution)/shard_map/ppermute | solution.py:21
  94.7 8.8 %collective-permute-done.21 = bf16[128,256]{1,0:T(8,128)(2,1)S(1)} collective-permute-done((bf16[128,256]{1,0:T(8,128)(2,1)S(1)}, bf16[128,256]{1,0:T(8,128)(2,1)S(1)}, u32[]{:S(2)}, u32[]{:S(2)}) %collective-permute-start.21) | collective-permute-done | bytes 65568 | tf_op jit(solution)/shard_map/ppermute | solution.py:79
  104.1 2.8 %collective-permute-done.22 = bf16[128,256]{1,0:T(8,128)(2,1)S(1)} collective-permute-done((bf16[128,256]{1,0:T(8,128)(2,1)S(1)}, bf16[128,256]{1,0:T(8,128)(2,1)S(1)}, u32[]{:S(2)}, u32[]{:S(2)}) %collective-permute-start.22) | collective-permute-done | bytes 65568 | tf_op jit(solution)/shard_map/ppermute | solution.py:21
  107.0 6.1 %collective-permute-start.23 = (bf16[256,256]{1,0:T(8,128)(2,1)S(1)}, bf16[256,256]{1,0:T(8,128)(2,1)S(1)}, u32[]{:S(2)}, u32[]{:S(2)}) collective-permute-start(bf16[256,256]{1,0:T(8,128)(2,1)S(1)} %pad_maximum_fusion.11), channel_id=1, source_target_pairs={{0,64},{64,0},{128,192},{192,128},{1,65},{65,1},{129,193},{193,129... | collective-permute-start | bytes 393224 | tf_op jit(solution)/shard_map/ppermute | solution.py:21
  115.0 4.3 %collective-permute-done.24 = f32[128,256]{1,0:T(8,128)S(1)} collective-permute-done((f32[128,256]{1,0:T(8,128)S(1)}, f32[128,256]{1,0:T(8,128)S(1)}, u32[]{:S(2)}, u32[]{:S(2)}) %collective-permute-start.24) | collective-permute-done | bytes 131104 | tf_op jit(solution)/shard_map/ppermute | solution.py:21
  121.6 3.1 %collective-permute-done.25 = f32[128,256]{1,0:T(8,128)S(1)} collective-permute-done((f32[128,256]{1,0:T(8,128)S(1)}, f32[128,256]{1,0:T(8,128)S(1)}, u32[]{:S(2)}, u32[]{:S(2)}) %collective-permute-start.25) | collective-permute-done | bytes 131104 | tf_op jit(solution)/shard_map/ppermute | solution.py:21
  124.9 5.3 %collective-permute-done.26 = f32[128,256]{1,0:T(8,128)S(1)} collective-permute-done((f32[128,256]{1,0:T(8,128)S(1)}, f32[128,256]{1,0:T(8,128)S(1)}, u32[]{:S(2)}, u32[]{:S(2)}) %collective-permute-start.26) | collective-permute-done | bytes 131104 | tf_op jit(solution)/shard_map/ppermute | solution.py:21
  130.7 4.6 %collective-permute-start.20 = (bf16[256,256]{1,0:T(8,128)(2,1)S(1)}, bf16[256,256]{1,0:T(8,128)(2,1)S(1)}, u32[]{:S(2)}, u32[]{:S(2)}) collective-permute-start(bf16[256,256]{1,0:T(8,128)(2,1)S(1)} %pad_maximum_fusion.10), channel_id=1, source_target_pairs={{0,64},{64,0},{128,192},{192,128},{1,65},{65,1},{129,193},{193,129... | collective-permute-start | bytes 393224 | tf_op jit(solution)/shard_map/ppermute | solution.py:21
  135.3 3.7 %collective-permute-start.28 = (bf16[256,256]{1,0:T(8,128)(2,1)S(1)}, bf16[256,256]{1,0:T(8,128)(2,1)S(1)}, u32[]{:S(2)}, u32[]{:S(2)}) collective-permute-start(bf16[256,256]{1,0:T(8,128)(2,1)S(1)} %pad_maximum_fusion.12), channel_id=1, source_target_pairs={{0,64},{64,0},{128,192},{192,128},{1,65},{65,1},{129,193},{193,129... | collective-permute-start | bytes 393224 | tf_op jit(solution)/shard_map/ppermute | solution.py:21
  (112 shorter events, 29.7 us)
Async XLA Ops:
  12.1 7.7 %collective-permute-start = (f32[256,256]{1,0:T(8,128)S(1)}, f32[256,256]{1,0:T(8,128)S(1)}, u32[]{:S(2)}, u32[]{:S(2)}) collective-permute-start(f32[256,256]{1,0:T(8,128)S(1)} %constant_dynamic-slice_fusion.2), channel_id=1, source_target_pairs={{0,64},{64,0},{128,192},{192,128},{1,65},{65,1},{129,193},{193,129... | collective-permute-start | bytes 786440 | tf_op jit(solution)/shard_map/ppermute | solution.py:21
  16.6 20.0 %collective-permute-start.7 = (bf16[2,512,256]{1,2,0:T(8,128)(2,1)}, bf16[2,512,256]{1,2,0:T(8,128)(2,1)}, u32[]{:S(2)}, u32[]{:S(2)}) collective-permute-start(bf16[2,512,256]{1,2,0:T(8,128)(2,1)} %slice.57), channel_id=1, source_target_pairs={{0,64},{64,128},{128,192},{1,65},{65,129},{129,193},{2,66},{66,130... | collective-permute-start | bytes 1572872 | tf_op jit(solution)/shard_map/ppermute | solution.py:119
  19.8 9.0 %collective-permute-start.1 = (f32[128,256]{1,0:T(8,128)S(1)}, f32[128,256]{1,0:T(8,128)S(1)}, u32[]{:S(2)}, u32[]{:S(2)}) collective-permute-start(f32[128,256]{1,0:T(8,128)S(1)} %constant_dynamic-slice_fusion.1), channel_id=1, source_target_pairs={{0,128},{64,192},{128,0},{192,64},{1,129},{65,193},{129,1},{193,65... | collective-permute-start | bytes 393224 | tf_op jit(solution)/shard_map/ppermute | solution.py:21
  28.8 4.9 %collective-permute-start.2 = (f32[128,256]{1,0:T(8,128)S(1)}, f32[128,256]{1,0:T(8,128)S(1)}, u32[]{:S(2)}, u32[]{:S(2)}) collective-permute-start(f32[128,256]{1,0:T(8,128)S(1)} %dynamic-slice_add_fusion.2), channel_id=1, source_target_pairs={{0,1},{1,0},{2,3},{3,2},{4,5},{5,4},{6,7},{7,6},{8,9},{9,8},{10,11... | collective-permute-start | bytes 393224 | tf_op jit(solution)/shard_map/ppermute | solution.py:21
  33.8 8.2 %collective-permute-start.3 = (f32[128,256]{1,0:T(8,128)S(1)}, f32[128,256]{1,0:T(8,128)S(1)}, u32[]{:S(2)}, u32[]{:S(2)}) collective-permute-start(f32[128,256]{1,0:T(8,128)S(1)} %add.118), channel_id=1, source_target_pairs={{0,2},{1,3},{2,0},{3,1},{4,6},{5,7},{6,4},{7,5},{8,10},{9,11},{10,... | collective-permute-start | bytes 393224 | tf_op jit(solution)/shard_map/ppermute | solution.py:21
  42.0 8.2 %collective-permute-start.4 = (f32[128,256]{1,0:T(8,128)S(1)}, f32[128,256]{1,0:T(8,128)S(1)}, u32[]{:S(2)}, u32[]{:S(2)}) collective-permute-start(f32[128,256]{1,0:T(8,128)S(1)} %add.119), channel_id=1, source_target_pairs={{0,4},{1,5},{2,6},{3,7},{4,0},{5,1},{6,2},{7,3},{8,12},{9,13},{10,... | collective-permute-start | bytes 393224 | tf_op jit(solution)/shard_map/ppermute | solution.py:21
  49.3 20.7 %collective-permute-start.8 = (f32[256,512]{1,0:T(8,128)}, f32[256,512]{1,0:T(8,128)}, u32[]{:S(2)}, u32[]{:S(2)}) collective-permute-start(f32[256,512]{1,0:T(8,128)} %fusion.20), channel_id=1, source_target_pairs={{0,64},{64,0},{128,192},{192,128},{1,65},{65,1},{129,193},{193,129... | collective-permute-start | bytes 1572872 | tf_op jit(solution)/shard_map/ppermute | solution.py:21
  51.2 9.4 %collective-permute-start.13 = (bf16[128,256]{1,0:T(8,128)(2,1)S(1)}, bf16[128,256]{1,0:T(8,128)(2,1)S(1)}, u32[]{:S(2)}, u32[]{:S(2)}) collective-permute-start(bf16[128,256]{1,0:T(8,128)(2,1)S(1)} %multiply_convert_fusion.2), channel_id=1, source_target_pairs={{0,32},{1,24},{3,40},{2,16},{4,48},{5,8},{7,56},{6,0},{9,41},{8,33... | collective-permute-start | bytes 196616 | tf_op jit(solution)/shard_map/ppermute | solution.py:79
  61.6 9.7 %collective-permute-start.10 = (bf16[2,128,512]{2,1,0:T(8,128)(2,1)}, bf16[2,128,512]{2,1,0:T(8,128)(2,1)S(1)}, u32[]{:S(2)}, u32[]{:S(2)}) collective-permute-start(bf16[2,128,512]{2,1,0:T(8,128)(2,1)} %get-tuple-element.12), channel_id=1, source_target_pairs={{0,192},{1,193},{2,194},{3,195},{4,196},{5,197},{6,198},{7,199},{8... | collective-permute-start | bytes 786440 | tf_op jit(solution)/shard_map/ppermute | solution.py:115
  62.3 9.1 %collective-permute-start.11 = (bf16[2,128,512]{2,1,0:T(8,128)(2,1)}, bf16[2,128,512]{2,1,0:T(8,128)(2,1)}, u32[]{:S(2)}, u32[]{:S(2)}) collective-permute-start(bf16[2,128,512]{2,1,0:T(8,128)(2,1)} %get-tuple-element.13), channel_id=1, source_target_pairs={{0,128},{1,129},{2,130},{3,131},{4,132},{5,133},{6,134},{7,135},{8... | collective-permute-start | bytes 786440 | tf_op jit(solution)/shard_map/ppermute | solution.py:115
  63.6 7.7 %collective-permute-start.12 = (bf16[2,128,512]{2,1,0:T(8,128)(2,1)S(1)}, bf16[2,128,512]{2,1,0:T(8,128)(2,1)}, u32[]{:S(2)}, u32[]{:S(2)}) collective-permute-start(bf16[2,128,512]{2,1,0:T(8,128)(2,1)S(1)} %get-tuple-element.11), channel_id=1, source_target_pairs={{0,64},{1,65},{2,66},{3,67},{4,68},{5,69},{6,70},{7,71},{8,72},{9,... | collective-permute-start | bytes 786440 | tf_op jit(solution)/shard_map/ppermute | solution.py:115
  65.0 7.5 %collective-permute-start.15 = (bf16[256,256]{1,0:T(8,128)(2,1)S(1)}, bf16[256,256]{1,0:T(8,128)(2,1)S(1)}, u32[]{:S(2)}, u32[]{:S(2)}) collective-permute-start(bf16[256,256]{1,0:T(8,128)(2,1)S(1)} %pad_maximum_fusion.9), channel_id=1, source_target_pairs={{0,64},{64,0},{128,192},{192,128},{1,65},{65,1},{129,193},{193,129... | collective-permute-start | bytes 393224 | tf_op jit(solution)/shard_map/ppermute | solution.py:21
  71.2 7.9 %collective-permute-start.9 = (f32[128,512]{1,0:T(8,128)S(1)}, f32[128,512]{1,0:T(8,128)S(1)}, u32[]{:S(2)}, u32[]{:S(2)}) collective-permute-start(f32[128,512]{1,0:T(8,128)S(1)} %constant_dynamic-slice_fusion), channel_id=1, source_target_pairs={{0,128},{64,192},{128,0},{192,64},{1,129},{65,193},{129,1},{193,65... | collective-permute-start | bytes 786440 | tf_op jit(solution)/shard_map/ppermute | solution.py:21
  83.6 5.4 %collective-permute-start.17 = (f32[128,256]{1,0:T(8,128)S(1)}, f32[128,256]{1,0:T(8,128)S(1)}, u32[]{:S(2)}, u32[]{:S(2)}) collective-permute-start(f32[128,256]{1,0:T(8,128)S(1)} %add.125), channel_id=1, source_target_pairs={{0,2},{1,3},{2,0},{3,1},{4,6},{5,7},{6,4},{7,5},{8,10},{9,11},{10,... | collective-permute-start | bytes 393224 | tf_op jit(solution)/shard_map/ppermute | solution.py:21
  89.1 5.4 %collective-permute-start.18 = (f32[128,256]{1,0:T(8,128)S(1)}, f32[128,256]{1,0:T(8,128)S(1)}, u32[]{:S(2)}, u32[]{:S(2)}) collective-permute-start(f32[128,256]{1,0:T(8,128)S(1)} %add.126), channel_id=1, source_target_pairs={{0,4},{1,5},{2,6},{3,7},{4,0},{5,1},{6,2},{7,3},{8,12},{9,13},{10,... | collective-permute-start | bytes 393224 | tf_op jit(solution)/shard_map/ppermute | solution.py:21
  94.6 8.9 %collective-permute-start.21 = (bf16[128,256]{1,0:T(8,128)(2,1)S(1)}, bf16[128,256]{1,0:T(8,128)(2,1)S(1)}, u32[]{:S(2)}, u32[]{:S(2)}) collective-permute-start(bf16[128,256]{1,0:T(8,128)(2,1)S(1)} %multiply_convert_fusion.1), channel_id=1, source_target_pairs={{0,32},{1,24},{3,40},{2,16},{4,48},{5,8},{7,56},{6,0},{9,41},{8,33... | collective-permute-start | bytes 196616 | tf_op jit(solution)/shard_map/ppermute | solution.py:79
  107.0 7.1 %collective-permute-start.23 = (bf16[256,256]{1,0:T(8,128)(2,1)S(1)}, bf16[256,256]{1,0:T(8,128)(2,1)S(1)}, u32[]{:S(2)}, u32[]{:S(2)}) collective-permute-start(bf16[256,256]{1,0:T(8,128)(2,1)S(1)} %pad_maximum_fusion.11), channel_id=1, source_target_pairs={{0,64},{64,0},{128,192},{192,128},{1,65},{65,1},{129,193},{193,129... | collective-permute-start | bytes 393224 | tf_op jit(solution)/shard_map/ppermute | solution.py:21
  114.6 4.8 %collective-permute-start.5 = (bf16[128,256]{1,0:T(8,128)(2,1)S(1)}, bf16[128,256]{1,0:T(8,128)(2,1)S(1)}, u32[]{:S(2)}, u32[]{:S(2)}) collective-permute-start(bf16[128,256]{1,0:T(8,128)(2,1)S(1)} %multiply_convert_fusion.2), channel_id=1, source_target_pairs={{0,128},{64,192},{128,0},{192,64},{1,129},{65,193},{129,1},{193,65... | collective-permute-start | bytes 196616 | tf_op jit(solution)/shard_map/ppermute | solution.py:21
  119.3 5.4 %collective-permute-start.25 = (f32[128,256]{1,0:T(8,128)S(1)}, f32[128,256]{1,0:T(8,128)S(1)}, u32[]{:S(2)}, u32[]{:S(2)}) collective-permute-start(f32[128,256]{1,0:T(8,128)S(1)} %add.131), channel_id=1, source_target_pairs={{0,2},{1,3},{2,0},{3,1},{4,6},{5,7},{6,4},{7,5},{8,10},{9,11},{10,... | collective-permute-start | bytes 393224 | tf_op jit(solution)/shard_map/ppermute | solution.py:21
  119.5 5.4 %collective-permute-start.19 = (bf16[128,256]{1,0:T(8,128)(2,1)S(1)}, bf16[128,256]{1,0:T(8,128)(2,1)S(1)}, u32[]{:S(2)}, u32[]{:S(2)}) collective-permute-start(bf16[128,256]{1,0:T(8,128)(2,1)S(1)} %multiply_convert_fusion.1), channel_id=1, source_target_pairs={{0,128},{64,192},{128,0},{192,64},{1,129},{65,193},{129,1},{193,65... | collective-permute-start | bytes 196616 | tf_op jit(solution)/shard_map/ppermute | solution.py:21
  120.1 18.9 %collective-permute-start.6 = (bf16[256,256]{1,0:T(8,128)(2,1)S(1)}, bf16[256,256]{1,0:T(8,128)(2,1)S(1)}, u32[]{:S(2)}, u32[]{:S(2)}) collective-permute-start(bf16[256,256]{1,0:T(8,128)(2,1)S(1)} %pad_maximum_fusion.8), channel_id=1, source_target_pairs={{0,64},{64,0},{128,192},{192,128},{1,65},{65,1},{129,193},{193,129... | collective-permute-start | bytes 393224 | tf_op jit(solution)/shard_map/ppermute | solution.py:21
  124.8 5.4 %collective-permute-start.26 = (f32[128,256]{1,0:T(8,128)S(1)}, f32[128,256]{1,0:T(8,128)S(1)}, u32[]{:S(2)}, u32[]{:S(2)}) collective-permute-start(f32[128,256]{1,0:T(8,128)S(1)} %add.132), channel_id=1, source_target_pairs={{0,4},{1,5},{2,6},{3,7},{4,0},{5,1},{6,2},{7,3},{8,12},{9,13},{10,... | collective-permute-start | bytes 393224 | tf_op jit(solution)/shard_map/ppermute | solution.py:21
  130.3 5.0 %collective-permute-start.27 = (bf16[128,256]{1,0:T(8,128)(2,1)S(1)}, bf16[128,256]{1,0:T(8,128)(2,1)S(1)}, u32[]{:S(2)}, u32[]{:S(2)}) collective-permute-start(bf16[128,256]{1,0:T(8,128)(2,1)S(1)} %multiply_convert_fusion), channel_id=1, source_target_pairs={{0,128},{64,192},{128,0},{192,64},{1,129},{65,193},{129,1},{193,65... | collective-permute-start | bytes 196616 | tf_op jit(solution)/shard_map/ppermute | solution.py:21
  130.7 8.4 %collective-permute-start.20 = (bf16[256,256]{1,0:T(8,128)(2,1)S(1)}, bf16[256,256]{1,0:T(8,128)(2,1)S(1)}, u32[]{:S(2)}, u32[]{:S(2)}) collective-permute-start(bf16[256,256]{1,0:T(8,128)(2,1)S(1)} %pad_maximum_fusion.10), channel_id=1, source_target_pairs={{0,64},{64,0},{128,192},{192,128},{1,65},{65,1},{129,193},{193,129... | collective-permute-start | bytes 393224 | tf_op jit(solution)/shard_map/ppermute | solution.py:21
  (14 other events, 103.5 us)

commit v6 on v5

--- a/solution.py
+++ b/solution.py
@@ -108,12 +108,8 @@
     for lag_index in range(SERIAL):
         allowed_here = jnp.repeat(jnp.repeat(causal_mask[:, lag_index, :], block_size, 0), block_size, 1) > 0
         serial.append(jnp.where(allowed_here, kernel[:, lag_index, :], jnp.zeros_like(kernel[:, lag_index, :])))
-    serial = jnp.stack(serial)
-    own = lax.dynamic_slice_in_dim(serial, offset, chunk_rows, 1)
-    for target in range(1, lag_n):
-        start = chunk_offset(target, rows_here)
-        arrived = lax.ppermute(serial[:, start:start + chunk_rows], "lag", [(0, target)])
-        own = jnp.where(lag_pos == target, arrived, own)
+    serial = jnp.stack(serial).transpose(1, 0, 2).reshape(rows_here, SERIAL * cols_here)
+    serial = jnp.where(lag_pos == 0, serial, jnp.zeros_like(serial)).astype(jnp.float32)
 
     ahead = STEPS - 1
     earlier = lax.ppermute(history[lag_here - ahead:], "lag", [(i, i + 1) for i in range(lag_n - 1)])
@@ -125,7 +121,9 @@
         shifted = extended[ahead - step_index: ahead - step_index + lag_here]
         later.append(jnp.dot(masked_rows, shifted.reshape(lag_here * cols_here, scenarios),
                              preferred_element_type=jnp.float32))
-    later = reduce_scatter_lag(jnp.concatenate(later, axis=1))
+    later = reduce_scatter_lag(jnp.concatenate(later + [serial], axis=1))
+    own = later[:, (STEPS - 1) * scenarios:].astype(kernel.dtype)
+    own = own.reshape(chunk_rows, SERIAL, cols_here).transpose(1, 0, 2)
     known = [reduce_scatter_lag(first)] + [
         later[:, (t - 1) * scenarios: t * scenarios] for t in range(1, STEPS)
     ]

time: 143 us -> 160 us (1.12)
  local copies, waits for them, and re-layouts: 13.4 us -> 21.1 us
  starting transfers between devices: 41.1 us -> 47.4 us
  waiting for transfers between devices: 57.3 us -> 63 us
  matrix products: 11.9 us -> 10 us
    ppermute x23, waiting for transfers between devices: 39.2 us -> 51.8 us  [swap(): return lax.ppermute(block, axis, [(i, i ^ mask) for i in range(size)])]
    ppermute x2, waiting for transfers between devices: 18 us -> 11.2 us  [transposed(): return lax.ppermute(chunk, ('recv', 'src'), route)]
    unnamed x19 -> x23, local copies, waits for them, and re-layouts: 2.91 us -> 8.57 us
    ppermute x2, starting transfers between devices: 0.2 us -> 4.69 us  [transposed(): return lax.ppermute(chunk, ('recv', 'src'), route)]
    ppermute x23, starting transfers between devices: 34.5 us -> 39 us  [swap(): return lax.ppermute(block, axis, [(i, i ^ mask) for i in range(size)])]
    ppermute x3 -> x0, starting transfers between devices: 3.3 us -> none  [local(): lax.ppermute(serial[:, start:start + chunk_rows], 'lag', [(0, target)])]
    add x4, other arithmetic: 1.19 us -> 3.96 us  [reduce_scatter_lag(): x = keep + swap(send, 'lag', mask)]
    dynamic_slice x3 -> x4, local copies, waits for them, and re-layouts: 0.07 us -> 2.83 us  [reduce_scatter_lag(): send = lax.dynamic_slice_in_dim(x, (1 - bit) * half, half, 0)]
  transfers between devices with their start and end apart: 29 -> 26, of which waited for: 14 -> 17; matrix products, arithmetic and copies ran while one was open for 20% -> 23% of each run, Pallas kernels for 0% -> 0%
where the time goes in v6:
time: 160 us; the launch traced here: 159 us
  waiting for transfers between devices  63 us (39%)
  starting transfers between devices  47.4 us (30%)
  local copies, waits for them, and re-layouts  21.1 us (13%)
  other arithmetic  16.4 us (10%)
  matrix products  10 us (6%)
    ppermute x23, waiting for transfers between devices, swap(): return lax.ppermute(block, axis, [(i, i ^ mask) for i in range(size)])  51.8 us
    ppermute x23, starting transfers between devices, swap(): return lax.ppermute(block, axis, [(i, i ^ mask) for i in range(size)])  39 us
    ppermute x2, waiting for transfers between devices, transposed(): return lax.ppermute(chunk, ('recv', 'src'), route)  11.2 us
    select_n x1, other arithmetic, local(): jnp.where(allowed, kernel, jnp.zeros_like(kernel))  8.71 us
    unnamed x23, local copies, waits for them, and re-layouts  8.57 us
    dot_general x2, matrix products, local(): jnp.dot(masked_rows, shifted.reshape(lag_here * cols_here, scenarios), pr...  7.02 us
    slice x1, local copies, waits for them, and re-layouts, local(): kernel[:, lag_index, :]  4.9 us
    ppermute x2, starting transfers between devices, transposed(): return lax.ppermute(chunk, ('recv', 'src'), route)  4.69 us
  transfers between devices with their start and end apart: 26, of which 17 were waited for; matrix products, arithmetic and copies ran while one was open for 23% of the time, Pallas kernels for 0%

profile of v6, /device:TPU:225, one launch (start us, length us, event | category | flops | bytes accessed | tf_op | source)
XLA Modules:
  0.0 158.5 jit_solution(68085759145715589)
XLA Ops:
  0.0 2.9 %copy.29 = bf16[8,512,256]{1,2,0:T(8,128)(2,1)S(1)} copy(bf16[8,512,256]{2,1,0:T(8,128)(2,1)} %param.9) | data formatting | bytes 4194304 | tf_op args[2]
  2.9 3.8 %collective-permute-start.7 = (bf16[2,512,256]{1,2,0:T(8,128)(2,1)S(1)}, bf16[2,512,256]{1,2,0:T(8,128)(2,1)}, u32[]{:S(2)}, u32[]{:S(2)}) collective-permute-start(bf16[2,512,256]{1,2,0:T(8,128)(2,1)S(1)} %slice.50), channel_id=1, source_target_pairs={{0,64},{64,128},{128,192},{1,65},{65,129},{129,193},{2,66},{66,130... | collective-permute-start | bytes 1572872 | tf_op jit(solution)/shard_map/ppermute | solution.py:115
  6.9 8.7 %bitcast_select_fusion = bf16[512,8,512]{2,1,0:T(8,128)(2,1)S(1)} fusion(bf16[512,8,512]{2,1,0:T(8,128)(2,1)} %param.7, pred[512,8,4]{1,2,0:T(4,128)(4,1)S(1)} %bitcast.49), kind=kLoop, calls=%fused_computation | loop fusion | flops 2097152 | bytes 8404992 | tf_op jit(solution)/shard_map/jit(_where)/select_n | solution.py:98
  20.9 4.9 %fusion.36 = (bf16[512,1,512]{2,1,0:T(2,128)(2,1)S(1)}, bf16[512,1,512]{2,1,0:T(2,128)(2,1)S(1)}) fusion(bf16[512,8,512]{2,1,0:T(8,128)(2,1)} %param.7), kind=kLoop, calls=%fused_computation.89 | loop fusion | bytes 2097152 | tf_op jit(solution)/shard_map/slice | solution.py:110
  32.9 3.4 %fusion.15 = f32[512,256]{1,0:T(8,128)S(1)} fusion(bf16[2,512,256]{1,2,0:T(8,128)(2,1)} %collective-permute-done.7, bf16[8,512,256]{1,2,0:T(8,128)(2,1)S(1)} %copy-done.4, bf16[512,8,512]{2,1,0:T(8,128)(2,1)S(1)} %copy-done.2), kind=kOutput, calls=%fused_computation.17 | convolution fusion | flops 1074790400 | bytes 7340032 | tf_op jit(solution)/shard_map/dot_general | solution.py:122
  36.3 3.6 %fusion.12 = f32[512,256]{1,0:T(8,128)S(1)} fusion(bf16[8,512,256]{1,2,0:T(8,128)(2,1)S(1)} %copy-done.4, bf16[2,512,256]{1,2,0:T(8,128)(2,1)} %collective-permute-done.7, bf16[512,8,512]{2,1,0:T(8,128)(2,1)S(1)} %copy-done.2), kind=kOutput, calls=%fused_computation.16 | convolution fusion | flops 1074790400 | bytes 7340032 | tf_op jit(solution)/shard_map/dot_general | solution.py:122
  43.8 5.3 %collective-permute-done.1 = f32[128,256]{1,0:T(8,128)S(1)} collective-permute-done((f32[128,256]{1,0:T(8,128)}, f32[128,256]{1,0:T(8,128)S(1)}, u32[]{:S(2)}, u32[]{:S(2)}) %collective-permute-start.1) | collective-permute-done | bytes 131104 | tf_op jit(solution)/shard_map/ppermute | solution.py:21
  50.4 3.0 %collective-permute-done.2 = f32[128,256]{1,0:T(8,128)S(1)} collective-permute-done((f32[128,256]{1,0:T(8,128)S(1)}, f32[128,256]{1,0:T(8,128)S(1)}, u32[]{:S(2)}, u32[]{:S(2)}) %collective-permute-start.2) | collective-permute-done | bytes 131104 | tf_op jit(solution)/shard_map/ppermute | solution.py:21
  53.4 2.8 %collective-permute-start.3 = (f32[128,256]{1,0:T(8,128)S(1)}, f32[128,256]{1,0:T(8,128)S(1)}, u32[]{:S(2)}, u32[]{:S(2)}) collective-permute-start(f32[128,256]{1,0:T(8,128)S(1)} %add.117), channel_id=1, source_target_pairs={{0,2},{1,3},{2,0},{3,1},{4,6},{5,7},{6,4},{7,5},{8,10},{9,11},{10,... | collective-permute-start | bytes 393224 | tf_op jit(solution)/shard_map/ppermute | solution.py:21
  70.1 4.4 %collective-permute-done.10 = bf16[128,256]{1,0:T(8,128)(2,1)S(1)} collective-permute-done((bf16[128,256]{1,0:T(8,128)(2,1)S(1)}, bf16[128,256]{1,0:T(8,128)(2,1)S(1)}, u32[]{:S(2)}, u32[]{:S(2)}) %collective-permute-start.10) | collective-permute-done | bytes 65568 | tf_op jit(solution)/shard_map/ppermute | solution.py:79
  74.5 11.8 %collective-permute-done.11 = bf16[128,256]{1,0:T(8,128)(2,1)S(1)} collective-permute-done((bf16[128,256]{1,0:T(8,128)(2,1)S(1)}, bf16[128,256]{1,0:T(8,128)(2,1)S(1)}, u32[]{:S(2)}, u32[]{:S(2)}) %collective-permute-start.11) | collective-permute-done | bytes 65568 | tf_op jit(solution)/shard_map/ppermute | solution.py:21
  86.4 5.2 %collective-permute-start.12 = (bf16[256,256]{1,0:T(8,128)(2,1)S(1)}, bf16[256,256]{1,0:T(8,128)(2,1)S(1)}, u32[]{:S(2)}, u32[]{:S(2)}) collective-permute-start(bf16[256,256]{1,0:T(8,128)(2,1)S(1)} %pad_maximum_fusion.10), channel_id=1, source_target_pairs={{0,64},{64,0},{128,192},{192,128},{1,65},{65,1},{129,193},{193,129... | collective-permute-start | bytes 393224 | tf_op jit(solution)/shard_map/ppermute | solution.py:21
  94.2 3.8 %collective-permute-start.13 = (f32[128,256]{1,0:T(8,128)S(1)}, f32[128,256]{1,0:T(8,128)S(1)}, u32[]{:S(2)}, u32[]{:S(2)}) collective-permute-start(f32[128,256]{1,0:T(8,128)S(1)} %slice_add_fusion.1), channel_id=1, source_target_pairs={{0,1},{1,0},{2,3},{3,2},{4,5},{5,4},{6,7},{7,6},{8,9},{9,8},{10,11... | collective-permute-start | bytes 393224 | tf_op jit(solution)/shard_map/ppermute | solution.py:21
  98.0 3.5 %collective-permute-done.13 = f32[128,256]{1,0:T(8,128)S(1)} collective-permute-done((f32[128,256]{1,0:T(8,128)S(1)}, f32[128,256]{1,0:T(8,128)S(1)}, u32[]{:S(2)}, u32[]{:S(2)}) %collective-permute-start.13) | collective-permute-done | bytes 131104 | tf_op jit(solution)/shard_map/ppermute | solution.py:21
  101.6 3.0 %collective-permute-start.14 = (f32[128,256]{1,0:T(8,128)S(1)}, f32[128,256]{1,0:T(8,128)S(1)}, u32[]{:S(2)}, u32[]{:S(2)}) collective-permute-start(f32[128,256]{1,0:T(8,128)S(1)} %add.124), channel_id=1, source_target_pairs={{0,2},{1,3},{2,0},{3,1},{4,6},{5,7},{6,4},{7,5},{8,10},{9,11},{10,... | collective-permute-start | bytes 393224 | tf_op jit(solution)/shard_map/ppermute | solution.py:21
  109.3 3.4 %collective-permute-done.15 = f32[128,256]{1,0:T(8,128)S(1)} collective-permute-done((f32[128,256]{1,0:T(8,128)S(1)}, f32[128,256]{1,0:T(8,128)S(1)}, u32[]{:S(2)}, u32[]{:S(2)}) %collective-permute-start.15) | collective-permute-done | bytes 131104 | tf_op jit(solution)/shard_map/ppermute | solution.py:21
  112.8 2.8 %collective-permute-start.18 = (bf16[128,256]{1,0:T(8,128)(2,1)S(1)}, bf16[128,256]{1,0:T(8,128)(2,1)S(1)}, u32[]{:S(2)}, u32[]{:S(2)}) collective-permute-start(bf16[128,256]{1,0:T(8,128)(2,1)S(1)} %multiply_convert_fusion.1), channel_id=1, source_target_pairs={{0,32},{1,24},{3,40},{2,16},{4,48},{5,8},{7,56},{6,0},{9,41},{8,33... | collective-permute-start | bytes 196616 | tf_op jit(solution)/shard_map/ppermute | solution.py:79
  115.6 6.7 %collective-permute-done.18 = bf16[128,256]{1,0:T(8,128)(2,1)S(1)} collective-permute-done((bf16[128,256]{1,0:T(8,128)(2,1)S(1)}, bf16[128,256]{1,0:T(8,128)(2,1)S(1)}, u32[]{:S(2)}, u32[]{:S(2)}) %collective-permute-start.18) | collective-permute-done | bytes 65568 | tf_op jit(solution)/shard_map/ppermute | solution.py:79
  125.5 5.2 %collective-permute-start.20 = (bf16[256,256]{1,0:T(8,128)(2,1)S(1)}, bf16[256,256]{1,0:T(8,128)(2,1)S(1)}, u32[]{:S(2)}, u32[]{:S(2)}) collective-permute-start(bf16[256,256]{1,0:T(8,128)(2,1)S(1)} %pad_maximum_fusion.12), channel_id=1, source_target_pairs={{0,64},{64,0},{128,192},{192,128},{1,65},{65,1},{129,193},{193,129... | collective-permute-start | bytes 393224 | tf_op jit(solution)/shard_map/ppermute | solution.py:21
  132.7 4.2 %collective-permute-done.21 = f32[128,256]{1,0:T(8,128)S(1)} collective-permute-done((f32[128,256]{1,0:T(8,128)S(1)}, f32[128,256]{1,0:T(8,128)S(1)}, u32[]{:S(2)}, u32[]{:S(2)}) %collective-permute-start.21) | collective-permute-done | bytes 131104 | tf_op jit(solution)/shard_map/ppermute | solution.py:21
  138.6 3.8 %collective-permute-done.22 = f32[128,256]{1,0:T(8,128)S(1)} collective-permute-done((f32[128,256]{1,0:T(8,128)S(1)}, f32[128,256]{1,0:T(8,128)S(1)}, u32[]{:S(2)}, u32[]{:S(2)}) %collective-permute-start.22) | collective-permute-done | bytes 131104 | tf_op jit(solution)/shard_map/ppermute | solution.py:21
  142.6 5.2 %collective-permute-done.23 = f32[128,256]{1,0:T(8,128)S(1)} collective-permute-done((f32[128,256]{1,0:T(8,128)S(1)}, f32[128,256]{1,0:T(8,128)S(1)}, u32[]{:S(2)}, u32[]{:S(2)}) %collective-permute-start.23) | collective-permute-done | bytes 131104 | tf_op jit(solution)/shard_map/ppermute | solution.py:21
  148.0 4.2 %collective-permute-start.17 = (bf16[256,256]{1,0:T(8,128)(2,1)S(1)}, bf16[256,256]{1,0:T(8,128)(2,1)S(1)}, u32[]{:S(2)}, u32[]{:S(2)}) collective-permute-start(bf16[256,256]{1,0:T(8,128)(2,1)S(1)} %pad_maximum_fusion.11), channel_id=1, source_target_pairs={{0,64},{64,0},{128,192},{192,128},{1,65},{65,1},{129,193},{193,129... | collective-permute-start | bytes 393224 | tf_op jit(solution)/shard_map/ppermute | solution.py:21
  152.2 4.2 %collective-permute-start.25 = (bf16[256,256]{1,0:T(8,128)(2,1)S(1)}, bf16[256,256]{1,0:T(8,128)(2,1)S(1)}, u32[]{:S(2)}, u32[]{:S(2)}) collective-permute-start(bf16[256,256]{1,0:T(8,128)(2,1)S(1)} %pad_maximum_fusion.13), channel_id=1, source_target_pairs={{0,64},{64,0},{128,192},{192,128},{1,65},{65,1},{129,193},{193,129... | collective-permute-start | bytes 393224 | tf_op jit(solution)/shard_map/ppermute | solution.py:21
  (113 shorter events, 48.0 us)
Async XLA Ops:
  2.9 27.4 %collective-permute-start.7 = (bf16[2,512,256]{1,2,0:T(8,128)(2,1)S(1)}, bf16[2,512,256]{1,2,0:T(8,128)(2,1)}, u32[]{:S(2)}, u32[]{:S(2)}) collective-permute-start(bf16[2,512,256]{1,2,0:T(8,128)(2,1)S(1)} %slice.50), channel_id=1, source_target_pairs={{0,64},{64,128},{128,192},{1,65},{65,129},{129,193},{2,66},{66,130... | collective-permute-start | bytes 1572872 | tf_op jit(solution)/shard_map/ppermute | solution.py:115
  20.9 21.2 %collective-permute-start = (f32[256,256]{1,0:T(8,128)}, f32[256,256]{1,0:T(8,128)}, u32[]{:S(2)}, u32[]{:S(2)}) collective-permute-start(f32[256,256]{1,0:T(8,128)} %constant_dynamic-slice_fusion.3), channel_id=1, source_target_pairs={{0,64},{64,0},{128,192},{192,128},{1,65},{65,1},{129,193},{193,129... | collective-permute-start | bytes 786440 | tf_op jit(solution)/shard_map/ppermute | solution.py:21
  41.5 25.6 %collective-permute-start.8 = (f32[256,1536]{1,0:T(8,128)}, f32[256,1536]{1,0:T(8,128)}, u32[]{:S(2)}, u32[]{:S(2)}) collective-permute-start(f32[256,1536]{1,0:T(8,128)} %constant_dynamic-slice_fusion.1), channel_id=1, source_target_pairs={{0,64},{64,0},{128,192},{192,128},{1,65},{65,1},{129,193},{193,129... | collective-permute-start | bytes 4718600 | tf_op jit(solution)/shard_map/ppermute | solution.py:21
  43.8 5.3 %collective-permute-start.1 = (f32[128,256]{1,0:T(8,128)}, f32[128,256]{1,0:T(8,128)S(1)}, u32[]{:S(2)}, u32[]{:S(2)}) collective-permute-start(f32[128,256]{1,0:T(8,128)} %constant_dynamic-slice_fusion.2), channel_id=1, source_target_pairs={{0,128},{64,192},{128,0},{192,64},{1,129},{65,193},{129,1},{193,65... | collective-permute-start | bytes 393224 | tf_op jit(solution)/shard_map/ppermute | solution.py:21
  49.1 4.3 %collective-permute-start.2 = (f32[128,256]{1,0:T(8,128)S(1)}, f32[128,256]{1,0:T(8,128)S(1)}, u32[]{:S(2)}, u32[]{:S(2)}) collective-permute-start(f32[128,256]{1,0:T(8,128)S(1)} %dynamic-slice_add_fusion.3), channel_id=1, source_target_pairs={{0,1},{1,0},{2,3},{3,2},{4,5},{5,4},{6,7},{7,6},{8,9},{9,8},{10,11... | collective-permute-start | bytes 393224 | tf_op jit(solution)/shard_map/ppermute | solution.py:21
  53.4 5.4 %collective-permute-start.3 = (f32[128,256]{1,0:T(8,128)S(1)}, f32[128,256]{1,0:T(8,128)S(1)}, u32[]{:S(2)}, u32[]{:S(2)}) collective-permute-start(f32[128,256]{1,0:T(8,128)S(1)} %add.117), channel_id=1, source_target_pairs={{0,2},{1,3},{2,0},{3,1},{4,6},{5,7},{6,4},{7,5},{8,10},{9,11},{10,... | collective-permute-start | bytes 393224 | tf_op jit(solution)/shard_map/ppermute | solution.py:21
  58.8 5.4 %collective-permute-start.4 = (f32[128,256]{1,0:T(8,128)S(1)}, f32[128,256]{1,0:T(8,128)S(1)}, u32[]{:S(2)}, u32[]{:S(2)}) collective-permute-start(f32[128,256]{1,0:T(8,128)S(1)} %add.118), channel_id=1, source_target_pairs={{0,4},{1,5},{2,6},{3,7},{4,0},{5,1},{6,2},{7,3},{8,12},{9,13},{10,... | collective-permute-start | bytes 393224 | tf_op jit(solution)/shard_map/ppermute | solution.py:21
  65.2 9.3 %collective-permute-start.10 = (bf16[128,256]{1,0:T(8,128)(2,1)S(1)}, bf16[128,256]{1,0:T(8,128)(2,1)S(1)}, u32[]{:S(2)}, u32[]{:S(2)}) collective-permute-start(bf16[128,256]{1,0:T(8,128)(2,1)S(1)} %multiply_convert_fusion.2), channel_id=1, source_target_pairs={{0,32},{1,24},{3,40},{2,16},{4,48},{5,8},{7,56},{6,0},{9,41},{8,33... | collective-permute-start | bytes 196616 | tf_op jit(solution)/shard_map/ppermute | solution.py:79
  70.0 22.6 %collective-permute-start.9 = (f32[128,1536]{1,0:T(8,128)S(1)}, f32[128,1536]{1,0:T(8,128)S(1)}, u32[]{:S(2)}, u32[]{:S(2)}) collective-permute-start(f32[128,1536]{1,0:T(8,128)S(1)} %constant_dynamic-slice_fusion), channel_id=1, source_target_pairs={{0,128},{64,192},{128,0},{192,64},{1,129},{65,193},{129,1},{193,65... | collective-permute-start | bytes 2359304 | tf_op jit(solution)/shard_map/ppermute | solution.py:21
  74.5 11.8 %collective-permute-start.11 = (bf16[128,256]{1,0:T(8,128)(2,1)S(1)}, bf16[128,256]{1,0:T(8,128)(2,1)S(1)}, u32[]{:S(2)}, u32[]{:S(2)}) collective-permute-start(bf16[128,256]{1,0:T(8,128)(2,1)S(1)} %collective-permute-done.10), channel_id=1, source_target_pairs={{0,128},{64,192},{128,0},{192,64},{1,129},{65,193},{129,1},{193,65... | collective-permute-start | bytes 196616 | tf_op jit(solution)/shard_map/ppermute | solution.py:21
  86.4 6.2 %collective-permute-start.12 = (bf16[256,256]{1,0:T(8,128)(2,1)S(1)}, bf16[256,256]{1,0:T(8,128)(2,1)S(1)}, u32[]{:S(2)}, u32[]{:S(2)}) collective-permute-start(bf16[256,256]{1,0:T(8,128)(2,1)S(1)} %pad_maximum_fusion.10), channel_id=1, source_target_pairs={{0,64},{64,0},{128,192},{192,128},{1,65},{65,1},{129,193},{193,129... | collective-permute-start | bytes 393224 | tf_op jit(solution)/shard_map/ppermute | solution.py:21
  94.2 7.4 %collective-permute-start.13 = (f32[128,256]{1,0:T(8,128)S(1)}, f32[128,256]{1,0:T(8,128)S(1)}, u32[]{:S(2)}, u32[]{:S(2)}) collective-permute-start(f32[128,256]{1,0:T(8,128)S(1)} %slice_add_fusion.1), channel_id=1, source_target_pairs={{0,1},{1,0},{2,3},{3,2},{4,5},{5,4},{6,7},{7,6},{8,9},{9,8},{10,11... | collective-permute-start | bytes 393224 | tf_op jit(solution)/shard_map/ppermute | solution.py:21
  101.6 5.7 %collective-permute-start.14 = (f32[128,256]{1,0:T(8,128)S(1)}, f32[128,256]{1,0:T(8,128)S(1)}, u32[]{:S(2)}, u32[]{:S(2)}) collective-permute-start(f32[128,256]{1,0:T(8,128)S(1)} %add.124), channel_id=1, source_target_pairs={{0,2},{1,3},{2,0},{3,1},{4,6},{5,7},{6,4},{7,5},{8,10},{9,11},{10,... | collective-permute-start | bytes 393224 | tf_op jit(solution)/shard_map/ppermute | solution.py:21
  107.3 5.4 %collective-permute-start.15 = (f32[128,256]{1,0:T(8,128)S(1)}, f32[128,256]{1,0:T(8,128)S(1)}, u32[]{:S(2)}, u32[]{:S(2)}) collective-permute-start(f32[128,256]{1,0:T(8,128)S(1)} %add.125), channel_id=1, source_target_pairs={{0,4},{1,5},{2,6},{3,7},{4,0},{5,1},{6,2},{7,3},{8,12},{9,13},{10,... | collective-permute-start | bytes 393224 | tf_op jit(solution)/shard_map/ppermute | solution.py:21
  112.8 9.5 %collective-permute-start.18 = (bf16[128,256]{1,0:T(8,128)(2,1)S(1)}, bf16[128,256]{1,0:T(8,128)(2,1)S(1)}, u32[]{:S(2)}, u32[]{:S(2)}) collective-permute-start(bf16[128,256]{1,0:T(8,128)(2,1)S(1)} %multiply_convert_fusion.1), channel_id=1, source_target_pairs={{0,32},{1,24},{3,40},{2,16},{4,48},{5,8},{7,56},{6,0},{9,41},{8,33... | collective-permute-start | bytes 196616 | tf_op jit(solution)/shard_map/ppermute | solution.py:79
  122.3 8.4 %collective-permute-start.5 = (bf16[128,256]{1,0:T(8,128)(2,1)S(1)}, bf16[128,256]{1,0:T(8,128)(2,1)S(1)}, u32[]{:S(2)}, u32[]{:S(2)}) collective-permute-start(bf16[128,256]{1,0:T(8,128)(2,1)S(1)} %multiply_convert_fusion.2), channel_id=1, source_target_pairs={{0,128},{64,192},{128,0},{192,64},{1,129},{65,193},{129,1},{193,65... | collective-permute-start | bytes 196616 | tf_op jit(solution)/shard_map/ppermute | solution.py:21
  125.5 6.2 %collective-permute-start.20 = (bf16[256,256]{1,0:T(8,128)(2,1)S(1)}, bf16[256,256]{1,0:T(8,128)(2,1)S(1)}, u32[]{:S(2)}, u32[]{:S(2)}) collective-permute-start(bf16[256,256]{1,0:T(8,128)(2,1)S(1)} %pad_maximum_fusion.12), channel_id=1, source_target_pairs={{0,64},{64,0},{128,192},{192,128},{1,65},{65,1},{129,193},{193,129... | collective-permute-start | bytes 393224 | tf_op jit(solution)/shard_map/ppermute | solution.py:21
  132.1 4.8 %collective-permute-start.21 = (f32[128,256]{1,0:T(8,128)S(1)}, f32[128,256]{1,0:T(8,128)S(1)}, u32[]{:S(2)}, u32[]{:S(2)}) collective-permute-start(f32[128,256]{1,0:T(8,128)S(1)} %fusion.28), channel_id=1, source_target_pairs={{0,1},{1,0},{2,3},{3,2},{4,5},{5,4},{6,7},{7,6},{8,9},{9,8},{10,11... | collective-permute-start | bytes 393224 | tf_op jit(solution)/shard_map/ppermute | solution.py:21
  132.3 6.1 %collective-permute-start.6 = (bf16[256,256]{1,0:T(8,128)(2,1)S(1)}, bf16[256,256]{1,0:T(8,128)(2,1)S(1)}, u32[]{:S(2)}, u32[]{:S(2)}) collective-permute-start(bf16[256,256]{1,0:T(8,128)(2,1)S(1)} %pad_maximum_fusion.9), channel_id=1, source_target_pairs={{0,64},{64,0},{128,192},{192,128},{1,65},{65,1},{129,193},{193,129... | collective-permute-start | bytes 393224 | tf_op jit(solution)/shard_map/ppermute | solution.py:21
  136.9 5.4 %collective-permute-start.22 = (f32[128,256]{1,0:T(8,128)S(1)}, f32[128,256]{1,0:T(8,128)S(1)}, u32[]{:S(2)}, u32[]{:S(2)}) collective-permute-start(f32[128,256]{1,0:T(8,128)S(1)} %add.130), channel_id=1, source_target_pairs={{0,2},{1,3},{2,0},{3,1},{4,6},{5,7},{6,4},{7,5},{8,10},{9,11},{10,... | collective-permute-start | bytes 393224 | tf_op jit(solution)/shard_map/ppermute | solution.py:21
  142.4 5.4 %collective-permute-start.23 = (f32[128,256]{1,0:T(8,128)S(1)}, f32[128,256]{1,0:T(8,128)S(1)}, u32[]{:S(2)}, u32[]{:S(2)}) collective-permute-start(f32[128,256]{1,0:T(8,128)S(1)} %add.131), channel_id=1, source_target_pairs={{0,4},{1,5},{2,6},{3,7},{4,0},{5,1},{6,2},{7,3},{8,12},{9,13},{10,... | collective-permute-start | bytes 393224 | tf_op jit(solution)/shard_map/ppermute | solution.py:21
  147.9 4.3 %collective-permute-start.24 = (bf16[128,256]{1,0:T(8,128)(2,1)S(1)}, bf16[128,256]{1,0:T(8,128)(2,1)S(1)}, u32[]{:S(2)}, u32[]{:S(2)}) collective-permute-start(bf16[128,256]{1,0:T(8,128)(2,1)S(1)} %multiply_convert_fusion), channel_id=1, source_target_pairs={{0,128},{64,192},{128,0},{192,64},{1,129},{65,193},{129,1},{193,65... | collective-permute-start | bytes 196616 | tf_op jit(solution)/shard_map/ppermute | solution.py:21
  148.0 8.5 %collective-permute-start.17 = (bf16[256,256]{1,0:T(8,128)(2,1)S(1)}, bf16[256,256]{1,0:T(8,128)(2,1)S(1)}, u32[]{:S(2)}, u32[]{:S(2)}) collective-permute-start(bf16[256,256]{1,0:T(8,128)(2,1)S(1)} %pad_maximum_fusion.11), channel_id=1, source_target_pairs={{0,64},{64,0},{128,192},{192,128},{1,65},{65,1},{129,193},{193,129... | collective-permute-start | bytes 393224 | tf_op jit(solution)/shard_map/ppermute | solution.py:21
  152.2 5.2 %collective-permute-start.25 = (bf16[256,256]{1,0:T(8,128)(2,1)S(1)}, bf16[256,256]{1,0:T(8,128)(2,1)S(1)}, u32[]{:S(2)}, u32[]{:S(2)}) collective-permute-start(bf16[256,256]{1,0:T(8,128)(2,1)S(1)} %pad_maximum_fusion.13), channel_id=1, source_target_pairs={{0,64},{64,0},{128,192},{192,128},{1,65},{65,1},{129,193},{193,129... | collective-permute-start | bytes 393224 | tf_op jit(solution)/shard_map/ppermute | solution.py:21
  (13 other events, 114.8 us)

commit v7 on v5

--- a/solution.py
+++ b/solution.py
@@ -109,11 +109,17 @@
         allowed_here = jnp.repeat(jnp.repeat(causal_mask[:, lag_index, :], block_size, 0), block_size, 1) > 0
         serial.append(jnp.where(allowed_here, kernel[:, lag_index, :], jnp.zeros_like(kernel[:, lag_index, :])))
     serial = jnp.stack(serial)
-    own = lax.dynamic_slice_in_dim(serial, offset, chunk_rows, 1)
-    for target in range(1, lag_n):
-        start = chunk_offset(target, rows_here)
-        arrived = lax.ppermute(serial[:, start:start + chunk_rows], "lag", [(0, target)])
-        own = jnp.where(lag_pos == target, arrived, own)
+    def rows_of(targets):
+        starts = [chunk_offset(t, rows_here) for t in targets]
+        return jnp.concatenate([serial[:, a:a + chunk_rows] for a in starts], axis=1)
+
+    far, near = lag_n // 2, 1
+    far_side = rows_of([far, far + near])
+    arrived = lax.ppermute(far_side, "lag", [(0, far)])
+    held = jnp.where(lag_pos == far, arrived, far_side)
+    passed = jnp.where(lag_pos == 0, rows_of([near]), held[:, chunk_rows:])
+    arrived = lax.ppermute(passed, "lag", [(0, near), (far, far + near)])
+    own = jnp.where(lag_pos == 0, rows_of([0]), jnp.where(lag_pos == far, held[:, :chunk_rows], arrived))
 
     ahead = STEPS - 1
     earlier = lax.ppermute(history[lag_here - ahead:], "lag", [(i, i + 1) for i in range(lag_n - 1)])

time: 143 us -> 149 us (1.042)
  waiting for transfers between devices: 57.3 us -> 60.5 us
  local copies, waits for them, and re-layouts: 13.4 us -> 16.6 us
    ppermute x23, waiting for transfers between devices: 39.2 us -> 42.7 us  [swap(): return lax.ppermute(block, axis, [(i, i ^ mask) for i in range(size)])]
    unnamed x19 -> x25, local copies, waits for them, and re-layouts: 2.91 us -> 5.4 us
    concatenate x0 -> x1, other arithmetic: none -> 1.82 us  [rows_of(): jnp.concatenate([serial[:, a:a + chunk_rows] for a in starts], axis=1)]
    ppermute x3 -> x2, starting transfers between devices: 3.3 us -> 2.74 us  [the longest x1 1.44 us: local(): arrived = lax.ppermute(far_side, 'lag', [(0, far)])]
  transfers between devices with their start and end apart: 29 -> 28, of which waited for: 14 -> 15; matrix products, arithmetic and copies ran while one was open for 20% -> 25% of each run, Pallas kernels for 0% -> 0%
where the time goes in v7:
time: 149 us; the launch traced here: 147 us
  waiting for transfers between devices  60.5 us (41%)
  starting transfers between devices  40.7 us (27%)
  other arithmetic  17.1 us (11%)
  local copies, waits for them, and re-layouts  16.6 us (11%)
  matrix products  11.4 us (8%)
    ppermute x23, waiting for transfers between devices, swap(): return lax.ppermute(block, axis, [(i, i ^ mask) for i in range(size)])  42.7 us
    ppermute x23, starting transfers between devices, swap(): return lax.ppermute(block, axis, [(i, i ^ mask) for i in range(size)])  33.8 us
    ppermute x2, waiting for transfers between devices, transposed(): return lax.ppermute(chunk, ('recv', 'src'), route)  17.8 us
    select_n x1, other arithmetic, local(): jnp.where(allowed, kernel, jnp.zeros_like(kernel))  8.71 us
    dot_general x2, matrix products, local(): jnp.dot(masked_rows, shifted.reshape(lag_here * cols_here, scenarios), pr...  8.38 us
    unnamed x25, local copies, waits for them, and re-layouts  5.4 us
    slice x1, local copies, waits for them, and re-layouts, local(): kernel[:, lag_index, :]  4.9 us
    ppermute x1, starting transfers between devices, local(): lax.ppermute(history[lag_here - ahead:], 'lag', [(i, i + 1) for i in rang...  3.75 us
  transfers between devices with their start and end apart: 28, of which 15 were waited for; matrix products, arithmetic and copies ran while one was open for 25% of the time, Pallas kernels for 0%

profile of v7, /device:TPU:225, one launch (start us, length us, event | category | flops | bytes accessed | tf_op | source)
XLA Modules:
  0.0 146.9 jit_solution(8152467605437109322)
XLA Ops:
  0.0 2.9 %copy.26 = bf16[8,512,256]{1,2,0:T(8,128)(2,1)S(1)} copy(bf16[8,512,256]{2,1,0:T(8,128)(2,1)} %param.9) | data formatting | bytes 4194304 | tf_op args[2]
  3.8 3.8 %collective-permute-start.7 = (bf16[2,512,256]{1,2,0:T(8,128)(2,1)}, bf16[2,512,256]{1,2,0:T(8,128)(2,1)}, u32[]{:S(2)}, u32[]{:S(2)}) collective-permute-start(bf16[2,512,256]{1,2,0:T(8,128)(2,1)} %slice.69), channel_id=1, source_target_pairs={{0,64},{64,128},{128,192},{1,65},{65,129},{129,193},{2,66},{66,130... | collective-permute-start | bytes 1572872 | tf_op jit(solution)/shard_map/ppermute | solution.py:125
  7.7 8.7 %bitcast_select_fusion = bf16[512,8,512]{2,1,0:T(8,128)(2,1)S(1)} fusion(bf16[512,8,512]{2,1,0:T(8,128)(2,1)} %param.7, pred[512,8,4]{1,2,0:T(4,128)(4,1)S(1)} %bitcast.37), kind=kLoop, calls=%fused_computation | loop fusion | flops 2097152 | bytes 8404992 | tf_op jit(solution)/shard_map/jit(_where)/select_n | solution.py:98
  18.4 2.4 %fusion.9 = f32[512,256]{1,0:T(8,128)S(1)} fusion(bf16[8,512,256]{2,1,0:T(8,128)(2,1)S(1)} %copy-done.5, bf16[512,8,512]{2,1,0:T(8,128)(2,1)S(1)} %bitcast_select_fusion), kind=kOutput, calls=%fused_computation.22 | convolution fusion | flops 1073741824 | bytes 6815744 | tf_op jit(solution)/shard_map/dot_general | solution.py:127
  21.8 4.9 %fusion.43 = (bf16[512,1,512]{2,1,0:T(2,128)(2,1)S(1)}, bf16[512,1,512]{2,1,0:T(2,128)(2,1)S(1)}) fusion(bf16[512,8,512]{2,1,0:T(8,128)(2,1)} %param.7), kind=kLoop, calls=%fused_computation.104 | loop fusion | bytes 2097152 | tf_op jit(solution)/shard_map/slice | solution.py:110
  33.6 3.2 %collective-permute-done.1 = f32[128,256]{1,0:T(8,128)} collective-permute-done((f32[128,256]{1,0:T(8,128)S(1)}, f32[128,256]{1,0:T(8,128)}, u32[]{:S(2)}, u32[]{:S(2)}) %collective-permute-start.1) | collective-permute-done | bytes 131104 | tf_op jit(solution)/shard_map/ppermute | solution.py:21
  44.1 2.5 %collective-permute-start.3 = (f32[128,256]{1,0:T(8,128)S(1)}, f32[128,256]{1,0:T(8,128)S(1)}, u32[]{:S(2)}, u32[]{:S(2)}) collective-permute-start(f32[128,256]{1,0:T(8,128)S(1)} %add.117), channel_id=1, source_target_pairs={{0,2},{1,3},{2,0},{3,1},{4,6},{5,7},{6,4},{7,5},{8,10},{9,11},{10,... | collective-permute-start | bytes 393224 | tf_op jit(solution)/shard_map/ppermute | solution.py:21
  46.6 4.7 %fusion.15 = f32[512,256]{1,0:T(8,128)S(1)} fusion(bf16[2,512,256]{1,2,0:T(8,128)(2,1)} %collective-permute-done.7, bf16[8,512,256]{1,2,0:T(8,128)(2,1)S(1)} %copy-done.3, bf16[512,8,512]{2,1,0:T(8,128)(2,1)} %copy-done), kind=kOutput, calls=%fused_computation.24 | convolution fusion | flops 1074790400 | bytes 7340032 | tf_op jit(solution)/shard_map/dot_general | solution.py:132
  51.4 2.9 %collective-permute-start.4 = (f32[128,256]{1,0:T(8,128)S(1)}, f32[128,256]{1,0:T(8,128)S(1)}, u32[]{:S(2)}, u32[]{:S(2)}) collective-permute-start(f32[128,256]{1,0:T(8,128)S(1)} %add.118), channel_id=1, source_target_pairs={{0,4},{1,5},{2,6},{3,7},{4,0},{5,1},{6,2},{7,3},{8,12},{9,13},{10,... | collective-permute-start | bytes 393224 | tf_op jit(solution)/shard_map/ppermute | solution.py:21
  54.3 3.7 %fusion.12 = f32[512,256]{1,0:T(8,128)S(1)} fusion(bf16[8,512,256]{1,2,0:T(8,128)(2,1)S(1)} %copy-done.3, bf16[2,512,256]{1,2,0:T(8,128)(2,1)} %collective-permute-done.7, bf16[512,8,512]{2,1,0:T(8,128)(2,1)S(1)} %copy-done.1), kind=kOutput, calls=%fused_computation.23 | convolution fusion | flops 1074790400 | bytes 7340032 | tf_op jit(solution)/shard_map/dot_general | solution.py:132
  58.1 3.9 %collective-permute-start.8 = (f32[256,512]{1,0:T(8,128)S(1)}, f32[256,512]{1,0:T(8,128)S(1)}, u32[]{:S(2)}, u32[]{:S(2)}) collective-permute-start(f32[256,512]{1,0:T(8,128)S(1)} %fusion.20), channel_id=1, source_target_pairs={{0,64},{64,0},{128,192},{192,128},{1,65},{65,1},{129,193},{193,129... | collective-permute-start | bytes 1572872 | tf_op jit(solution)/shard_map/ppermute | solution.py:21
  62.4 9.2 %collective-permute-done.12 = bf16[128,256]{1,0:T(8,128)(2,1)S(1)} collective-permute-done((bf16[128,256]{1,0:T(8,128)(2,1)S(1)}, bf16[128,256]{1,0:T(8,128)(2,1)S(1)}, u32[]{:S(2)}, u32[]{:S(2)}) %collective-permute-start.12) | collective-permute-done | bytes 65568 | tf_op jit(solution)/shard_map/ppermute | solution.py:79
  77.9 7.0 %collective-permute-done.9 = f32[128,512]{1,0:T(8,128)S(1)} collective-permute-done((f32[128,512]{1,0:T(8,128)S(1)}, f32[128,512]{1,0:T(8,128)S(1)}, u32[]{:S(2)}, u32[]{:S(2)}) %collective-permute-start.9) | collective-permute-done | bytes 262176 | tf_op jit(solution)/shard_map/ppermute | solution.py:21
  85.3 4.2 %collective-permute-done.15 = f32[128,256]{1,0:T(8,128)S(1)} collective-permute-done((f32[128,256]{1,0:T(8,128)S(1)}, f32[128,256]{1,0:T(8,128)S(1)}, u32[]{:S(2)}, u32[]{:S(2)}) %collective-permute-start.15) | collective-permute-done | bytes 131104 | tf_op jit(solution)/shard_map/ppermute | solution.py:21
  90.6 4.3 %collective-permute-done.16 = f32[128,256]{1,0:T(8,128)S(1)} collective-permute-done((f32[128,256]{1,0:T(8,128)S(1)}, f32[128,256]{1,0:T(8,128)S(1)}, u32[]{:S(2)}, u32[]{:S(2)}) %collective-permute-start.16) | collective-permute-done | bytes 131104 | tf_op jit(solution)/shard_map/ppermute | solution.py:21
  96.1 4.2 %collective-permute-done.17 = f32[128,256]{1,0:T(8,128)S(1)} collective-permute-done((f32[128,256]{1,0:T(8,128)S(1)}, f32[128,256]{1,0:T(8,128)S(1)}, u32[]{:S(2)}, u32[]{:S(2)}) %collective-permute-start.17) | collective-permute-done | bytes 131104 | tf_op jit(solution)/shard_map/ppermute | solution.py:21
  100.7 8.6 %collective-permute-done.20 = bf16[128,256]{1,0:T(8,128)(2,1)S(1)} collective-permute-done((bf16[128,256]{1,0:T(8,128)(2,1)S(1)}, bf16[128,256]{1,0:T(8,128)(2,1)S(1)}, u32[]{:S(2)}, u32[]{:S(2)}) %collective-permute-start.20) | collective-permute-done | bytes 65568 | tf_op jit(solution)/shard_map/ppermute | solution.py:79
  109.9 2.8 %collective-permute-done.21 = bf16[128,256]{1,0:T(8,128)(2,1)S(1)} collective-permute-done((bf16[128,256]{1,0:T(8,128)(2,1)S(1)}, bf16[128,256]{1,0:T(8,128)(2,1)S(1)}, u32[]{:S(2)}, u32[]{:S(2)}) %collective-permute-start.21) | collective-permute-done | bytes 65568 | tf_op jit(solution)/shard_map/ppermute | solution.py:21
  112.8 6.1 %collective-permute-start.22 = (bf16[256,256]{1,0:T(8,128)(2,1)S(1)}, bf16[256,256]{1,0:T(8,128)(2,1)S(1)}, u32[]{:S(2)}, u32[]{:S(2)}) collective-permute-start(bf16[256,256]{1,0:T(8,128)(2,1)S(1)} %pad_maximum_fusion.13), channel_id=1, source_target_pairs={{0,64},{64,0},{128,192},{192,128},{1,65},{65,1},{129,193},{193,129... | collective-permute-start | bytes 393224 | tf_op jit(solution)/shard_map/ppermute | solution.py:21
  120.8 4.3 %collective-permute-done.23 = f32[128,256]{1,0:T(8,128)S(1)} collective-permute-done((f32[128,256]{1,0:T(8,128)S(1)}, f32[128,256]{1,0:T(8,128)S(1)}, u32[]{:S(2)}, u32[]{:S(2)}) %collective-permute-start.23) | collective-permute-done | bytes 131104 | tf_op jit(solution)/shard_map/ppermute | solution.py:21
  127.5 3.1 %collective-permute-done.24 = f32[128,256]{1,0:T(8,128)S(1)} collective-permute-done((f32[128,256]{1,0:T(8,128)S(1)}, f32[128,256]{1,0:T(8,128)S(1)}, u32[]{:S(2)}, u32[]{:S(2)}) %collective-permute-start.24) | collective-permute-done | bytes 131104 | tf_op jit(solution)/shard_map/ppermute | solution.py:21
  130.7 5.3 %collective-permute-done.25 = f32[128,256]{1,0:T(8,128)S(1)} collective-permute-done((f32[128,256]{1,0:T(8,128)S(1)}, f32[128,256]{1,0:T(8,128)S(1)}, u32[]{:S(2)}, u32[]{:S(2)}) %collective-permute-start.25) | collective-permute-done | bytes 131104 | tf_op jit(solution)/shard_map/ppermute | solution.py:21
  136.5 4.6 %collective-permute-start.19 = (bf16[256,256]{1,0:T(8,128)(2,1)S(1)}, bf16[256,256]{1,0:T(8,128)(2,1)S(1)}, u32[]{:S(2)}, u32[]{:S(2)}) collective-permute-start(bf16[256,256]{1,0:T(8,128)(2,1)S(1)} %pad_maximum_fusion.12), channel_id=1, source_target_pairs={{0,64},{64,0},{128,192},{192,128},{1,65},{65,1},{129,193},{193,129... | collective-permute-start | bytes 393224 | tf_op jit(solution)/shard_map/ppermute | solution.py:21
  141.1 3.7 %collective-permute-start.27 = (bf16[256,256]{1,0:T(8,128)(2,1)S(1)}, bf16[256,256]{1,0:T(8,128)(2,1)S(1)}, u32[]{:S(2)}, u32[]{:S(2)}) collective-permute-start(bf16[256,256]{1,0:T(8,128)(2,1)S(1)} %pad_maximum_fusion.14), channel_id=1, source_target_pairs={{0,64},{64,0},{128,192},{192,128},{1,65},{65,1},{129,193},{193,129... | collective-permute-start | bytes 393224 | tf_op jit(solution)/shard_map/ppermute | solution.py:21
  (119 shorter events, 35.3 us)
Async XLA Ops:
  3.8 42.9 %collective-permute-start.7 = (bf16[2,512,256]{1,2,0:T(8,128)(2,1)}, bf16[2,512,256]{1,2,0:T(8,128)(2,1)}, u32[]{:S(2)}, u32[]{:S(2)}) collective-permute-start(bf16[2,512,256]{1,2,0:T(8,128)(2,1)} %slice.69), channel_id=1, source_target_pairs={{0,64},{64,128},{128,192},{1,65},{65,129},{129,193},{2,66},{66,130... | collective-permute-start | bytes 1572872 | tf_op jit(solution)/shard_map/ppermute | solution.py:125
  21.8 9.1 %collective-permute-start = (f32[256,256]{1,0:T(8,128)}, f32[256,256]{1,0:T(8,128)}, u32[]{:S(2)}, u32[]{:S(2)}) collective-permute-start(f32[256,256]{1,0:T(8,128)} %constant_dynamic-slice_fusion.2), channel_id=1, source_target_pairs={{0,64},{64,0},{128,192},{192,128},{1,65},{65,1},{129,193},{193,129... | collective-permute-start | bytes 786440 | tf_op jit(solution)/shard_map/ppermute | solution.py:21
  32.0 4.7 %collective-permute-start.1 = (f32[128,256]{1,0:T(8,128)S(1)}, f32[128,256]{1,0:T(8,128)}, u32[]{:S(2)}, u32[]{:S(2)}) collective-permute-start(f32[128,256]{1,0:T(8,128)S(1)} %constant_dynamic-slice_fusion.1), channel_id=1, source_target_pairs={{0,128},{64,192},{128,0},{192,64},{1,129},{65,193},{129,1},{193,65... | collective-permute-start | bytes 393224 | tf_op jit(solution)/shard_map/ppermute | solution.py:21
  37.7 5.4 %collective-permute-start.2 = (f32[128,256]{1,0:T(8,128)S(1)}, f32[128,256]{1,0:T(8,128)}, u32[]{:S(2)}, u32[]{:S(2)}) collective-permute-start(f32[128,256]{1,0:T(8,128)S(1)} %dynamic-slice_add_fusion.2), channel_id=1, source_target_pairs={{0,1},{1,0},{2,3},{3,2},{4,5},{5,4},{6,7},{7,6},{8,9},{9,8},{10,11... | collective-permute-start | bytes 393224 | tf_op jit(solution)/shard_map/ppermute | solution.py:21
  40.9 21.3 %collective-permute-start.10 = (bf16[2,256,512]{2,1,0:T(8,128)(2,1)}, bf16[2,256,512]{2,1,0:T(8,128)(2,1)}, u32[]{:S(2)}, u32[]{:S(2)}) collective-permute-start(bf16[2,256,512]{2,1,0:T(8,128)(2,1)} %pad_maximum_fusion.5), channel_id=1, source_target_pairs={{0,128},{1,129},{2,130},{3,131},{4,132},{5,133},{6,134},{7,135},{8... | collective-permute-start | bytes 1572872 | tf_op jit(solution)/shard_map/ppermute | solution.py:118
  44.1 7.2 %collective-permute-start.3 = (f32[128,256]{1,0:T(8,128)S(1)}, f32[128,256]{1,0:T(8,128)S(1)}, u32[]{:S(2)}, u32[]{:S(2)}) collective-permute-start(f32[128,256]{1,0:T(8,128)S(1)} %add.117), channel_id=1, source_target_pairs={{0,2},{1,3},{2,0},{3,1},{4,6},{5,7},{6,4},{7,5},{8,10},{9,11},{10,... | collective-permute-start | bytes 393224 | tf_op jit(solution)/shard_map/ppermute | solution.py:21
  51.4 10.6 %collective-permute-start.4 = (f32[128,256]{1,0:T(8,128)S(1)}, f32[128,256]{1,0:T(8,128)S(1)}, u32[]{:S(2)}, u32[]{:S(2)}) collective-permute-start(f32[128,256]{1,0:T(8,128)S(1)} %add.118), channel_id=1, source_target_pairs={{0,4},{1,5},{2,6},{3,7},{4,0},{5,1},{6,2},{7,3},{8,12},{9,13},{10,... | collective-permute-start | bytes 393224 | tf_op jit(solution)/shard_map/ppermute | solution.py:21
  58.1 18.9 %collective-permute-start.8 = (f32[256,512]{1,0:T(8,128)S(1)}, f32[256,512]{1,0:T(8,128)S(1)}, u32[]{:S(2)}, u32[]{:S(2)}) collective-permute-start(f32[256,512]{1,0:T(8,128)S(1)} %fusion.20), channel_id=1, source_target_pairs={{0,64},{64,0},{128,192},{192,128},{1,65},{65,1},{129,193},{193,129... | collective-permute-start | bytes 1572872 | tf_op jit(solution)/shard_map/ppermute | solution.py:21
  62.1 9.4 %collective-permute-start.12 = (bf16[128,256]{1,0:T(8,128)(2,1)S(1)}, bf16[128,256]{1,0:T(8,128)(2,1)S(1)}, u32[]{:S(2)}, u32[]{:S(2)}) collective-permute-start(bf16[128,256]{1,0:T(8,128)(2,1)S(1)} %multiply_convert_fusion.2), channel_id=1, source_target_pairs={{0,32},{1,24},{3,40},{2,16},{4,48},{5,8},{7,56},{6,0},{9,41},{8,33... | collective-permute-start | bytes 196616 | tf_op jit(solution)/shard_map/ppermute | solution.py:79
  71.6 5.5 %collective-permute-start.11 = (bf16[2,128,512]{2,1,0:T(8,128)(2,1)S(1)}, bf16[2,128,512]{2,1,0:T(8,128)(2,1)S(1)}, u32[]{:S(2)}, u32[]{:S(2)}) collective-permute-start(bf16[2,128,512]{2,1,0:T(8,128)(2,1)S(1)} %slice_select_fusion), channel_id=1, source_target_pairs={{0,64},{128,192},{1,65},{129,193},{2,66},{130,194},{3,67},{131,195... | collective-permute-start | bytes 786440 | tf_op jit(solution)/shard_map/ppermute | solution.py:121
  77.0 7.9 %collective-permute-start.9 = (f32[128,512]{1,0:T(8,128)S(1)}, f32[128,512]{1,0:T(8,128)S(1)}, u32[]{:S(2)}, u32[]{:S(2)}) collective-permute-start(f32[128,512]{1,0:T(8,128)S(1)} %constant_dynamic-slice_fusion), channel_id=1, source_target_pairs={{0,128},{64,192},{128,0},{192,64},{1,129},{65,193},{129,1},{193,65... | collective-permute-start | bytes 786440 | tf_op jit(solution)/shard_map/ppermute | solution.py:21
  89.5 5.4 %collective-permute-start.16 = (f32[128,256]{1,0:T(8,128)S(1)}, f32[128,256]{1,0:T(8,128)S(1)}, u32[]{:S(2)}, u32[]{:S(2)}) collective-permute-start(f32[128,256]{1,0:T(8,128)S(1)} %add.124), channel_id=1, source_target_pairs={{0,2},{1,3},{2,0},{3,1},{4,6},{5,7},{6,4},{7,5},{8,10},{9,11},{10,... | collective-permute-start | bytes 393224 | tf_op jit(solution)/shard_map/ppermute | solution.py:21
  94.9 5.4 %collective-permute-start.17 = (f32[128,256]{1,0:T(8,128)S(1)}, f32[128,256]{1,0:T(8,128)S(1)}, u32[]{:S(2)}, u32[]{:S(2)}) collective-permute-start(f32[128,256]{1,0:T(8,128)S(1)} %add.125), channel_id=1, source_target_pairs={{0,4},{1,5},{2,6},{3,7},{4,0},{5,1},{6,2},{7,3},{8,12},{9,13},{10,... | collective-permute-start | bytes 393224 | tf_op jit(solution)/shard_map/ppermute | solution.py:21
  100.4 8.9 %collective-permute-start.20 = (bf16[128,256]{1,0:T(8,128)(2,1)S(1)}, bf16[128,256]{1,0:T(8,128)(2,1)S(1)}, u32[]{:S(2)}, u32[]{:S(2)}) collective-permute-start(bf16[128,256]{1,0:T(8,128)(2,1)S(1)} %multiply_convert_fusion.1), channel_id=1, source_target_pairs={{0,32},{1,24},{3,40},{2,16},{4,48},{5,8},{7,56},{6,0},{9,41},{8,33... | collective-permute-start | bytes 196616 | tf_op jit(solution)/shard_map/ppermute | solution.py:79
  112.8 7.1 %collective-permute-start.22 = (bf16[256,256]{1,0:T(8,128)(2,1)S(1)}, bf16[256,256]{1,0:T(8,128)(2,1)S(1)}, u32[]{:S(2)}, u32[]{:S(2)}) collective-permute-start(bf16[256,256]{1,0:T(8,128)(2,1)S(1)} %pad_maximum_fusion.13), channel_id=1, source_target_pairs={{0,64},{64,0},{128,192},{192,128},{1,65},{65,1},{129,193},{193,129... | collective-permute-start | bytes 393224 | tf_op jit(solution)/shard_map/ppermute | solution.py:21
  120.4 4.8 %collective-permute-start.23 = (f32[128,256]{1,0:T(8,128)S(1)}, f32[128,256]{1,0:T(8,128)S(1)}, u32[]{:S(2)}, u32[]{:S(2)}) collective-permute-start(f32[128,256]{1,0:T(8,128)S(1)} %fusion.35), channel_id=1, source_target_pairs={{0,1},{1,0},{2,3},{3,2},{4,5},{5,4},{6,7},{7,6},{8,9},{9,8},{10,11... | collective-permute-start | bytes 393224 | tf_op jit(solution)/shard_map/ppermute | solution.py:21
  120.5 4.8 %collective-permute-start.5 = (bf16[128,256]{1,0:T(8,128)(2,1)S(1)}, bf16[128,256]{1,0:T(8,128)(2,1)S(1)}, u32[]{:S(2)}, u32[]{:S(2)}) collective-permute-start(bf16[128,256]{1,0:T(8,128)(2,1)S(1)} %multiply_convert_fusion.2), channel_id=1, source_target_pairs={{0,128},{64,192},{128,0},{192,64},{1,129},{65,193},{129,1},{193,65... | collective-permute-start | bytes 196616 | tf_op jit(solution)/shard_map/ppermute | solution.py:21
  125.2 5.4 %collective-permute-start.24 = (f32[128,256]{1,0:T(8,128)S(1)}, f32[128,256]{1,0:T(8,128)S(1)}, u32[]{:S(2)}, u32[]{:S(2)}) collective-permute-start(f32[128,256]{1,0:T(8,128)S(1)} %add.130), channel_id=1, source_target_pairs={{0,2},{1,3},{2,0},{3,1},{4,6},{5,7},{6,4},{7,5},{8,10},{9,11},{10,... | collective-permute-start | bytes 393224 | tf_op jit(solution)/shard_map/ppermute | solution.py:21
  125.3 5.4 %collective-permute-start.18 = (bf16[128,256]{1,0:T(8,128)(2,1)S(1)}, bf16[128,256]{1,0:T(8,128)(2,1)S(1)}, u32[]{:S(2)}, u32[]{:S(2)}) collective-permute-start(bf16[128,256]{1,0:T(8,128)(2,1)S(1)} %multiply_convert_fusion.1), channel_id=1, source_target_pairs={{0,128},{64,192},{128,0},{192,64},{1,129},{65,193},{129,1},{193,65... | collective-permute-start | bytes 196616 | tf_op jit(solution)/shard_map/ppermute | solution.py:21
  125.9 18.9 %collective-permute-start.6 = (bf16[256,256]{1,0:T(8,128)(2,1)S(1)}, bf16[256,256]{1,0:T(8,128)(2,1)S(1)}, u32[]{:S(2)}, u32[]{:S(2)}) collective-permute-start(bf16[256,256]{1,0:T(8,128)(2,1)S(1)} %pad_maximum_fusion.10), channel_id=1, source_target_pairs={{0,64},{64,0},{128,192},{192,128},{1,65},{65,1},{129,193},{193,129... | collective-permute-start | bytes 393224 | tf_op jit(solution)/shard_map/ppermute | solution.py:21
  130.6 5.4 %collective-permute-start.25 = (f32[128,256]{1,0:T(8,128)S(1)}, f32[128,256]{1,0:T(8,128)S(1)}, u32[]{:S(2)}, u32[]{:S(2)}) collective-permute-start(f32[128,256]{1,0:T(8,128)S(1)} %add.131), channel_id=1, source_target_pairs={{0,4},{1,5},{2,6},{3,7},{4,0},{5,1},{6,2},{7,3},{8,12},{9,13},{10,... | collective-permute-start | bytes 393224 | tf_op jit(solution)/shard_map/ppermute | solution.py:21
  136.1 5.0 %collective-permute-start.26 = (bf16[128,256]{1,0:T(8,128)(2,1)S(1)}, bf16[128,256]{1,0:T(8,128)(2,1)S(1)}, u32[]{:S(2)}, u32[]{:S(2)}) collective-permute-start(bf16[128,256]{1,0:T(8,128)(2,1)S(1)} %multiply_convert_fusion), channel_id=1, source_target_pairs={{0,128},{64,192},{128,0},{192,64},{1,129},{65,193},{129,1},{193,65... | collective-permute-start | bytes 196616 | tf_op jit(solution)/shard_map/ppermute | solution.py:21
  136.5 8.4 %collective-permute-start.19 = (bf16[256,256]{1,0:T(8,128)(2,1)S(1)}, bf16[256,256]{1,0:T(8,128)(2,1)S(1)}, u32[]{:S(2)}, u32[]{:S(2)}) collective-permute-start(bf16[256,256]{1,0:T(8,128)(2,1)S(1)} %pad_maximum_fusion.12), channel_id=1, source_target_pairs={{0,64},{64,0},{128,192},{192,128},{1,65},{65,1},{129,193},{193,129... | collective-permute-start | bytes 393224 | tf_op jit(solution)/shard_map/ppermute | solution.py:21
  141.1 4.7 %collective-permute-start.27 = (bf16[256,256]{1,0:T(8,128)(2,1)S(1)}, bf16[256,256]{1,0:T(8,128)(2,1)S(1)}, u32[]{:S(2)}, u32[]{:S(2)}) collective-permute-start(bf16[256,256]{1,0:T(8,128)(2,1)S(1)} %pad_maximum_fusion.14), channel_id=1, source_target_pairs={{0,64},{64,0},{128,192},{192,128},{1,65},{65,1},{129,193},{193,129... | collective-permute-start | bytes 393224 | tf_op jit(solution)/shard_map/ppermute | solution.py:21
  (16 other events, 117.1 us)

commit v8 on v5

--- a/solution.py
+++ b/solution.py
@@ -67,16 +67,28 @@
     return hops_x + hops_y
 
 
-def transposed(chunk):
+def sources_of(chunk, rows_total):
+    lag_n = lax.axis_size("lag")
     recv_n = lax.axis_size("recv")
     src_n = lax.axis_size("src")
-    route = []
+    lag_pos = lax.axis_index("lag")
+    senders = {}
     for s in range(src_n):
         far_first = sorted(range(recv_n), key=lambda r: (-ring_distance(r, s, recv_n), r))
         near_first = sorted(range(src_n), key=lambda q: (src_distance(q, s), q))
         for r, sender in zip(far_first, near_first):
-            route.append((s * src_n + sender, r * src_n + s))
-    return lax.ppermute(chunk, ("recv", "src"), route)
+            senders[(r, s)] = sender
+    block = jnp.zeros((rows_total,) + chunk.shape[1:], chunk.dtype)
+    for shift in range(lag_n):
+        route = []
+        for g in range(lag_n):
+            for (r, s), sender in senders.items():
+                source = (((g - shift) % lag_n) * recv_n + s) * src_n + sender
+                route.append((source, (g * recv_n + r) * src_n + s))
+        piece = lax.ppermute(chunk, ("lag", "recv", "src"), route)
+        owner = (lag_pos - shift) % lag_n
+        block = lax.dynamic_update_slice_in_dim(block, piece, chunk_offset(owner, rows_total), 0)
+    return block
 
 
 def friction(stress, offset, background, classes, rate_scale, stress_scale):
@@ -140,7 +152,7 @@
         total = all_reduce_src(partial)
         rates_chunk = friction(total, offset, background, classes, rate_scale, stress_scale)
         if step_index + 1 < STEPS:
-            block = all_gather_lag(transposed(rates_chunk))
+            block = sources_of(rates_chunk, rows_here)
             sources.append(block)
         outputs.append(all_gather_lag(rates_chunk))
     return jnp.stack(outputs)

time: 143 us -> 161 us (1.13)
  the two profiles are of different devices: /device:TPU:225 before, /device:TPU:45 now
where the time goes in v8:
time: 161 us; the launch traced here: 160 us
  starting transfers between devices  68.4 us (42%)
  waiting for transfers between devices  45.5 us (28%)
  local copies, waits for them, and re-layouts  17.4 us (11%)
  other arithmetic  16.6 us (10%)
  matrix products  11.8 us (7%)
    ppermute x8, starting transfers between devices, sources_of(): piece = lax.ppermute(chunk, ('lag', 'recv', 'src'), route)  32 us
    ppermute x19, starting transfers between devices, swap(): return lax.ppermute(block, axis, [(i, i ^ mask) for i in range(size)])  31.1 us
    ppermute x19, waiting for transfers between devices, swap(): return lax.ppermute(block, axis, [(i, i ^ mask) for i in range(size)])  23.6 us
    ppermute x8, waiting for transfers between devices, sources_of(): piece = lax.ppermute(chunk, ('lag', 'recv', 'src'), route)  22 us
    dot_general x2, matrix products, local(): jnp.dot(masked_rows, shifted.reshape(lag_here * cols_here, scenarios), pr...  8.77 us
    select_n x1, other arithmetic, local(): jnp.where(allowed, kernel, jnp.zeros_like(kernel))  8.71 us
    slice x1, local copies, waits for them, and re-layouts, local(): kernel[:, lag_index, :]  4.9 us
    unnamed x19, local copies, waits for them, and re-layouts  4.88 us
  transfers between devices with their start and end apart: 31, of which 14 were waited for; matrix products, arithmetic and copies ran while one was open for 24% of the time, Pallas kernels for 0%

profile of v8, /device:TPU:45, one launch (start us, length us, event | category | flops | bytes accessed | tf_op | source)
XLA Modules:
  0.0 160.2 jit_solution(9092561412826605563)
XLA Ops:
  0.0 2.9 %copy.26 = bf16[8,512,256]{1,2,0:T(8,128)(2,1)S(1)} copy(bf16[8,512,256]{2,1,0:T(8,128)(2,1)} %param.9) | data formatting | bytes 4194304 | tf_op args[2]
  5.2 8.7 %bitcast_select_fusion = bf16[512,8,512]{2,1,0:T(8,128)(2,1)S(1)} fusion(bf16[512,8,512]{2,1,0:T(8,128)(2,1)} %param.7, pred[512,8,4]{1,2,0:T(4,128)(4,1)S(1)} %bitcast.40), kind=kLoop, calls=%fused_computation | loop fusion | flops 2097152 | bytes 8404992 | tf_op jit(solution)/shard_map/jit(_where)/select_n | solution.py:110
  15.9 2.4 %fusion.9 = f32[512,256]{1,0:T(8,128)S(1)} fusion(bf16[8,512,256]{2,1,0:T(8,128)(2,1)S(1)} %copy-done.2, bf16[512,8,512]{2,1,0:T(8,128)(2,1)S(1)} %bitcast_select_fusion), kind=kOutput, calls=%fused_computation.24 | convolution fusion | flops 1073741824 | bytes 6815744 | tf_op jit(solution)/shard_map/dot_general | solution.py:133
  24.5 4.9 %fusion.40 = (bf16[512,1,512]{2,1,0:T(2,128)(2,1)S(1)}, bf16[512,1,512]{2,1,0:T(2,128)(2,1)S(1)}) fusion(bf16[512,8,512]{2,1,0:T(8,128)(2,1)} %param.7), kind=kLoop, calls=%fused_computation.95 | loop fusion | bytes 2097152 | tf_op jit(solution)/shard_map/slice | solution.py:122
  32.8 3.5 %collective-permute-done.1 = f32[128,256]{1,0:T(8,128)S(1)} collective-permute-done((f32[128,256]{1,0:T(8,128)}, f32[128,256]{1,0:T(8,128)S(1)}, u32[]{:S(2)}, u32[]{:S(2)}) %collective-permute-start.1) | collective-permute-done | bytes 131104 | tf_op jit(solution)/shard_map/ppermute | solution.py:21
  47.0 5.1 %fusion.15 = f32[512,256]{1,0:T(8,128)S(1)} fusion(bf16[2,512,256]{1,2,0:T(8,128)(2,1)} %collective-permute-done.7, bf16[8,512,256]{1,2,0:T(8,128)(2,1)S(1)} %copy.26, bf16[512,8,512]{2,1,0:T(8,128)(2,1)} %copy-done), kind=kOutput, calls=%fused_computation.26 | convolution fusion | flops 1074790400 | bytes 7340032 | tf_op jit(solution)/shard_map/dot_general | solution.py:138
  54.5 3.7 %fusion.12 = f32[512,256]{1,0:T(8,128)S(1)} fusion(bf16[8,512,256]{1,2,0:T(8,128)(2,1)S(1)} %copy.26, bf16[2,512,256]{1,2,0:T(8,128)(2,1)} %collective-permute-done.7, bf16[512,8,512]{2,1,0:T(8,128)(2,1)S(1)} %copy-done.1), kind=kOutput, calls=%fused_computation.25 | convolution fusion | flops 1074790400 | bytes 7340032 | tf_op jit(solution)/shard_map/dot_general | solution.py:138
  61.1 5.3 %collective-permute-start.13 = (bf16[128,256]{1,0:T(8,128)(2,1)S(1)}, bf16[128,256]{1,0:T(8,128)(2,1)S(1)}, u32[]{:S(2)}, u32[]{:S(2)}) collective-permute-start(bf16[128,256]{1,0:T(8,128)(2,1)S(1)} %multiply_convert_fusion.2), channel_id=1, source_target_pairs={{0,32},{1,24},{3,40},{2,16},{4,48},{5,8},{7,56},{6,0},{9,41},{8,33... | collective-permute-start | bytes 196616 | tf_op jit(solution)/shard_map/ppermute | solution.py:88
  66.6 7.9 %collective-permute-start.14 = (bf16[128,256]{1,0:T(8,128)(2,1)S(1)}, bf16[128,256]{1,0:T(8,128)(2,1)S(1)}, u32[]{:S(2)}, u32[]{:S(2)}) collective-permute-start(bf16[128,256]{1,0:T(8,128)(2,1)S(1)} %multiply_convert_fusion.2), channel_id=1, source_target_pairs={{192,32},{193,24},{195,40},{194,16},{196,48},{197,8},{199,56},{198... | collective-permute-start | bytes 196616 | tf_op jit(solution)/shard_map/ppermute | solution.py:88
  75.8 10.3 %collective-permute-done.15 = bf16[128,256]{1,0:T(8,128)(2,1)S(1)} collective-permute-done((bf16[128,256]{1,0:T(8,128)(2,1)S(1)}, bf16[128,256]{1,0:T(8,128)(2,1)S(1)}, u32[]{:S(2)}, u32[]{:S(2)}) %collective-permute-start.15) | collective-permute-done | bytes 65568 | tf_op jit(solution)/shard_map/ppermute | solution.py:88
  86.9 4.5 %collective-permute-done.17 = f32[128,256]{1,0:T(8,128)S(1)} collective-permute-done((f32[128,256]{1,0:T(8,128)S(1)}, f32[128,256]{1,0:T(8,128)S(1)}, u32[]{:S(2)}, u32[]{:S(2)}) %collective-permute-start.17) | collective-permute-done | bytes 131104 | tf_op jit(solution)/shard_map/ppermute | solution.py:21
  93.1 3.8 %collective-permute-done.18 = f32[128,256]{1,0:T(8,128)S(1)} collective-permute-done((f32[128,256]{1,0:T(8,128)S(1)}, f32[128,256]{1,0:T(8,128)S(1)}, u32[]{:S(2)}, u32[]{:S(2)}) %collective-permute-start.18) | collective-permute-done | bytes 131104 | tf_op jit(solution)/shard_map/ppermute | solution.py:21
  96.9 2.9 %collective-permute-start.19 = (f32[128,256]{1,0:T(8,128)S(1)}, f32[128,256]{1,0:T(8,128)S(1)}, u32[]{:S(2)}, u32[]{:S(2)}) collective-permute-start(f32[128,256]{1,0:T(8,128)S(1)} %add.233), channel_id=1, source_target_pairs={{0,4},{1,5},{2,6},{3,7},{4,0},{5,1},{6,2},{7,3},{8,12},{9,13},{10,... | collective-permute-start | bytes 393224 | tf_op jit(solution)/shard_map/ppermute | solution.py:21
  100.1 2.4 %collective-permute-done.19 = f32[128,256]{1,0:T(8,128)S(1)} collective-permute-done((f32[128,256]{1,0:T(8,128)S(1)}, f32[128,256]{1,0:T(8,128)S(1)}, u32[]{:S(2)}, u32[]{:S(2)}) %collective-permute-start.19) | collective-permute-done | bytes 131104 | tf_op jit(solution)/shard_map/ppermute | solution.py:21
  102.6 5.3 %collective-permute-start.22 = (bf16[128,256]{1,0:T(8,128)(2,1)S(1)}, bf16[128,256]{1,0:T(8,128)(2,1)S(1)}, u32[]{:S(2)}, u32[]{:S(2)}) collective-permute-start(bf16[128,256]{1,0:T(8,128)(2,1)S(1)} %multiply_convert_fusion.1), channel_id=1, source_target_pairs={{0,32},{1,24},{3,40},{2,16},{4,48},{5,8},{7,56},{6,0},{9,41},{8,33... | collective-permute-start | bytes 196616 | tf_op jit(solution)/shard_map/ppermute | solution.py:88
  107.9 11.0 %collective-permute-start.23 = (bf16[128,256]{1,0:T(8,128)(2,1)S(1)}, bf16[128,256]{1,0:T(8,128)(2,1)S(1)}, u32[]{:S(2)}, u32[]{:S(2)}) collective-permute-start(bf16[128,256]{1,0:T(8,128)(2,1)S(1)} %multiply_convert_fusion.1), channel_id=1, source_target_pairs={{192,32},{193,24},{195,40},{194,16},{196,48},{197,8},{199,56},{198... | collective-permute-start | bytes 196616 | tf_op jit(solution)/shard_map/ppermute | solution.py:88
  120.8 9.1 %collective-permute-done.24 = bf16[128,256]{1,0:T(8,128)(2,1)S(1)} collective-permute-done((bf16[128,256]{1,0:T(8,128)(2,1)S(1)}, bf16[128,256]{1,0:T(8,128)(2,1)S(1)}, u32[]{:S(2)}, u32[]{:S(2)}) %collective-permute-start.24) | collective-permute-done | bytes 65568 | tf_op jit(solution)/shard_map/ppermute | solution.py:88
  136.4 2.4 %collective-permute-start.20 = (bf16[128,256]{1,0:T(8,128)(2,1)S(1)}, bf16[128,256]{1,0:T(8,128)(2,1)S(1)}, u32[]{:S(2)}, u32[]{:S(2)}) collective-permute-start(bf16[128,256]{1,0:T(8,128)(2,1)S(1)} %multiply_convert_fusion.1), channel_id=1, source_target_pairs={{0,128},{64,192},{128,0},{192,64},{1,129},{65,193},{129,1},{193,65... | collective-permute-start | bytes 196616 | tf_op jit(solution)/shard_map/ppermute | solution.py:21
  138.8 2.8 %collective-permute-done.27 = f32[128,256]{1,0:T(8,128)S(1)} collective-permute-done((f32[128,256]{1,0:T(8,128)S(1)}, f32[128,256]{1,0:T(8,128)S(1)}, u32[]{:S(2)}, u32[]{:S(2)}) %collective-permute-start.27) | collective-permute-done | bytes 131104 | tf_op jit(solution)/shard_map/ppermute | solution.py:21
  141.6 2.3 %collective-permute-start.28 = (f32[128,256]{1,0:T(8,128)S(1)}, f32[128,256]{1,0:T(8,128)S(1)}, u32[]{:S(2)}, u32[]{:S(2)}) collective-permute-start(f32[128,256]{1,0:T(8,128)S(1)} %add.239), channel_id=1, source_target_pairs={{0,4},{1,5},{2,6},{3,7},{4,0},{5,1},{6,2},{7,3},{8,12},{9,13},{10,... | collective-permute-start | bytes 393224 | tf_op jit(solution)/shard_map/ppermute | solution.py:21
  143.9 3.1 %collective-permute-done.28 = f32[128,256]{1,0:T(8,128)S(1)} collective-permute-done((f32[128,256]{1,0:T(8,128)S(1)}, f32[128,256]{1,0:T(8,128)S(1)}, u32[]{:S(2)}, u32[]{:S(2)}) %collective-permute-start.28) | collective-permute-done | bytes 131104 | tf_op jit(solution)/shard_map/ppermute | solution.py:21
  147.1 2.4 %collective-permute-start.29 = (bf16[128,256]{1,0:T(8,128)(2,1)S(1)}, bf16[128,256]{1,0:T(8,128)(2,1)S(1)}, u32[]{:S(2)}, u32[]{:S(2)}) collective-permute-start(bf16[128,256]{1,0:T(8,128)(2,1)S(1)} %multiply_convert_fusion), channel_id=1, source_target_pairs={{0,128},{64,192},{128,0},{192,64},{1,129},{65,193},{129,1},{193,65... | collective-permute-start | bytes 196616 | tf_op jit(solution)/shard_map/ppermute | solution.py:21
  149.6 4.4 %collective-permute-start.21 = (bf16[256,256]{1,0:T(8,128)(2,1)S(1)}, bf16[256,256]{1,0:T(8,128)(2,1)S(1)}, u32[]{:S(2)}, u32[]{:S(2)}) collective-permute-start(bf16[256,256]{1,0:T(8,128)(2,1)S(1)} %pad_maximum_fusion.6), channel_id=1, source_target_pairs={{0,64},{64,0},{128,192},{192,128},{1,65},{65,1},{129,193},{193,129... | collective-permute-start | bytes 393224 | tf_op jit(solution)/shard_map/ppermute | solution.py:21
  154.1 4.2 %collective-permute-start.30 = (bf16[256,256]{1,0:T(8,128)(2,1)S(1)}, bf16[256,256]{1,0:T(8,128)(2,1)S(1)}, u32[]{:S(2)}, u32[]{:S(2)}) collective-permute-start(bf16[256,256]{1,0:T(8,128)(2,1)S(1)} %pad_maximum_fusion.7), channel_id=1, source_target_pairs={{0,64},{64,0},{128,192},{192,128},{1,65},{65,1},{129,193},{193,129... | collective-permute-start | bytes 393224 | tf_op jit(solution)/shard_map/ppermute | solution.py:21
  (120 shorter events, 44.4 us)
Async XLA Ops:
  3.7 43.3 %collective-permute-start.7 = (bf16[2,512,256]{1,2,0:T(8,128)(2,1)}, bf16[2,512,256]{1,2,0:T(8,128)(2,1)}, u32[]{:S(2)}, u32[]{:S(2)}) collective-permute-start(bf16[2,512,256]{1,2,0:T(8,128)(2,1)} %slice.57), channel_id=1, source_target_pairs={{0,64},{64,128},{128,192},{1,65},{65,129},{129,193},{2,66},{66,130... | collective-permute-start | bytes 1572872 | tf_op jit(solution)/shard_map/ppermute | solution.py:131
  18.4 11.0 %collective-permute-start = (f32[256,256]{1,0:T(8,128)S(1)}, f32[256,256]{1,0:T(8,128)}, u32[]{:S(2)}, u32[]{:S(2)}) collective-permute-start(f32[256,256]{1,0:T(8,128)S(1)} %constant_dynamic-slice_fusion.2), channel_id=1, source_target_pairs={{0,64},{64,0},{128,192},{192,128},{1,65},{65,1},{129,193},{193,129... | collective-permute-start | bytes 786440 | tf_op jit(solution)/shard_map/ppermute | solution.py:21
  37.2 8.0 %collective-permute-start.2 = (f32[128,256]{1,0:T(8,128)S(1)}, f32[128,256]{1,0:T(8,128)}, u32[]{:S(2)}, u32[]{:S(2)}) collective-permute-start(f32[128,256]{1,0:T(8,128)S(1)} %dynamic-slice_add_fusion.2), channel_id=1, source_target_pairs={{0,1},{1,0},{2,3},{3,2},{4,5},{5,4},{6,7},{7,6},{8,9},{9,8},{10,11... | collective-permute-start | bytes 393224 | tf_op jit(solution)/shard_map/ppermute | solution.py:21
  39.1 27.3 %collective-permute-start.10 = (bf16[2,128,512]{2,1,0:T(8,128)(2,1)}, bf16[2,128,512]{2,1,0:T(8,128)(2,1)S(1)}, u32[]{:S(2)}, u32[]{:S(2)}) collective-permute-start(bf16[2,128,512]{2,1,0:T(8,128)(2,1)} %get-tuple-element.12), channel_id=1, source_target_pairs={{0,192},{1,193},{2,194},{3,195},{4,196},{5,197},{6,198},{7,199},{8... | collective-permute-start | bytes 786440 | tf_op jit(solution)/shard_map/ppermute | solution.py:127
  40.4 26.0 %collective-permute-start.11 = (bf16[2,128,512]{2,1,0:T(8,128)(2,1)}, bf16[2,128,512]{2,1,0:T(8,128)(2,1)}, u32[]{:S(2)}, u32[]{:S(2)}) collective-permute-start(bf16[2,128,512]{2,1,0:T(8,128)(2,1)} %get-tuple-element.13), channel_id=1, source_target_pairs={{0,128},{1,129},{2,130},{3,131},{4,132},{5,133},{6,134},{7,135},{8... | collective-permute-start | bytes 786440 | tf_op jit(solution)/shard_map/ppermute | solution.py:127
  41.8 24.6 %collective-permute-start.12 = (bf16[2,128,512]{2,1,0:T(8,128)(2,1)}, bf16[2,128,512]{2,1,0:T(8,128)(2,1)}, u32[]{:S(2)}, u32[]{:S(2)}) collective-permute-start(bf16[2,128,512]{2,1,0:T(8,128)(2,1)} %get-tuple-element.11), channel_id=1, source_target_pairs={{0,64},{1,65},{2,66},{3,67},{4,68},{5,69},{6,70},{7,71},{8,72},{9,... | collective-permute-start | bytes 786440 | tf_op jit(solution)/shard_map/ppermute | solution.py:127
  46.2 6.2 %collective-permute-start.3 = (f32[128,256]{1,0:T(8,128)S(1)}, f32[128,256]{1,0:T(8,128)S(1)}, u32[]{:S(2)}, u32[]{:S(2)}) collective-permute-start(f32[128,256]{1,0:T(8,128)S(1)} %add.205), channel_id=1, source_target_pairs={{0,2},{1,3},{2,0},{3,1},{4,6},{5,7},{6,4},{7,5},{8,10},{9,11},{10,... | collective-permute-start | bytes 393224 | tf_op jit(solution)/shard_map/ppermute | solution.py:21
  52.4 7.7 %collective-permute-start.4 = (f32[128,256]{1,0:T(8,128)S(1)}, f32[128,256]{1,0:T(8,128)S(1)}, u32[]{:S(2)}, u32[]{:S(2)}) collective-permute-start(f32[128,256]{1,0:T(8,128)S(1)} %add.206), channel_id=1, source_target_pairs={{0,4},{1,5},{2,6},{3,7},{4,0},{5,1},{6,2},{7,3},{8,12},{9,13},{10,... | collective-permute-start | bytes 393224 | tf_op jit(solution)/shard_map/ppermute | solution.py:21
  58.3 17.0 %collective-permute-start.8 = (f32[256,512]{1,0:T(8,128)S(1)}, f32[256,512]{1,0:T(8,128)S(1)}, u32[]{:S(2)}, u32[]{:S(2)}) collective-permute-start(f32[256,512]{1,0:T(8,128)S(1)} %fusion.20), channel_id=1, source_target_pairs={{0,64},{64,0},{128,192},{192,128},{1,65},{65,1},{129,193},{193,129... | collective-permute-start | bytes 1572872 | tf_op jit(solution)/shard_map/ppermute | solution.py:21
  61.1 14.1 %collective-permute-start.13 = (bf16[128,256]{1,0:T(8,128)(2,1)S(1)}, bf16[128,256]{1,0:T(8,128)(2,1)S(1)}, u32[]{:S(2)}, u32[]{:S(2)}) collective-permute-start(bf16[128,256]{1,0:T(8,128)(2,1)S(1)} %multiply_convert_fusion.2), channel_id=1, source_target_pairs={{0,32},{1,24},{3,40},{2,16},{4,48},{5,8},{7,56},{6,0},{9,41},{8,33... | collective-permute-start | bytes 196616 | tf_op jit(solution)/shard_map/ppermute | solution.py:88
  66.6 9.3 %collective-permute-start.14 = (bf16[128,256]{1,0:T(8,128)(2,1)S(1)}, bf16[128,256]{1,0:T(8,128)(2,1)S(1)}, u32[]{:S(2)}, u32[]{:S(2)}) collective-permute-start(bf16[128,256]{1,0:T(8,128)(2,1)S(1)} %multiply_convert_fusion.2), channel_id=1, source_target_pairs={{192,32},{193,24},{195,40},{194,16},{196,48},{197,8},{199,56},{198... | collective-permute-start | bytes 196616 | tf_op jit(solution)/shard_map/ppermute | solution.py:88
  74.5 11.6 %collective-permute-start.15 = (bf16[128,256]{1,0:T(8,128)(2,1)S(1)}, bf16[128,256]{1,0:T(8,128)(2,1)S(1)}, u32[]{:S(2)}, u32[]{:S(2)}) collective-permute-start(bf16[128,256]{1,0:T(8,128)(2,1)S(1)} %multiply_convert_fusion.2), channel_id=1, source_target_pairs={{128,32},{129,24},{131,40},{130,16},{132,48},{133,8},{135,56},{134... | collective-permute-start | bytes 196616 | tf_op jit(solution)/shard_map/ppermute | solution.py:88
  74.5 12.0 %collective-permute-start.16 = (bf16[128,256]{1,0:T(8,128)(2,1)S(1)}, bf16[128,256]{1,0:T(8,128)(2,1)S(1)}, u32[]{:S(2)}, u32[]{:S(2)}) collective-permute-start(bf16[128,256]{1,0:T(8,128)(2,1)S(1)} %multiply_convert_fusion.2), channel_id=1, source_target_pairs={{64,32},{65,24},{67,40},{66,16},{68,48},{69,8},{71,56},{70,0},{73,... | collective-permute-start | bytes 196616 | tf_op jit(solution)/shard_map/ppermute | solution.py:88
  75.4 11.1 %collective-permute-start.9 = (f32[128,512]{1,0:T(8,128)S(1)}, f32[128,512]{1,0:T(8,128)S(1)}, u32[]{:S(2)}, u32[]{:S(2)}) collective-permute-start(f32[128,512]{1,0:T(8,128)S(1)} %constant_dynamic-slice_fusion), channel_id=1, source_target_pairs={{0,128},{64,192},{128,0},{192,64},{1,129},{65,193},{129,1},{193,65... | collective-permute-start | bytes 786440 | tf_op jit(solution)/shard_map/ppermute | solution.py:21
  91.4 5.4 %collective-permute-start.18 = (f32[128,256]{1,0:T(8,128)S(1)}, f32[128,256]{1,0:T(8,128)S(1)}, u32[]{:S(2)}, u32[]{:S(2)}) collective-permute-start(f32[128,256]{1,0:T(8,128)S(1)} %add.232), channel_id=1, source_target_pairs={{0,2},{1,3},{2,0},{3,1},{4,6},{5,7},{6,4},{7,5},{8,10},{9,11},{10,... | collective-permute-start | bytes 393224 | tf_op jit(solution)/shard_map/ppermute | solution.py:21
  96.9 5.6 %collective-permute-start.19 = (f32[128,256]{1,0:T(8,128)S(1)}, f32[128,256]{1,0:T(8,128)S(1)}, u32[]{:S(2)}, u32[]{:S(2)}) collective-permute-start(f32[128,256]{1,0:T(8,128)S(1)} %add.233), channel_id=1, source_target_pairs={{0,4},{1,5},{2,6},{3,7},{4,0},{5,1},{6,2},{7,3},{8,12},{9,13},{10,... | collective-permute-start | bytes 393224 | tf_op jit(solution)/shard_map/ppermute | solution.py:21
  99.8 8.1 %collective-permute-start.5 = (bf16[128,256]{1,0:T(8,128)(2,1)S(1)}, bf16[128,256]{1,0:T(8,128)(2,1)S(1)}, u32[]{:S(2)}, u32[]{:S(2)}) collective-permute-start(bf16[128,256]{1,0:T(8,128)(2,1)S(1)} %multiply_convert_fusion.2), channel_id=1, source_target_pairs={{0,128},{64,192},{128,0},{192,64},{1,129},{65,193},{129,1},{193,65... | collective-permute-start | bytes 196616 | tf_op jit(solution)/shard_map/ppermute | solution.py:21
  102.6 18.2 %collective-permute-start.22 = (bf16[128,256]{1,0:T(8,128)(2,1)S(1)}, bf16[128,256]{1,0:T(8,128)(2,1)S(1)}, u32[]{:S(2)}, u32[]{:S(2)}) collective-permute-start(bf16[128,256]{1,0:T(8,128)(2,1)S(1)} %multiply_convert_fusion.1), channel_id=1, source_target_pairs={{0,32},{1,24},{3,40},{2,16},{4,48},{5,8},{7,56},{6,0},{9,41},{8,33... | collective-permute-start | bytes 196616 | tf_op jit(solution)/shard_map/ppermute | solution.py:88
  107.9 12.9 %collective-permute-start.23 = (bf16[128,256]{1,0:T(8,128)(2,1)S(1)}, bf16[128,256]{1,0:T(8,128)(2,1)S(1)}, u32[]{:S(2)}, u32[]{:S(2)}) collective-permute-start(bf16[128,256]{1,0:T(8,128)(2,1)S(1)} %multiply_convert_fusion.1), channel_id=1, source_target_pairs={{192,32},{193,24},{195,40},{194,16},{196,48},{197,8},{199,56},{198... | collective-permute-start | bytes 196616 | tf_op jit(solution)/shard_map/ppermute | solution.py:88
  118.9 11.1 %collective-permute-start.24 = (bf16[128,256]{1,0:T(8,128)(2,1)S(1)}, bf16[128,256]{1,0:T(8,128)(2,1)S(1)}, u32[]{:S(2)}, u32[]{:S(2)}) collective-permute-start(bf16[128,256]{1,0:T(8,128)(2,1)S(1)} %multiply_convert_fusion.1), channel_id=1, source_target_pairs={{128,32},{129,24},{131,40},{130,16},{132,48},{133,8},{135,56},{134... | collective-permute-start | bytes 196616 | tf_op jit(solution)/shard_map/ppermute | solution.py:88
  120.8 11.1 %collective-permute-start.25 = (bf16[128,256]{1,0:T(8,128)(2,1)S(1)}, bf16[128,256]{1,0:T(8,128)(2,1)S(1)}, u32[]{:S(2)}, u32[]{:S(2)}) collective-permute-start(bf16[128,256]{1,0:T(8,128)(2,1)S(1)} %multiply_convert_fusion.1), channel_id=1, source_target_pairs={{64,32},{65,24},{67,40},{66,16},{68,48},{69,8},{71,56},{70,0},{73,... | collective-permute-start | bytes 196616 | tf_op jit(solution)/shard_map/ppermute | solution.py:88
  136.4 7.5 %collective-permute-start.20 = (bf16[128,256]{1,0:T(8,128)(2,1)S(1)}, bf16[128,256]{1,0:T(8,128)(2,1)S(1)}, u32[]{:S(2)}, u32[]{:S(2)}) collective-permute-start(bf16[128,256]{1,0:T(8,128)(2,1)S(1)} %multiply_convert_fusion.1), channel_id=1, source_target_pairs={{0,128},{64,192},{128,0},{192,64},{1,129},{65,193},{129,1},{193,65... | collective-permute-start | bytes 196616 | tf_op jit(solution)/shard_map/ppermute | solution.py:21
  147.1 6.9 %collective-permute-start.29 = (bf16[128,256]{1,0:T(8,128)(2,1)S(1)}, bf16[128,256]{1,0:T(8,128)(2,1)S(1)}, u32[]{:S(2)}, u32[]{:S(2)}) collective-permute-start(bf16[128,256]{1,0:T(8,128)(2,1)S(1)} %multiply_convert_fusion), channel_id=1, source_target_pairs={{0,128},{64,192},{128,0},{192,64},{1,129},{65,193},{129,1},{193,65... | collective-permute-start | bytes 196616 | tf_op jit(solution)/shard_map/ppermute | solution.py:21
  149.6 8.6 %collective-permute-start.21 = (bf16[256,256]{1,0:T(8,128)(2,1)S(1)}, bf16[256,256]{1,0:T(8,128)(2,1)S(1)}, u32[]{:S(2)}, u32[]{:S(2)}) collective-permute-start(bf16[256,256]{1,0:T(8,128)(2,1)S(1)} %pad_maximum_fusion.6), channel_id=1, source_target_pairs={{0,64},{64,0},{128,192},{192,128},{1,65},{65,1},{129,193},{193,129... | collective-permute-start | bytes 393224 | tf_op jit(solution)/shard_map/ppermute | solution.py:21
  (16 other events, 121.0 us)

commit v9 on v5

--- a/solution.py
+++ b/solution.py
@@ -45,13 +45,13 @@
     return x
 
 
-def all_gather_lag(y):
+def all_gather_lag(y, axis=0):
     for mask in reversed(bit_masks("lag")):
         bit = (lax.axis_index("lag") // mask) % 2
         other = swap(y, "lag", mask)
         first = jnp.where(bit == 0, y, other)
         second = jnp.where(bit == 0, other, y)
-        y = jnp.concatenate([first, second], axis=0)
+        y = jnp.concatenate([first, second], axis=axis)
     return y
 
 
@@ -142,8 +142,8 @@
         if step_index + 1 < STEPS:
             block = all_gather_lag(transposed(rates_chunk))
             sources.append(block)
-        outputs.append(all_gather_lag(rates_chunk))
-    return jnp.stack(outputs)
+        outputs.append(rates_chunk)
+    return all_gather_lag(jnp.stack(outputs), axis=1)
 
 
 def solution(mesh):

time: 143 us -> 144 us (level)
  waiting for transfers between devices: 57.3 us -> 65.5 us
  starting transfers between devices: 41.1 us -> 34 us
    ppermute x23 -> x19, waiting for transfers between devices: 39.2 us -> 47.8 us  [swap(): return lax.ppermute(block, axis, [(i, i ^ mask) for i in range(size)])]
    ppermute x23 -> x19, starting transfers between devices: 34.5 us -> 27.4 us  [swap(): return lax.ppermute(block, axis, [(i, i ^ mask) for i in range(size)])]
    unnamed x19 -> x29, local copies, waits for them, and re-layouts: 2.91 us -> 2.93 us
  transfers between devices with their start and end apart: 29 -> 25, of which waited for: 14 -> 14; matrix products, arithmetic and copies ran while one was open for 20% -> 20% of each run, Pallas kernels for 0% -> 0%
where the time goes in v9:
time: 144 us; the launch traced here: 143 us
  waiting for transfers between devices  65.5 us (45%)
  starting transfers between devices  34 us (24%)
  other arithmetic  17.6 us (12%)
  local copies, waits for them, and re-layouts  13.2 us (9%)
  matrix products  11.9 us (8%)
    ppermute x19, waiting for transfers between devices, swap(): return lax.ppermute(block, axis, [(i, i ^ mask) for i in range(size)])  47.8 us
    ppermute x19, starting transfers between devices, swap(): return lax.ppermute(block, axis, [(i, i ^ mask) for i in range(size)])  27.4 us
    ppermute x2, waiting for transfers between devices, transposed(): return lax.ppermute(chunk, ('recv', 'src'), route)  17.6 us
    dot_general x2, matrix products, local(): jnp.dot(masked_rows, shifted.reshape(lag_here * cols_here, scenarios), pr...  8.9 us
    select_n x1, other arithmetic, local(): jnp.where(allowed, kernel, jnp.zeros_like(kernel))  8.71 us
    slice x1, local copies, waits for them, and re-layouts, local(): kernel[:, lag_index, :]  4.91 us
    ppermute x3, starting transfers between devices, local(): lax.ppermute(serial[:, start:start + chunk_rows], 'lag', [(0, target)])  3.31 us
    broadcast_in_dim x2, local copies, waits for them, and re-layouts, local(): jnp.repeat(jnp.repeat(causal_mask[:, lag_index, :], block_size, 0), block...  3.2 us
  transfers between devices with their start and end apart: 25, of which 14 were waited for; matrix products, arithmetic and copies ran while one was open for 20% of the time, Pallas kernels for 0%

profile of v9, /device:TPU:225, one launch (start us, length us, event | category | flops | bytes accessed | tf_op | source)
XLA Modules:
  0.0 142.8 jit_solution(11509640437275591627)
XLA Ops:
  0.9 8.7 %bitcast_select_fusion = bf16[512,8,512]{2,1,0:T(8,128)(2,1)S(1)} fusion(bf16[512,8,512]{2,1,0:T(8,128)(2,1)} %param.7, pred[512,8,4]{1,2,0:T(4,128)(4,1)S(1)} %bitcast.35), kind=kLoop, calls=%fused_computation | loop fusion | flops 2097152 | bytes 8404992 | tf_op jit(solution)/shard_map/jit(_where)/select_n | solution.py:98
  9.6 2.4 %fusion.9 = f32[512,256]{1,0:T(8,128)S(1)} fusion(bf16[8,512,256]{2,1,0:T(8,128)(2,1)S(1)} %copy-done.8, bf16[512,8,512]{2,1,0:T(8,128)(2,1)S(1)} %bitcast_select_fusion), kind=kOutput, calls=%fused_computation.24 | convolution fusion | flops 1073741824 | bytes 6815744 | tf_op jit(solution)/shard_map/dot_general | solution.py:121
  12.8 2.9 %copy.26 = bf16[8,512,256]{1,2,0:T(8,128)(2,1)S(1)} copy(bf16[8,512,256]{2,1,0:T(8,128)(2,1)} %param.9) | data formatting | bytes 4194304 | tf_op args[2]
  15.7 3.1 %collective-permute-start.5 = (bf16[2,512,256]{1,2,0:T(8,128)(2,1)S(1)}, bf16[2,512,256]{1,2,0:T(8,128)(2,1)}, u32[]{:S(2)}, u32[]{:S(2)}) collective-permute-start(bf16[2,512,256]{1,2,0:T(8,128)(2,1)S(1)} %slice.57), channel_id=1, source_target_pairs={{0,64},{64,128},{128,192},{1,65},{65,129},{129,193},{2,66},{66,130... | collective-permute-start | bytes 1572872 | tf_op jit(solution)/shard_map/ppermute | solution.py:119
  20.1 4.9 %fusion.47 = (bf16[512,1,512]{2,1,0:T(2,128)(2,1)S(1)}, bf16[512,1,512]{2,1,0:T(2,128)(2,1)S(1)}) fusion(bf16[512,8,512]{2,1,0:T(8,128)(2,1)} %param.7), kind=kLoop, calls=%fused_computation.93 | loop fusion | bytes 2097152 | tf_op jit(solution)/shard_map/slice | solution.py:110
  25.0 2.8 %collective-permute-done.1 = f32[128,256]{1,0:T(8,128)S(1)} collective-permute-done((f32[128,256]{1,0:T(8,128)S(1)}, f32[128,256]{1,0:T(8,128)S(1)}, u32[]{:S(2)}, u32[]{:S(2)}) %collective-permute-start.1) | collective-permute-done | bytes 131104 | tf_op jit(solution)/shard_map/ppermute | solution.py:21
  34.7 2.5 %collective-permute-start.3 = (f32[128,256]{1,0:T(8,128)S(1)}, f32[128,256]{1,0:T(8,128)S(1)}, u32[]{:S(2)}, u32[]{:S(2)}) collective-permute-start(f32[128,256]{1,0:T(8,128)S(1)} %add.114), channel_id=1, source_target_pairs={{0,2},{1,3},{2,0},{3,1},{4,6},{5,7},{6,4},{7,5},{8,10},{9,11},{10,... | collective-permute-start | bytes 393224 | tf_op jit(solution)/shard_map/ppermute | solution.py:21
  37.3 5.3 %fusion.15 = f32[512,256]{1,0:T(8,128)S(1)} fusion(bf16[2,512,256]{1,2,0:T(8,128)(2,1)} %collective-permute-done.5, bf16[8,512,256]{1,2,0:T(8,128)(2,1)} %copy-done.2, bf16[512,8,512]{2,1,0:T(8,128)(2,1)} %copy-done), kind=kOutput, calls=%fused_computation.26 | convolution fusion | flops 1074790400 | bytes 7340032 | tf_op jit(solution)/shard_map/dot_general | solution.py:126
  42.6 2.9 %collective-permute-start.4 = (f32[128,256]{1,0:T(8,128)S(1)}, f32[128,256]{1,0:T(8,128)S(1)}, u32[]{:S(2)}, u32[]{:S(2)}) collective-permute-start(f32[128,256]{1,0:T(8,128)S(1)} %add.115), channel_id=1, source_target_pairs={{0,4},{1,5},{2,6},{3,7},{4,0},{5,1},{6,2},{7,3},{8,12},{9,13},{10,... | collective-permute-start | bytes 393224 | tf_op jit(solution)/shard_map/ppermute | solution.py:21
  45.5 3.6 %fusion.12 = f32[512,256]{1,0:T(8,128)S(1)} fusion(bf16[8,512,256]{1,2,0:T(8,128)(2,1)S(1)} %copy-done.3, bf16[2,512,256]{1,2,0:T(8,128)(2,1)} %collective-permute-done.5, bf16[512,8,512]{2,1,0:T(8,128)(2,1)S(1)} %copy-done.1), kind=kOutput, calls=%fused_computation.25 | convolution fusion | flops 1074790400 | bytes 7340032 | tf_op jit(solution)/shard_map/dot_general | solution.py:126
  51.4 8.8 %collective-permute-done.11 = bf16[128,256]{1,0:T(8,128)(2,1)S(1)} collective-permute-done((bf16[128,256]{1,0:T(8,128)(2,1)S(1)}, bf16[128,256]{1,0:T(8,128)(2,1)S(1)}, u32[]{:S(2)}, u32[]{:S(2)}) %collective-permute-start.11) | collective-permute-done | bytes 65568 | tf_op jit(solution)/shard_map/ppermute | solution.py:79
  65.7 4.4 %collective-permute-start.13 = (bf16[256,256]{1,0:T(8,128)(2,1)S(1)}, bf16[256,256]{1,0:T(8,128)(2,1)S(1)}, u32[]{:S(2)}, u32[]{:S(2)}) collective-permute-start(bf16[256,256]{1,0:T(8,128)(2,1)S(1)} %pad_maximum_fusion.10), channel_id=1, source_target_pairs={{0,64},{64,0},{128,192},{192,128},{1,65},{65,1},{129,193},{193,129... | collective-permute-start | bytes 393224 | tf_op jit(solution)/shard_map/ppermute | solution.py:21
  72.5 6.6 %collective-permute-done.7 = f32[128,512]{1,0:T(8,128)S(1)} collective-permute-done((f32[128,512]{1,0:T(8,128)S(1)}, f32[128,512]{1,0:T(8,128)S(1)}, u32[]{:S(2)}, u32[]{:S(2)}) %collective-permute-start.7) | collective-permute-done | bytes 262176 | tf_op jit(solution)/shard_map/ppermute | solution.py:21
  79.5 4.2 %collective-permute-done.14 = f32[128,256]{1,0:T(8,128)S(1)} collective-permute-done((f32[128,256]{1,0:T(8,128)S(1)}, f32[128,256]{1,0:T(8,128)S(1)}, u32[]{:S(2)}, u32[]{:S(2)}) %collective-permute-start.14) | collective-permute-done | bytes 131104 | tf_op jit(solution)/shard_map/ppermute | solution.py:21
  83.8 5.2 %collective-permute-done.15 = f32[128,256]{1,0:T(8,128)S(1)} collective-permute-done((f32[128,256]{1,0:T(8,128)S(1)}, f32[128,256]{1,0:T(8,128)S(1)}, u32[]{:S(2)}, u32[]{:S(2)}) %collective-permute-start.15) | collective-permute-done | bytes 131104 | tf_op jit(solution)/shard_map/ppermute | solution.py:21
  89.9 4.6 %collective-permute-done.16 = f32[128,256]{1,0:T(8,128)S(1)} collective-permute-done((f32[128,256]{1,0:T(8,128)S(1)}, f32[128,256]{1,0:T(8,128)S(1)}, u32[]{:S(2)}, u32[]{:S(2)}) %collective-permute-start.16) | collective-permute-done | bytes 131104 | tf_op jit(solution)/shard_map/ppermute | solution.py:21
  94.7 8.8 %collective-permute-done.17 = bf16[128,256]{1,0:T(8,128)(2,1)S(1)} collective-permute-done((bf16[128,256]{1,0:T(8,128)(2,1)S(1)}, bf16[128,256]{1,0:T(8,128)(2,1)S(1)}, u32[]{:S(2)}, u32[]{:S(2)}) %collective-permute-start.17) | collective-permute-done | bytes 65568 | tf_op jit(solution)/shard_map/ppermute | solution.py:79
  104.3 2.7 %collective-permute-done.18 = bf16[128,256]{1,0:T(8,128)(2,1)S(1)} collective-permute-done((bf16[128,256]{1,0:T(8,128)(2,1)S(1)}, bf16[128,256]{1,0:T(8,128)(2,1)S(1)}, u32[]{:S(2)}, u32[]{:S(2)}) %collective-permute-start.18) | collective-permute-done | bytes 65568 | tf_op jit(solution)/shard_map/ppermute | solution.py:21
  107.0 6.1 %collective-permute-start.19 = (bf16[256,256]{1,0:T(8,128)(2,1)S(1)}, bf16[256,256]{1,0:T(8,128)(2,1)S(1)}, u32[]{:S(2)}, u32[]{:S(2)}) collective-permute-start(bf16[256,256]{1,0:T(8,128)(2,1)S(1)} %pad_maximum_fusion.11), channel_id=1, source_target_pairs={{0,64},{64,0},{128,192},{192,128},{1,65},{65,1},{129,193},{193,129... | collective-permute-start | bytes 393224 | tf_op jit(solution)/shard_map/ppermute | solution.py:21
  114.7 4.7 %collective-permute-done.20 = f32[128,256]{1,0:T(8,128)S(1)} collective-permute-done((f32[128,256]{1,0:T(8,128)S(1)}, f32[128,256]{1,0:T(8,128)S(1)}, u32[]{:S(2)}, u32[]{:S(2)}) %collective-permute-start.20) | collective-permute-done | bytes 131104 | tf_op jit(solution)/shard_map/ppermute | solution.py:21
  119.5 5.3 %collective-permute-done.21 = f32[128,256]{1,0:T(8,128)S(1)} collective-permute-done((f32[128,256]{1,0:T(8,128)S(1)}, f32[128,256]{1,0:T(8,128)S(1)}, u32[]{:S(2)}, u32[]{:S(2)}) %collective-permute-start.21) | collective-permute-done | bytes 131104 | tf_op jit(solution)/shard_map/ppermute | solution.py:21
  124.9 5.3 %collective-permute-done.22 = f32[128,256]{1,0:T(8,128)S(1)} collective-permute-done((f32[128,256]{1,0:T(8,128)S(1)}, f32[128,256]{1,0:T(8,128)S(1)}, u32[]{:S(2)}, u32[]{:S(2)}) %collective-permute-start.22) | collective-permute-done | bytes 131104 | tf_op jit(solution)/shard_map/ppermute | solution.py:21
  130.8 4.1 %collective-permute-done.23 = bf16[3,128,256]{2,1,0:T(8,128)(2,1)S(1)} collective-permute-done((bf16[3,128,256]{2,1,0:T(8,128)(2,1)S(1)}, bf16[3,128,256]{2,1,0:T(8,128)(2,1)S(1)}, u32[]{:S(2)}, u32[]{:S(2)}) %collective-permute-start.23) | collective-permute-done | bytes 196640 | tf_op jit(solution)/shard_map/ppermute | solution.py:21
  135.0 5.4 %collective-permute-start.24 = (bf16[3,256,256]{2,1,0:T(8,128)(2,1)S(1)}, bf16[3,256,256]{2,1,0:T(8,128)(2,1)S(1)}, u32[]{:S(2)}, u32[]{:S(2)}) collective-permute-start(bf16[3,256,256]{2,1,0:T(8,128)(2,1)S(1)} %pad_maximum_fusion.5), channel_id=1, source_target_pairs={{0,64},{64,0},{128,192},{192,128},{1,65},{65,1},{129,193},{193,129... | collective-permute-start | bytes 1179656 | tf_op jit(solution)/shard_map/ppermute | solution.py:21
  (106 shorter events, 26.8 us)
Async XLA Ops:
  12.1 6.9 %collective-permute-start = (f32[256,256]{1,0:T(8,128)S(1)}, f32[256,256]{1,0:T(8,128)}, u32[]{:S(2)}, u32[]{:S(2)}) collective-permute-start(f32[256,256]{1,0:T(8,128)S(1)} %constant_dynamic-slice_fusion.2), channel_id=1, source_target_pairs={{0,64},{64,0},{128,192},{192,128},{1,65},{65,1},{129,193},{193,129... | collective-permute-start | bytes 786440 | tf_op jit(solution)/shard_map/ppermute | solution.py:21
  15.7 21.5 %collective-permute-start.5 = (bf16[2,512,256]{1,2,0:T(8,128)(2,1)S(1)}, bf16[2,512,256]{1,2,0:T(8,128)(2,1)}, u32[]{:S(2)}, u32[]{:S(2)}) collective-permute-start(bf16[2,512,256]{1,2,0:T(8,128)(2,1)S(1)} %slice.57), channel_id=1, source_target_pairs={{0,64},{64,128},{128,192},{1,65},{65,129},{129,193},{2,66},{66,130... | collective-permute-start | bytes 1572872 | tf_op jit(solution)/shard_map/ppermute | solution.py:119
  20.0 7.8 %collective-permute-start.1 = (f32[128,256]{1,0:T(8,128)S(1)}, f32[128,256]{1,0:T(8,128)S(1)}, u32[]{:S(2)}, u32[]{:S(2)}) collective-permute-start(f32[128,256]{1,0:T(8,128)S(1)} %constant_dynamic-slice_fusion.1), channel_id=1, source_target_pairs={{0,128},{64,192},{128,0},{192,64},{1,129},{65,193},{129,1},{193,65... | collective-permute-start | bytes 393224 | tf_op jit(solution)/shard_map/ppermute | solution.py:21
  27.8 6.9 %collective-permute-start.2 = (f32[128,256]{1,0:T(8,128)S(1)}, f32[128,256]{1,0:T(8,128)S(1)}, u32[]{:S(2)}, u32[]{:S(2)}) collective-permute-start(f32[128,256]{1,0:T(8,128)S(1)} %dynamic-slice_add_fusion.2), channel_id=1, source_target_pairs={{0,1},{1,0},{2,3},{3,2},{4,5},{5,4},{6,7},{7,6},{8,9},{9,8},{10,11... | collective-permute-start | bytes 393224 | tf_op jit(solution)/shard_map/ppermute | solution.py:21
  34.7 7.9 %collective-permute-start.3 = (f32[128,256]{1,0:T(8,128)S(1)}, f32[128,256]{1,0:T(8,128)S(1)}, u32[]{:S(2)}, u32[]{:S(2)}) collective-permute-start(f32[128,256]{1,0:T(8,128)S(1)} %add.114), channel_id=1, source_target_pairs={{0,2},{1,3},{2,0},{3,1},{4,6},{5,7},{6,4},{7,5},{8,10},{9,11},{10,... | collective-permute-start | bytes 393224 | tf_op jit(solution)/shard_map/ppermute | solution.py:21
  42.6 7.4 %collective-permute-start.4 = (f32[128,256]{1,0:T(8,128)S(1)}, f32[128,256]{1,0:T(8,128)S(1)}, u32[]{:S(2)}, u32[]{:S(2)}) collective-permute-start(f32[128,256]{1,0:T(8,128)S(1)} %add.115), channel_id=1, source_target_pairs={{0,4},{1,5},{2,6},{3,7},{4,0},{5,1},{6,2},{7,3},{8,12},{9,13},{10,... | collective-permute-start | bytes 393224 | tf_op jit(solution)/shard_map/ppermute | solution.py:21
  50.0 20.0 %collective-permute-start.6 = (f32[256,512]{1,0:T(8,128)}, f32[256,512]{1,0:T(8,128)}, u32[]{:S(2)}, u32[]{:S(2)}) collective-permute-start(f32[256,512]{1,0:T(8,128)} %fusion.20), channel_id=1, source_target_pairs={{0,64},{64,0},{128,192},{192,128},{1,65},{65,1},{129,193},{193,129... | collective-permute-start | bytes 1572872 | tf_op jit(solution)/shard_map/ppermute | solution.py:21
  51.0 9.2 %collective-permute-start.11 = (bf16[128,256]{1,0:T(8,128)(2,1)S(1)}, bf16[128,256]{1,0:T(8,128)(2,1)S(1)}, u32[]{:S(2)}, u32[]{:S(2)}) collective-permute-start(bf16[128,256]{1,0:T(8,128)(2,1)S(1)} %multiply_convert_fusion.2), channel_id=1, source_target_pairs={{0,32},{1,24},{3,40},{2,16},{4,48},{5,8},{7,56},{6,0},{9,41},{8,33... | collective-permute-start | bytes 196616 | tf_op jit(solution)/shard_map/ppermute | solution.py:79
  60.2 5.4 %collective-permute-start.12 = (bf16[128,256]{1,0:T(8,128)(2,1)S(1)}, bf16[128,256]{1,0:T(8,128)(2,1)S(1)}, u32[]{:S(2)}, u32[]{:S(2)}) collective-permute-start(bf16[128,256]{1,0:T(8,128)(2,1)S(1)} %collective-permute-done.11), channel_id=1, source_target_pairs={{0,128},{64,192},{128,0},{192,64},{1,129},{65,193},{129,1},{193,65... | collective-permute-start | bytes 196616 | tf_op jit(solution)/shard_map/ppermute | solution.py:21
  62.3 9.1 %collective-permute-start.8 = (bf16[2,128,512]{2,1,0:T(8,128)(2,1)}, bf16[2,128,512]{2,1,0:T(8,128)(2,1)S(1)}, u32[]{:S(2)}, u32[]{:S(2)}) collective-permute-start(bf16[2,128,512]{2,1,0:T(8,128)(2,1)} %get-tuple-element.12), channel_id=1, source_target_pairs={{0,192},{1,193},{2,194},{3,195},{4,196},{5,197},{6,198},{7,199},{8... | collective-permute-start | bytes 786440 | tf_op jit(solution)/shard_map/ppermute | solution.py:115
  62.9 8.4 %collective-permute-start.9 = (bf16[2,128,512]{2,1,0:T(8,128)(2,1)}, bf16[2,128,512]{2,1,0:T(8,128)(2,1)}, u32[]{:S(2)}, u32[]{:S(2)}) collective-permute-start(bf16[2,128,512]{2,1,0:T(8,128)(2,1)} %get-tuple-element.13), channel_id=1, source_target_pairs={{0,128},{1,129},{2,130},{3,131},{4,132},{5,133},{6,134},{7,135},{8... | collective-permute-start | bytes 786440 | tf_op jit(solution)/shard_map/ppermute | solution.py:115
  64.3 7.1 %collective-permute-start.10 = (bf16[2,128,512]{2,1,0:T(8,128)(2,1)S(1)}, bf16[2,128,512]{2,1,0:T(8,128)(2,1)}, u32[]{:S(2)}, u32[]{:S(2)}) collective-permute-start(bf16[2,128,512]{2,1,0:T(8,128)(2,1)S(1)} %get-tuple-element.11), channel_id=1, source_target_pairs={{0,64},{1,65},{2,66},{3,67},{4,68},{5,69},{6,70},{7,71},{8,72},{9,... | collective-permute-start | bytes 786440 | tf_op jit(solution)/shard_map/ppermute | solution.py:115
  65.7 6.8 %collective-permute-start.13 = (bf16[256,256]{1,0:T(8,128)(2,1)S(1)}, bf16[256,256]{1,0:T(8,128)(2,1)S(1)}, u32[]{:S(2)}, u32[]{:S(2)}) collective-permute-start(bf16[256,256]{1,0:T(8,128)(2,1)S(1)} %pad_maximum_fusion.10), channel_id=1, source_target_pairs={{0,64},{64,0},{128,192},{192,128},{1,65},{65,1},{129,193},{193,129... | collective-permute-start | bytes 393224 | tf_op jit(solution)/shard_map/ppermute | solution.py:21
  71.2 7.9 %collective-permute-start.7 = (f32[128,512]{1,0:T(8,128)S(1)}, f32[128,512]{1,0:T(8,128)S(1)}, u32[]{:S(2)}, u32[]{:S(2)}) collective-permute-start(f32[128,512]{1,0:T(8,128)S(1)} %constant_dynamic-slice_fusion), channel_id=1, source_target_pairs={{0,128},{64,192},{128,0},{192,64},{1,129},{65,193},{129,1},{193,65... | collective-permute-start | bytes 786440 | tf_op jit(solution)/shard_map/ppermute | solution.py:21
  79.4 4.3 %collective-permute-start.14 = (f32[128,256]{1,0:T(8,128)S(1)}, f32[128,256]{1,0:T(8,128)S(1)}, u32[]{:S(2)}, u32[]{:S(2)}) collective-permute-start(f32[128,256]{1,0:T(8,128)S(1)} %slice_add_fusion.1), channel_id=1, source_target_pairs={{0,1},{1,0},{2,3},{3,2},{4,5},{5,4},{6,7},{7,6},{8,9},{9,8},{10,11... | collective-permute-start | bytes 393224 | tf_op jit(solution)/shard_map/ppermute | solution.py:21
  83.7 5.4 %collective-permute-start.15 = (f32[128,256]{1,0:T(8,128)S(1)}, f32[128,256]{1,0:T(8,128)S(1)}, u32[]{:S(2)}, u32[]{:S(2)}) collective-permute-start(f32[128,256]{1,0:T(8,128)S(1)} %add.121), channel_id=1, source_target_pairs={{0,2},{1,3},{2,0},{3,1},{4,6},{5,7},{6,4},{7,5},{8,10},{9,11},{10,... | collective-permute-start | bytes 393224 | tf_op jit(solution)/shard_map/ppermute | solution.py:21
  89.1 5.4 %collective-permute-start.16 = (f32[128,256]{1,0:T(8,128)S(1)}, f32[128,256]{1,0:T(8,128)S(1)}, u32[]{:S(2)}, u32[]{:S(2)}) collective-permute-start(f32[128,256]{1,0:T(8,128)S(1)} %add.122), channel_id=1, source_target_pairs={{0,4},{1,5},{2,6},{3,7},{4,0},{5,1},{6,2},{7,3},{8,12},{9,13},{10,... | collective-permute-start | bytes 393224 | tf_op jit(solution)/shard_map/ppermute | solution.py:21
  94.6 8.9 %collective-permute-start.17 = (bf16[128,256]{1,0:T(8,128)(2,1)S(1)}, bf16[128,256]{1,0:T(8,128)(2,1)S(1)}, u32[]{:S(2)}, u32[]{:S(2)}) collective-permute-start(bf16[128,256]{1,0:T(8,128)(2,1)S(1)} %multiply_convert_fusion.1), channel_id=1, source_target_pairs={{0,32},{1,24},{3,40},{2,16},{4,48},{5,8},{7,56},{6,0},{9,41},{8,33... | collective-permute-start | bytes 196616 | tf_op jit(solution)/shard_map/ppermute | solution.py:79
  107.0 7.1 %collective-permute-start.19 = (bf16[256,256]{1,0:T(8,128)(2,1)S(1)}, bf16[256,256]{1,0:T(8,128)(2,1)S(1)}, u32[]{:S(2)}, u32[]{:S(2)}) collective-permute-start(bf16[256,256]{1,0:T(8,128)(2,1)S(1)} %pad_maximum_fusion.11), channel_id=1, source_target_pairs={{0,64},{64,0},{128,192},{192,128},{1,65},{65,1},{129,193},{193,129... | collective-permute-start | bytes 393224 | tf_op jit(solution)/shard_map/ppermute | solution.py:21
  114.6 4.8 %collective-permute-start.20 = (f32[128,256]{1,0:T(8,128)S(1)}, f32[128,256]{1,0:T(8,128)S(1)}, u32[]{:S(2)}, u32[]{:S(2)}) collective-permute-start(f32[128,256]{1,0:T(8,128)S(1)} %fusion.38), channel_id=1, source_target_pairs={{0,1},{1,0},{2,3},{3,2},{4,5},{5,4},{6,7},{7,6},{8,9},{9,8},{10,11... | collective-permute-start | bytes 393224 | tf_op jit(solution)/shard_map/ppermute | solution.py:21
  119.4 5.4 %collective-permute-start.21 = (f32[128,256]{1,0:T(8,128)S(1)}, f32[128,256]{1,0:T(8,128)S(1)}, u32[]{:S(2)}, u32[]{:S(2)}) collective-permute-start(f32[128,256]{1,0:T(8,128)S(1)} %add.127), channel_id=1, source_target_pairs={{0,2},{1,3},{2,0},{3,1},{4,6},{5,7},{6,4},{7,5},{8,10},{9,11},{10,... | collective-permute-start | bytes 393224 | tf_op jit(solution)/shard_map/ppermute | solution.py:21
  124.8 5.4 %collective-permute-start.22 = (f32[128,256]{1,0:T(8,128)S(1)}, f32[128,256]{1,0:T(8,128)S(1)}, u32[]{:S(2)}, u32[]{:S(2)}) collective-permute-start(f32[128,256]{1,0:T(8,128)S(1)} %add.128), channel_id=1, source_target_pairs={{0,4},{1,5},{2,6},{3,7},{4,0},{5,1},{6,2},{7,3},{8,12},{9,13},{10,... | collective-permute-start | bytes 393224 | tf_op jit(solution)/shard_map/ppermute | solution.py:21
  130.3 4.6 %collective-permute-start.23 = (bf16[3,128,256]{2,1,0:T(8,128)(2,1)S(1)}, bf16[3,128,256]{2,1,0:T(8,128)(2,1)S(1)}, u32[]{:S(2)}, u32[]{:S(2)}) collective-permute-start(bf16[3,128,256]{2,1,0:T(8,128)(2,1)S(1)} %pad_maximum_fusion.7), channel_id=1, source_target_pairs={{0,128},{64,192},{128,0},{192,64},{1,129},{65,193},{129,1},{193,65... | collective-permute-start | bytes 589832 | tf_op jit(solution)/shard_map/ppermute | solution.py:21
  135.0 6.7 %collective-permute-start.24 = (bf16[3,256,256]{2,1,0:T(8,128)(2,1)S(1)}, bf16[3,256,256]{2,1,0:T(8,128)(2,1)S(1)}, u32[]{:S(2)}, u32[]{:S(2)}) collective-permute-start(bf16[3,256,256]{2,1,0:T(8,128)(2,1)S(1)} %pad_maximum_fusion.5), channel_id=1, source_target_pairs={{0,64},{64,0},{128,192},{192,128},{1,65},{65,1},{129,193},{193,129... | collective-permute-start | bytes 1179656 | tf_op jit(solution)/shard_map/ppermute | solution.py:21
  (15 other events, 131.4 us)

commit v10 on v9

--- a/solution.py
+++ b/solution.py
@@ -143,7 +143,8 @@
             block = all_gather_lag(transposed(rates_chunk))
             sources.append(block)
         outputs.append(rates_chunk)
-    return all_gather_lag(jnp.stack(outputs), axis=1)
+    earlier_steps = all_gather_lag(jnp.stack(outputs[:-1]), axis=1)
+    return jnp.concatenate([earlier_steps, all_gather_lag(outputs[-1])[None]], axis=0)
 
 
 def solution(mesh):

time: 144 us -> 142 us (0.986)
  waiting for transfers between devices: 65.5 us -> 60 us
  starting transfers between devices: 34 us -> 37.5 us
    ppermute x19 -> x21, waiting for transfers between devices: 47.8 us -> 42.4 us  [swap(): return lax.ppermute(block, axis, [(i, i ^ mask) for i in range(size)])]
    ppermute x19 -> x21, starting transfers between devices: 27.4 us -> 30.8 us  [swap(): return lax.ppermute(block, axis, [(i, i ^ mask) for i in range(size)])]
  transfers between devices with their start and end apart: 25 -> 27, of which waited for: 14 -> 13; matrix products, arithmetic and copies ran while one was open for 20% -> 20% of each run, Pallas kernels for 0% -> 0%
where the time goes in v10:
time: 142 us; the launch traced here: 141 us
  waiting for transfers between devices  60 us (42%)
  starting transfers between devices  37.5 us (26%)
  other arithmetic  17.6 us (12%)
  local copies, waits for them, and re-layouts  13.2 us (9%)
  matrix products  11.9 us (8%)
    ppermute x21, waiting for transfers between devices, swap(): return lax.ppermute(block, axis, [(i, i ^ mask) for i in range(size)])  42.4 us
    ppermute x21, starting transfers between devices, swap(): return lax.ppermute(block, axis, [(i, i ^ mask) for i in range(size)])  30.8 us
    ppermute x2, waiting for transfers between devices, transposed(): return lax.ppermute(chunk, ('recv', 'src'), route)  17.6 us
    dot_general x2, matrix products, local(): jnp.dot(masked_rows, shifted.reshape(lag_here * cols_here, scenarios), pr...  8.9 us
    select_n x1, other arithmetic, local(): jnp.where(allowed, kernel, jnp.zeros_like(kernel))  8.71 us
    slice x1, local copies, waits for them, and re-layouts, local(): kernel[:, lag_index, :]  4.91 us
    ppermute x3, starting transfers between devices, local(): lax.ppermute(serial[:, start:start + chunk_rows], 'lag', [(0, target)])  3.31 us
    broadcast_in_dim x2, local copies, waits for them, and re-layouts, local(): jnp.repeat(jnp.repeat(causal_mask[:, lag_index, :], block_size, 0), block...  3.2 us
  transfers between devices with their start and end apart: 27, of which 13 were waited for; matrix products, arithmetic and copies ran while one was open for 20% of the time, Pallas kernels for 0%

profile of v10, /device:TPU:225, one launch (start us, length us, event | category | flops | bytes accessed | tf_op | source)
XLA Modules:
  0.0 140.9 jit_solution(2066489867811640990)
XLA Ops:
  0.9 8.7 %bitcast_select_fusion = bf16[512,8,512]{2,1,0:T(8,128)(2,1)S(1)} fusion(bf16[512,8,512]{2,1,0:T(8,128)(2,1)} %param.7, pred[512,8,4]{1,2,0:T(4,128)(4,1)S(1)} %bitcast.35), kind=kLoop, calls=%fused_computation | loop fusion | flops 2097152 | bytes 8404992 | tf_op jit(solution)/shard_map/jit(_where)/select_n | solution.py:98
  9.6 2.4 %fusion.9 = f32[512,256]{1,0:T(8,128)S(1)} fusion(bf16[8,512,256]{2,1,0:T(8,128)(2,1)S(1)} %copy-done.8, bf16[512,8,512]{2,1,0:T(8,128)(2,1)S(1)} %bitcast_select_fusion), kind=kOutput, calls=%fused_computation.24 | convolution fusion | flops 1073741824 | bytes 6815744 | tf_op jit(solution)/shard_map/dot_general | solution.py:121
  12.8 2.9 %copy.26 = bf16[8,512,256]{1,2,0:T(8,128)(2,1)S(1)} copy(bf16[8,512,256]{2,1,0:T(8,128)(2,1)} %param.9) | data formatting | bytes 4194304 | tf_op args[2]
  15.7 3.1 %collective-permute-start.5 = (bf16[2,512,256]{1,2,0:T(8,128)(2,1)S(1)}, bf16[2,512,256]{1,2,0:T(8,128)(2,1)}, u32[]{:S(2)}, u32[]{:S(2)}) collective-permute-start(bf16[2,512,256]{1,2,0:T(8,128)(2,1)S(1)} %slice.57), channel_id=1, source_target_pairs={{0,64},{64,128},{128,192},{1,65},{65,129},{129,193},{2,66},{66,130... | collective-permute-start | bytes 1572872 | tf_op jit(solution)/shard_map/ppermute | solution.py:119
  20.1 4.9 %fusion.46 = (bf16[512,1,512]{2,1,0:T(2,128)(2,1)S(1)}, bf16[512,1,512]{2,1,0:T(2,128)(2,1)S(1)}) fusion(bf16[512,8,512]{2,1,0:T(8,128)(2,1)} %param.7), kind=kLoop, calls=%fused_computation.98 | loop fusion | bytes 2097152 | tf_op jit(solution)/shard_map/slice | solution.py:110
  25.0 2.8 %collective-permute-done.1 = f32[128,256]{1,0:T(8,128)S(1)} collective-permute-done((f32[128,256]{1,0:T(8,128)S(1)}, f32[128,256]{1,0:T(8,128)S(1)}, u32[]{:S(2)}, u32[]{:S(2)}) %collective-permute-start.1) | collective-permute-done | bytes 131104 | tf_op jit(solution)/shard_map/ppermute | solution.py:21
  34.7 2.5 %collective-permute-start.3 = (f32[128,256]{1,0:T(8,128)S(1)}, f32[128,256]{1,0:T(8,128)S(1)}, u32[]{:S(2)}, u32[]{:S(2)}) collective-permute-start(f32[128,256]{1,0:T(8,128)S(1)} %add.116), channel_id=1, source_target_pairs={{0,2},{1,3},{2,0},{3,1},{4,6},{5,7},{6,4},{7,5},{8,10},{9,11},{10,... | collective-permute-start | bytes 393224 | tf_op jit(solution)/shard_map/ppermute | solution.py:21
  37.3 5.3 %fusion.15 = f32[512,256]{1,0:T(8,128)S(1)} fusion(bf16[2,512,256]{1,2,0:T(8,128)(2,1)} %collective-permute-done.5, bf16[8,512,256]{1,2,0:T(8,128)(2,1)} %copy-done.2, bf16[512,8,512]{2,1,0:T(8,128)(2,1)} %copy-done), kind=kOutput, calls=%fused_computation.26 | convolution fusion | flops 1074790400 | bytes 7340032 | tf_op jit(solution)/shard_map/dot_general | solution.py:126
  42.6 2.9 %collective-permute-start.4 = (f32[128,256]{1,0:T(8,128)S(1)}, f32[128,256]{1,0:T(8,128)S(1)}, u32[]{:S(2)}, u32[]{:S(2)}) collective-permute-start(f32[128,256]{1,0:T(8,128)S(1)} %add.117), channel_id=1, source_target_pairs={{0,4},{1,5},{2,6},{3,7},{4,0},{5,1},{6,2},{7,3},{8,12},{9,13},{10,... | collective-permute-start | bytes 393224 | tf_op jit(solution)/shard_map/ppermute | solution.py:21
  45.5 3.6 %fusion.12 = f32[512,256]{1,0:T(8,128)S(1)} fusion(bf16[8,512,256]{1,2,0:T(8,128)(2,1)S(1)} %copy-done.3, bf16[2,512,256]{1,2,0:T(8,128)(2,1)} %collective-permute-done.5, bf16[512,8,512]{2,1,0:T(8,128)(2,1)S(1)} %copy-done.1), kind=kOutput, calls=%fused_computation.25 | convolution fusion | flops 1074790400 | bytes 7340032 | tf_op jit(solution)/shard_map/dot_general | solution.py:126
  51.4 8.8 %collective-permute-done.11 = bf16[128,256]{1,0:T(8,128)(2,1)S(1)} collective-permute-done((bf16[128,256]{1,0:T(8,128)(2,1)S(1)}, bf16[128,256]{1,0:T(8,128)(2,1)S(1)}, u32[]{:S(2)}, u32[]{:S(2)}) %collective-permute-start.11) | collective-permute-done | bytes 65568 | tf_op jit(solution)/shard_map/ppermute | solution.py:79
  65.7 4.4 %collective-permute-start.13 = (bf16[256,256]{1,0:T(8,128)(2,1)S(1)}, bf16[256,256]{1,0:T(8,128)(2,1)S(1)}, u32[]{:S(2)}, u32[]{:S(2)}) collective-permute-start(bf16[256,256]{1,0:T(8,128)(2,1)S(1)} %pad_maximum_fusion.9), channel_id=1, source_target_pairs={{0,64},{64,0},{128,192},{192,128},{1,65},{65,1},{129,193},{193,129... | collective-permute-start | bytes 393224 | tf_op jit(solution)/shard_map/ppermute | solution.py:21
  72.5 6.6 %collective-permute-done.7 = f32[128,512]{1,0:T(8,128)S(1)} collective-permute-done((f32[128,512]{1,0:T(8,128)S(1)}, f32[128,512]{1,0:T(8,128)S(1)}, u32[]{:S(2)}, u32[]{:S(2)}) %collective-permute-start.7) | collective-permute-done | bytes 262176 | tf_op jit(solution)/shard_map/ppermute | solution.py:21
  79.5 4.1 %collective-permute-done.14 = f32[128,256]{1,0:T(8,128)S(1)} collective-permute-done((f32[128,256]{1,0:T(8,128)S(1)}, f32[128,256]{1,0:T(8,128)S(1)}, u32[]{:S(2)}, u32[]{:S(2)}) %collective-permute-start.14) | collective-permute-done | bytes 131104 | tf_op jit(solution)/shard_map/ppermute | solution.py:21
  83.8 5.2 %collective-permute-done.15 = f32[128,256]{1,0:T(8,128)S(1)} collective-permute-done((f32[128,256]{1,0:T(8,128)S(1)}, f32[128,256]{1,0:T(8,128)S(1)}, u32[]{:S(2)}, u32[]{:S(2)}) %collective-permute-start.15) | collective-permute-done | bytes 131104 | tf_op jit(solution)/shard_map/ppermute | solution.py:21
  89.9 4.6 %collective-permute-done.16 = f32[128,256]{1,0:T(8,128)S(1)} collective-permute-done((f32[128,256]{1,0:T(8,128)S(1)}, f32[128,256]{1,0:T(8,128)S(1)}, u32[]{:S(2)}, u32[]{:S(2)}) %collective-permute-start.16) | collective-permute-done | bytes 131104 | tf_op jit(solution)/shard_map/ppermute | solution.py:21
  94.7 8.8 %collective-permute-done.19 = bf16[128,256]{1,0:T(8,128)(2,1)S(1)} collective-permute-done((bf16[128,256]{1,0:T(8,128)(2,1)S(1)}, bf16[128,256]{1,0:T(8,128)(2,1)S(1)}, u32[]{:S(2)}, u32[]{:S(2)}) %collective-permute-start.19) | collective-permute-done | bytes 65568 | tf_op jit(solution)/shard_map/ppermute | solution.py:79
  104.3 2.7 %collective-permute-done.20 = bf16[128,256]{1,0:T(8,128)(2,1)S(1)} collective-permute-done((bf16[128,256]{1,0:T(8,128)(2,1)S(1)}, bf16[128,256]{1,0:T(8,128)(2,1)S(1)}, u32[]{:S(2)}, u32[]{:S(2)}) %collective-permute-start.20) | collective-permute-done | bytes 65568 | tf_op jit(solution)/shard_map/ppermute | solution.py:21
  107.0 6.1 %collective-permute-start.21 = (bf16[256,256]{1,0:T(8,128)(2,1)S(1)}, bf16[256,256]{1,0:T(8,128)(2,1)S(1)}, u32[]{:S(2)}, u32[]{:S(2)}) collective-permute-start(bf16[256,256]{1,0:T(8,128)(2,1)S(1)} %pad_maximum_fusion.11), channel_id=1, source_target_pairs={{0,64},{64,0},{128,192},{192,128},{1,65},{65,1},{129,193},{193,129... | collective-permute-start | bytes 393224 | tf_op jit(solution)/shard_map/ppermute | solution.py:21
  114.6 4.7 %collective-permute-done.22 = f32[128,256]{1,0:T(8,128)S(1)} collective-permute-done((f32[128,256]{1,0:T(8,128)S(1)}, f32[128,256]{1,0:T(8,128)S(1)}, u32[]{:S(2)}, u32[]{:S(2)}) %collective-permute-start.22) | collective-permute-done | bytes 131104 | tf_op jit(solution)/shard_map/ppermute | solution.py:21
  120.2 4.6 %collective-permute-done.23 = f32[128,256]{1,0:T(8,128)S(1)} collective-permute-done((f32[128,256]{1,0:T(8,128)S(1)}, f32[128,256]{1,0:T(8,128)S(1)}, u32[]{:S(2)}, u32[]{:S(2)}) %collective-permute-start.23) | collective-permute-done | bytes 131104 | tf_op jit(solution)/shard_map/ppermute | solution.py:21
  124.9 5.3 %collective-permute-done.24 = f32[128,256]{1,0:T(8,128)S(1)} collective-permute-done((f32[128,256]{1,0:T(8,128)S(1)}, f32[128,256]{1,0:T(8,128)S(1)}, u32[]{:S(2)}, u32[]{:S(2)}) %collective-permute-start.24) | collective-permute-done | bytes 131104 | tf_op jit(solution)/shard_map/ppermute | solution.py:21
  130.8 4.6 %collective-permute-start.18 = (bf16[2,256,256]{2,1,0:T(8,128)(2,1)S(1)}, bf16[2,256,256]{2,1,0:T(8,128)(2,1)S(1)}, u32[]{:S(2)}, u32[]{:S(2)}) collective-permute-start(bf16[2,256,256]{2,1,0:T(8,128)(2,1)S(1)} %pad_maximum_fusion.6), channel_id=1, source_target_pairs={{0,64},{64,0},{128,192},{192,128},{1,65},{65,1},{129,193},{193,129... | collective-permute-start | bytes 786440 | tf_op jit(solution)/shard_map/ppermute | solution.py:21
  135.4 3.5 %collective-permute-start.26 = (bf16[256,256]{1,0:T(8,128)(2,1)S(1)}, bf16[256,256]{1,0:T(8,128)(2,1)S(1)}, u32[]{:S(2)}, u32[]{:S(2)}) collective-permute-start(bf16[256,256]{1,0:T(8,128)(2,1)S(1)} %pad_maximum_fusion.12), channel_id=1, source_target_pairs={{0,64},{64,0},{128,192},{192,128},{1,65},{65,1},{129,193},{193,129... | collective-permute-start | bytes 393224 | tf_op jit(solution)/shard_map/ppermute | solution.py:21
  (114 shorter events, 27.2 us)
Async XLA Ops:
  12.1 6.9 %collective-permute-start = (f32[256,256]{1,0:T(8,128)S(1)}, f32[256,256]{1,0:T(8,128)}, u32[]{:S(2)}, u32[]{:S(2)}) collective-permute-start(f32[256,256]{1,0:T(8,128)S(1)} %constant_dynamic-slice_fusion.2), channel_id=1, source_target_pairs={{0,64},{64,0},{128,192},{192,128},{1,65},{65,1},{129,193},{193,129... | collective-permute-start | bytes 786440 | tf_op jit(solution)/shard_map/ppermute | solution.py:21
  15.7 21.5 %collective-permute-start.5 = (bf16[2,512,256]{1,2,0:T(8,128)(2,1)S(1)}, bf16[2,512,256]{1,2,0:T(8,128)(2,1)}, u32[]{:S(2)}, u32[]{:S(2)}) collective-permute-start(bf16[2,512,256]{1,2,0:T(8,128)(2,1)S(1)} %slice.57), channel_id=1, source_target_pairs={{0,64},{64,128},{128,192},{1,65},{65,129},{129,193},{2,66},{66,130... | collective-permute-start | bytes 1572872 | tf_op jit(solution)/shard_map/ppermute | solution.py:119
  20.0 7.8 %collective-permute-start.1 = (f32[128,256]{1,0:T(8,128)S(1)}, f32[128,256]{1,0:T(8,128)S(1)}, u32[]{:S(2)}, u32[]{:S(2)}) collective-permute-start(f32[128,256]{1,0:T(8,128)S(1)} %constant_dynamic-slice_fusion.1), channel_id=1, source_target_pairs={{0,128},{64,192},{128,0},{192,64},{1,129},{65,193},{129,1},{193,65... | collective-permute-start | bytes 393224 | tf_op jit(solution)/shard_map/ppermute | solution.py:21
  27.8 6.9 %collective-permute-start.2 = (f32[128,256]{1,0:T(8,128)S(1)}, f32[128,256]{1,0:T(8,128)S(1)}, u32[]{:S(2)}, u32[]{:S(2)}) collective-permute-start(f32[128,256]{1,0:T(8,128)S(1)} %dynamic-slice_add_fusion.2), channel_id=1, source_target_pairs={{0,1},{1,0},{2,3},{3,2},{4,5},{5,4},{6,7},{7,6},{8,9},{9,8},{10,11... | collective-permute-start | bytes 393224 | tf_op jit(solution)/shard_map/ppermute | solution.py:21
  34.7 7.9 %collective-permute-start.3 = (f32[128,256]{1,0:T(8,128)S(1)}, f32[128,256]{1,0:T(8,128)S(1)}, u32[]{:S(2)}, u32[]{:S(2)}) collective-permute-start(f32[128,256]{1,0:T(8,128)S(1)} %add.116), channel_id=1, source_target_pairs={{0,2},{1,3},{2,0},{3,1},{4,6},{5,7},{6,4},{7,5},{8,10},{9,11},{10,... | collective-permute-start | bytes 393224 | tf_op jit(solution)/shard_map/ppermute | solution.py:21
  42.6 7.4 %collective-permute-start.4 = (f32[128,256]{1,0:T(8,128)S(1)}, f32[128,256]{1,0:T(8,128)S(1)}, u32[]{:S(2)}, u32[]{:S(2)}) collective-permute-start(f32[128,256]{1,0:T(8,128)S(1)} %add.117), channel_id=1, source_target_pairs={{0,4},{1,5},{2,6},{3,7},{4,0},{5,1},{6,2},{7,3},{8,12},{9,13},{10,... | collective-permute-start | bytes 393224 | tf_op jit(solution)/shard_map/ppermute | solution.py:21
  50.0 20.0 %collective-permute-start.6 = (f32[256,512]{1,0:T(8,128)}, f32[256,512]{1,0:T(8,128)}, u32[]{:S(2)}, u32[]{:S(2)}) collective-permute-start(f32[256,512]{1,0:T(8,128)} %fusion.20), channel_id=1, source_target_pairs={{0,64},{64,0},{128,192},{192,128},{1,65},{65,1},{129,193},{193,129... | collective-permute-start | bytes 1572872 | tf_op jit(solution)/shard_map/ppermute | solution.py:21
  51.0 9.2 %collective-permute-start.11 = (bf16[128,256]{1,0:T(8,128)(2,1)S(1)}, bf16[128,256]{1,0:T(8,128)(2,1)S(1)}, u32[]{:S(2)}, u32[]{:S(2)}) collective-permute-start(bf16[128,256]{1,0:T(8,128)(2,1)S(1)} %multiply_convert_fusion.2), channel_id=1, source_target_pairs={{0,32},{1,24},{3,40},{2,16},{4,48},{5,8},{7,56},{6,0},{9,41},{8,33... | collective-permute-start | bytes 196616 | tf_op jit(solution)/shard_map/ppermute | solution.py:79
  60.2 5.4 %collective-permute-start.12 = (bf16[128,256]{1,0:T(8,128)(2,1)S(1)}, bf16[128,256]{1,0:T(8,128)(2,1)S(1)}, u32[]{:S(2)}, u32[]{:S(2)}) collective-permute-start(bf16[128,256]{1,0:T(8,128)(2,1)S(1)} %collective-permute-done.11), channel_id=1, source_target_pairs={{0,128},{64,192},{128,0},{192,64},{1,129},{65,193},{129,1},{193,65... | collective-permute-start | bytes 196616 | tf_op jit(solution)/shard_map/ppermute | solution.py:21
  62.2 9.1 %collective-permute-start.8 = (bf16[2,128,512]{2,1,0:T(8,128)(2,1)}, bf16[2,128,512]{2,1,0:T(8,128)(2,1)S(1)}, u32[]{:S(2)}, u32[]{:S(2)}) collective-permute-start(bf16[2,128,512]{2,1,0:T(8,128)(2,1)} %get-tuple-element.12), channel_id=1, source_target_pairs={{0,192},{1,193},{2,194},{3,195},{4,196},{5,197},{6,198},{7,199},{8... | collective-permute-start | bytes 786440 | tf_op jit(solution)/shard_map/ppermute | solution.py:115
  62.9 8.4 %collective-permute-start.9 = (bf16[2,128,512]{2,1,0:T(8,128)(2,1)}, bf16[2,128,512]{2,1,0:T(8,128)(2,1)}, u32[]{:S(2)}, u32[]{:S(2)}) collective-permute-start(bf16[2,128,512]{2,1,0:T(8,128)(2,1)} %get-tuple-element.13), channel_id=1, source_target_pairs={{0,128},{1,129},{2,130},{3,131},{4,132},{5,133},{6,134},{7,135},{8... | collective-permute-start | bytes 786440 | tf_op jit(solution)/shard_map/ppermute | solution.py:115
  64.3 7.0 %collective-permute-start.10 = (bf16[2,128,512]{2,1,0:T(8,128)(2,1)S(1)}, bf16[2,128,512]{2,1,0:T(8,128)(2,1)}, u32[]{:S(2)}, u32[]{:S(2)}) collective-permute-start(bf16[2,128,512]{2,1,0:T(8,128)(2,1)S(1)} %get-tuple-element.11), channel_id=1, source_target_pairs={{0,64},{1,65},{2,66},{3,67},{4,68},{5,69},{6,70},{7,71},{8,72},{9,... | collective-permute-start | bytes 786440 | tf_op jit(solution)/shard_map/ppermute | solution.py:115
  65.7 6.8 %collective-permute-start.13 = (bf16[256,256]{1,0:T(8,128)(2,1)S(1)}, bf16[256,256]{1,0:T(8,128)(2,1)S(1)}, u32[]{:S(2)}, u32[]{:S(2)}) collective-permute-start(bf16[256,256]{1,0:T(8,128)(2,1)S(1)} %pad_maximum_fusion.9), channel_id=1, source_target_pairs={{0,64},{64,0},{128,192},{192,128},{1,65},{65,1},{129,193},{193,129... | collective-permute-start | bytes 393224 | tf_op jit(solution)/shard_map/ppermute | solution.py:21
  71.2 7.9 %collective-permute-start.7 = (f32[128,512]{1,0:T(8,128)S(1)}, f32[128,512]{1,0:T(8,128)S(1)}, u32[]{:S(2)}, u32[]{:S(2)}) collective-permute-start(f32[128,512]{1,0:T(8,128)S(1)} %constant_dynamic-slice_fusion), channel_id=1, source_target_pairs={{0,128},{64,192},{128,0},{192,64},{1,129},{65,193},{129,1},{193,65... | collective-permute-start | bytes 786440 | tf_op jit(solution)/shard_map/ppermute | solution.py:21
  83.6 5.4 %collective-permute-start.15 = (f32[128,256]{1,0:T(8,128)S(1)}, f32[128,256]{1,0:T(8,128)S(1)}, u32[]{:S(2)}, u32[]{:S(2)}) collective-permute-start(f32[128,256]{1,0:T(8,128)S(1)} %add.123), channel_id=1, source_target_pairs={{0,2},{1,3},{2,0},{3,1},{4,6},{5,7},{6,4},{7,5},{8,10},{9,11},{10,... | collective-permute-start | bytes 393224 | tf_op jit(solution)/shard_map/ppermute | solution.py:21
  89.1 5.4 %collective-permute-start.16 = (f32[128,256]{1,0:T(8,128)S(1)}, f32[128,256]{1,0:T(8,128)S(1)}, u32[]{:S(2)}, u32[]{:S(2)}) collective-permute-start(f32[128,256]{1,0:T(8,128)S(1)} %add.124), channel_id=1, source_target_pairs={{0,4},{1,5},{2,6},{3,7},{4,0},{5,1},{6,2},{7,3},{8,12},{9,13},{10,... | collective-permute-start | bytes 393224 | tf_op jit(solution)/shard_map/ppermute | solution.py:21
  94.6 8.9 %collective-permute-start.19 = (bf16[128,256]{1,0:T(8,128)(2,1)S(1)}, bf16[128,256]{1,0:T(8,128)(2,1)S(1)}, u32[]{:S(2)}, u32[]{:S(2)}) collective-permute-start(bf16[128,256]{1,0:T(8,128)(2,1)S(1)} %multiply_convert_fusion.1), channel_id=1, source_target_pairs={{0,32},{1,24},{3,40},{2,16},{4,48},{5,8},{7,56},{6,0},{9,41},{8,33... | collective-permute-start | bytes 196616 | tf_op jit(solution)/shard_map/ppermute | solution.py:79
  107.0 7.1 %collective-permute-start.21 = (bf16[256,256]{1,0:T(8,128)(2,1)S(1)}, bf16[256,256]{1,0:T(8,128)(2,1)S(1)}, u32[]{:S(2)}, u32[]{:S(2)}) collective-permute-start(bf16[256,256]{1,0:T(8,128)(2,1)S(1)} %pad_maximum_fusion.11), channel_id=1, source_target_pairs={{0,64},{64,0},{128,192},{192,128},{1,65},{65,1},{129,193},{193,129... | collective-permute-start | bytes 393224 | tf_op jit(solution)/shard_map/ppermute | solution.py:21
  114.5 4.8 %collective-permute-start.22 = (f32[128,256]{1,0:T(8,128)S(1)}, f32[128,256]{1,0:T(8,128)S(1)}, u32[]{:S(2)}, u32[]{:S(2)}) collective-permute-start(f32[128,256]{1,0:T(8,128)S(1)} %fusion.38), channel_id=1, source_target_pairs={{0,1},{1,0},{2,3},{3,2},{4,5},{5,4},{6,7},{7,6},{8,9},{9,8},{10,11... | collective-permute-start | bytes 393224 | tf_op jit(solution)/shard_map/ppermute | solution.py:21
  119.3 5.4 %collective-permute-start.23 = (f32[128,256]{1,0:T(8,128)S(1)}, f32[128,256]{1,0:T(8,128)S(1)}, u32[]{:S(2)}, u32[]{:S(2)}) collective-permute-start(f32[128,256]{1,0:T(8,128)S(1)} %add.129), channel_id=1, source_target_pairs={{0,2},{1,3},{2,0},{3,1},{4,6},{5,7},{6,4},{7,5},{8,10},{9,11},{10,... | collective-permute-start | bytes 393224 | tf_op jit(solution)/shard_map/ppermute | solution.py:21
  119.5 5.4 %collective-permute-start.17 = (bf16[2,128,256]{2,1,0:T(8,128)(2,1)S(1)}, bf16[2,128,256]{2,1,0:T(8,128)(2,1)S(1)}, u32[]{:S(2)}, u32[]{:S(2)}) collective-permute-start(bf16[2,128,256]{2,1,0:T(8,128)(2,1)S(1)} %pad_maximum_fusion.10), channel_id=1, source_target_pairs={{0,128},{64,192},{128,0},{192,64},{1,129},{65,193},{129,1},{193,65... | collective-permute-start | bytes 393224 | tf_op jit(solution)/shard_map/ppermute | solution.py:21
  124.8 5.4 %collective-permute-start.24 = (f32[128,256]{1,0:T(8,128)S(1)}, f32[128,256]{1,0:T(8,128)S(1)}, u32[]{:S(2)}, u32[]{:S(2)}) collective-permute-start(f32[128,256]{1,0:T(8,128)S(1)} %add.130), channel_id=1, source_target_pairs={{0,4},{1,5},{2,6},{3,7},{4,0},{5,1},{6,2},{7,3},{8,12},{9,13},{10,... | collective-permute-start | bytes 393224 | tf_op jit(solution)/shard_map/ppermute | solution.py:21
  130.3 5.1 %collective-permute-start.25 = (bf16[128,256]{1,0:T(8,128)(2,1)S(1)}, bf16[128,256]{1,0:T(8,128)(2,1)S(1)}, u32[]{:S(2)}, u32[]{:S(2)}) collective-permute-start(bf16[128,256]{1,0:T(8,128)(2,1)S(1)} %multiply_convert_fusion), channel_id=1, source_target_pairs={{0,128},{64,192},{128,0},{192,64},{1,129},{65,193},{129,1},{193,65... | collective-permute-start | bytes 196616 | tf_op jit(solution)/shard_map/ppermute | solution.py:21
  130.8 8.1 %collective-permute-start.18 = (bf16[2,256,256]{2,1,0:T(8,128)(2,1)S(1)}, bf16[2,256,256]{2,1,0:T(8,128)(2,1)S(1)}, u32[]{:S(2)}, u32[]{:S(2)}) collective-permute-start(bf16[2,256,256]{2,1,0:T(8,128)(2,1)S(1)} %pad_maximum_fusion.6), channel_id=1, source_target_pairs={{0,64},{64,0},{128,192},{192,128},{1,65},{65,1},{129,193},{193,129... | collective-permute-start | bytes 786440 | tf_op jit(solution)/shard_map/ppermute | solution.py:21
  (17 other events, 140.1 us)
